TPU v7x, 32 devices: a whole 2x2x4 slice. The times are simulated.
32 devices in a mesh: grp: 4 (over z), node: 8 (over y, x, core).
Axes of the slice: x: 2, y: 2, z: 4, core: 2. Of those that a mesh axis runs over, the one named last changes fastest.
Arguments:
- params: bfloat16 [4, 14336, 4096], P('grp', 'node'), may hold values from -6 to 6
- momentum: bfloat16 [4, 14336, 4096], P('grp', 'node'), may hold values from -0.125 to 0.125
- hidden: bfloat16 [4, 1024, 14336], P('grp', 'node'), may hold values from -6 to 6
- cotangent: bfloat16 [4, 1024, 4096], P('grp', 'node'), may hold values from -6 to 6
- push_weight: float32 [4], P('grp'), may hold values from 0.5 to 2
- offsets: int32 [64], replicated, may hold values from 1 to 3
- step: int32 [1], replicated, may hold values from 0 to 63
Outputs:
- mixed: bfloat16 [4, 14336, 4096], P('grp', 'node')
- new_weight: float32 [4], P('grp')
All inputs are finite; a program needn't handle non-finite values.
Results may differ from a plain program's by a relative error of at most 0.005.
Values may be sent and summed in bfloat16 or wider, within the bound.
No kernel may reach another device: no remote copies, remote signals or barrier semaphores. Data moves between devices by JAX's collectives and lax.ppermute only.
A program may use at most 192 MiB of HBM per device.

v0:
```python
import jax
import jax.numpy as jnp
from jax import lax
from jax.sharding import PartitionSpec as P

base_rate = 40.0
moment_decay = 0.9
keep_share = 0.5
back_share = 0.3
front_share = 0.2
tokens_axis = (((0,), (0,)), ((), ()))
col_blocks = 4


def shifted(value, axis, steps):
    count = lax.axis_size(axis)
    pairs = [(source, (source + steps) % count) for source in range(count)]
    return lax.ppermute(value, axis, pairs)


def block_count(length, target, quantum):
    for count in range(target, 0, -1):
        if length % count == 0 and (length // count) % quantum == 0:
            return count
    return 1


def row_sizes(rows, quantum=16):
    sizes, size, left = [], 128, rows
    while left > 0:
        take = left if (left - size < size or size % quantum) else size
        sizes.append(take)
        left -= take
        size *= 2
    return sizes


def pipeline(amount, groups, params, momentum, hidden, cotangent, push_weight, rate, direct):
    nodes = lax.axis_size("node")
    rows_total = params.shape[1]
    acts = hidden.reshape(hidden.shape[0], nodes, rows_total)
    width = cotangent.shape[1]
    n_cols = block_count(width, col_blocks, 128)
    col_size = width // n_cols
    paired = (2 * amount) % groups == 0
    w_minus = jnp.where(direct, back_share, front_share).astype(jnp.float32)
    w_plus = jnp.where(direct, front_share, back_share).astype(jnp.float32)
    cots = [
        lax.all_gather(cotangent[:, b * col_size:(b + 1) * col_size], "node", axis=0, tiled=True)
        for b in range(n_cols)
    ]
    mixed = jnp.zeros(params.shape[1:], jnp.bfloat16)
    sizes = row_sizes(rows_total)
    starts = [sum(sizes[:i]) for i in range(len(sizes))]
    columns = [None] * len(sizes)
    last = None
    for b in range(n_cols):
        span = slice(b * col_size, (b + 1) * col_size)
        for a, (start, size) in enumerate(zip(starts, sizes)):
            if columns[a] is None:
                piece = acts[:, :, start:start + size]
                if last is not None:
                    piece, last = lax.optimization_barrier((piece, last))
                cols = lax.all_to_all(piece, "node", split_axis=1, concat_axis=0, tiled=True)
                columns[a] = cols.reshape(-1, size)
            cols, cot = columns[a], cots[b]
            if last is not None:
                cols, cot, last = lax.optimization_barrier((cols, cot, last))
            tok_group = cols.shape[0]
            rows = slice(start, start + size)
            grad = lax.dot_general(cols, cot, tokens_axis, preferred_element_type=jnp.float32)
            grad = grad / tok_group
            renewed = moment_decay * momentum[0, rows, span].astype(jnp.float32) + grad
            half = (params[0, rows, span].astype(jnp.float32) - rate * renewed).astype(jnp.bfloat16)
            last = half
            minus = shifted(half, "grp", amount)
            if paired:
                peers = (back_share * minus.astype(jnp.float32)) + front_share * minus.astype(jnp.float32)
            else:
                plus = shifted(half, "grp", groups - amount)
                peers = w_minus * minus.astype(jnp.float32) + w_plus * plus.astype(jnp.float32)
            total = keep_share * half.astype(jnp.float32) + peers
            mixed = lax.dynamic_update_slice(mixed, total.astype(jnp.bfloat16), (start, b * col_size))
    weight_minus = shifted(push_weight, "grp", amount)
    weight_plus = shifted(push_weight, "grp", groups - amount)
    new_weight = keep_share * push_weight + w_minus * weight_minus + w_plus * weight_plus
    return mixed[None], new_weight


def per_device(params, momentum, hidden, cotangent, push_weight, offsets, step):
    groups = lax.axis_size("grp")
    position = step[0]
    offset = offsets[position]
    rate = base_rate * (1.0 - 0.5 * position.astype(jnp.float32) / offsets.shape[0])
    amounts = list(range(1, groups // 2 + 1))
    direct = offset <= groups // 2
    index = jnp.where(direct, offset, groups - offset) - 1
    branches = [
        (lambda *a, amount=amount: pipeline(amount, groups, *a))
        for amount in amounts
    ]
    return lax.switch(
        index, branches, params, momentum, hidden[0], cotangent[0], push_weight, rate, direct
    )


def solution(mesh):
    in_specs = (
        P("grp", "node", None),
        P("grp", "node", None),
        P("grp", "node", None),
        P("grp", "node", None),
        P("grp"),
        P(),
        P(),
    )
    out_specs = (P("grp", "node", None), P("grp"))
    return jax.shard_map(
        per_device, mesh=mesh, in_specs=in_specs, out_specs=out_specs, check_vma=False
    )
```

profile of v0, /device:TPU:0, one launch (start us, length us, event | category | flops | bytes accessed | tf_op | source)
XLA Modules:
  0.0 768.5 jit_solution(4399742208264735254)
XLA Ops:
  11.0 749.3 %conditional.1 = (bf16[1,1792,4096]{2,1,0:T(8,128)(2,1)}, f32[1]{0:T(128)}) conditional(s32[]{:T(128)} %clamp.3, (bf16[1,1792,4096]{2,1,0:T(8,128)(2,1)}, f32[]{:T(128)}, bf16[1,1792,4096]{2,1,0:T(8,128)(2,1)}, bf16[1,128,14336]{2,1,0:T(8,128)(2,1)}, bf16[128,4096]{1,0:T(8,128)(2,1)}, /*index=5*/pred[]{:T(512)}, f32[1]{0:T(128)}) %tuple.89, ...), branch_computations={%region_0.1_spmd, %region_1.2_spmd} | conditional | flops 15157166080 | bytes 550244928 | solution.py:102
  14.8 6.1 copy.21
  22.6 5.2 all-to-all-start
  29.6 5.0 all-to-all-done
  34.9 9.5 %all-gather.9.cloned.1.call-done = bf16[1024,1024]{1,0:T(8,128)(2,1)} async-done(((bf16[128,1024]{1,0:T(8,128)(2,1)}), bf16[1024,1024]{1,0:T(8,128)(2,1)}) %all-gather.9.cloned.1.call-update) | async-done | bytes 2097168 | tf_op jit(solution)/shard_map/cond/branch_0_fun/all_gather | solution.py:49
  52.4 10.2 %all-to-all-done.1 = bf16[128,8,256]{0,2,1:T(8,128)(2,1)S(1)} async-done(((bf16[128,8,256]{0,2,1:T(8,128)(2,1)}), bf16[128,8,256]{0,2,1:T(8,128)(2,1)S(1)}, u32[]{:S(2)}, u32[]{:S(2)}) %all-to-all-start.1) | async-done | bytes 524320 | tf_op jit(solution)/shard_map/cond/branch_0_fun/all_to_all | solution.py:64
  80.8 6.4 all-to-all-done.2
  87.7 5.1 fusion.11
  101.0 7.3 pad_bitcast_fusion
  108.4 5.3 collective-permute-done.3
  113.7 11.6 %collective-permute-done.2 = bf16[256,1024]{1,0:T(8,128)(2,1)} collective-permute-done((bf16[256,1024]{1,0:T(8,128)(2,1)}, bf16[256,1024]{1,0:T(8,128)(2,1)}, u32[]{:S(2)}, u32[]{:S(2)}) %collective-permute-start.2) | collective-permute-done | bytes 524320 | tf_op jit(solution)/shard_map/cond/branch_0_fun/ppermute | solution.py:18
  132.5 7.2 fusion.3
  157.3 6.1 fusion.2
  172.0 6.1 fusion.1
  181.9 84.2 %collective-permute-done.9 = bf16[128,1024]{1,0:T(8,128)(2,1)} collective-permute-done((bf16[128,1024]{1,0:T(8,128)(2,1)}, bf16[128,1024]{1,0:T(8,128)(2,1)}, u32[]{:S(2)}, u32[]{:S(2)}) %collective-permute-start.9) | collective-permute-done | bytes 262176 | tf_op jit(solution)/shard_map/cond/branch_0_fun/ppermute | solution.py:18
  272.2 5.0 collective-permute-done.17
  283.4 11.3 %collective-permute-done.25 = bf16[128,1024]{1,0:T(8,128)(2,1)S(1)} collective-permute-done((bf16[128,1024]{1,0:T(8,128)(2,1)S(1)}, bf16[128,1024]{1,0:T(8,128)(2,1)S(1)}, u32[]{:S(2)}, u32[]{:S(2)}) %collective-permute-start.25) | collective-permute-done | bytes 262176 | tf_op jit(solution)/shard_map/cond/branch_0_fun/ppermute | solution.py:18
  294.7 16.7 %collective-permute-start.10 = (bf16[256,1024]{1,0:T(8,128)(2,1)S(1)}, bf16[256,1024]{1,0:T(8,128)(2,1)S(1)}, u32[]{:S(2)}, u32[]{:S(2)}) collective-permute-start(bf16[256,1024]{1,0:T(8,128)(2,1)S(1)} %copy-done.32), channel_id=1, source_target_pairs={{0,8},{8,16},{16,24},{24,0},{1,9},{9,17},{17,25},{25,1},{2,10},{10... | collective-permute-start | bytes 1572872 | tf_op jit(solution)/shard_map/cond/branch_0_fun/ppermute | solution.py:18
  311.4 11.0 %collective-permute-start.19 = (bf16[256,1024]{1,0:T(8,128)(2,1)S(1)}, bf16[256,1024]{1,0:T(8,128)(2,1)S(1)}, u32[]{:S(2)}, u32[]{:S(2)}) collective-permute-start(bf16[256,1024]{1,0:T(8,128)(2,1)S(1)} %copy-done.29), channel_id=1, source_target_pairs={{0,24},{8,0},{16,8},{24,16},{1,25},{9,1},{17,9},{25,17},{2,26},{10... | collective-permute-start | bytes 1572872 | tf_op jit(solution)/shard_map/cond/branch_0_fun/ppermute | solution.py:18
  331.6 5.7 collective-permute-done.19
  349.3 114.9 %collective-permute-done.18 = bf16[256,1024]{1,0:T(8,128)(2,1)S(1)} collective-permute-done((bf16[256,1024]{1,0:T(8,128)(2,1)S(1)}, bf16[256,1024]{1,0:T(8,128)(2,1)S(1)}, u32[]{:S(2)}, u32[]{:S(2)}) %collective-permute-start.18) | collective-permute-done | bytes 524320 | tf_op jit(solution)/shard_map/cond/branch_0_fun/ppermute | solution.py:18
  478.4 125.2 %collective-permute-done.27 = bf16[256,1024]{1,0:T(8,128)(2,1)S(1)} collective-permute-done((bf16[256,1024]{1,0:T(8,128)(2,1)S(1)}, bf16[256,1024]{1,0:T(8,128)(2,1)S(1)}, u32[]{:S(2)}, u32[]{:S(2)}) %collective-permute-start.27) | collective-permute-done | bytes 524320 | tf_op jit(solution)/shard_map/cond/branch_0_fun/ppermute | solution.py:18
  614.4 128.4 %collective-permute-done.26 = bf16[256,1024]{1,0:T(8,128)(2,1)S(1)} collective-permute-done((bf16[256,1024]{1,0:T(8,128)(2,1)S(1)}, bf16[256,1024]{1,0:T(8,128)(2,1)S(1)}, u32[]{:S(2)}, u32[]{:S(2)}) %collective-permute-start.26) | collective-permute-done | bytes 524320 | tf_op jit(solution)/shard_map/cond/branch_0_fun/ppermute | solution.py:18
  745.2 5.5 copy-done
  (182 shorter events, 139.6 us)
Async XLA Ops:
  13.3 129.8 %all-gather.11.cloned.1.call-start = ((), (), s32[]{:S(2)}) async-start(), calls=%async_computation.9 | async-start | bytes 2359296 | tf_op jit(solution)/shard_map/cond/branch_0_fun/all_gather | solution.py:49
  14.1 149.3 %all-gather.13.cloned.1.call-start = ((), (), s32[]{:S(2)}) async-start(), calls=%async_computation.10 | async-start | bytes 2359296 | tf_op jit(solution)/shard_map/cond/branch_0_fun/all_gather | solution.py:49
  70.0 108.0 %all-gather.15.cloned.1.call-start = ((), (), s32[]{:S(2)}) async-start(), calls=%async_computation.11 | async-start | bytes 2359296 | tf_op jit(solution)/shard_map/cond/branch_0_fun/all_gather | solution.py:49
  139.6 197.7 %collective-permute-start.7 = (bf16[896,1024]{1,0:T(8,128)(2,1)}, bf16[896,1024]{1,0:T(8,128)(2,1)}, u32[]{:S(2)}, u32[]{:S(2)}) collective-permute-start(bf16[896,1024]{1,0:T(8,128)(2,1)} %fusion.3), channel_id=1, source_target_pairs={{0,24},{8,0},{16,8},{24,16},{1,25},{9,1},{17,9},{25,17},{2,26},{10... | collective-permute-start | bytes 5505032 | tf_op jit(solution)/shard_map/cond/branch_0_fun/ppermute | solution.py:18
  143.2 194.2 %collective-permute-start.6 = (bf16[896,1024]{1,0:T(8,128)(2,1)}, bf16[896,1024]{1,0:T(8,128)(2,1)}, u32[]{:S(2)}, u32[]{:S(2)}) collective-permute-start(bf16[896,1024]{1,0:T(8,128)(2,1)} %fusion.3), channel_id=1, source_target_pairs={{0,8},{8,16},{16,24},{24,0},{1,9},{9,17},{17,25},{25,1},{2,10},{10... | collective-permute-start | bytes 5505032 | tf_op jit(solution)/shard_map/cond/branch_0_fun/ppermute | solution.py:18
  146.2 119.9 %collective-permute-start.9 = (bf16[128,1024]{1,0:T(8,128)(2,1)}, bf16[128,1024]{1,0:T(8,128)(2,1)}, u32[]{:S(2)}, u32[]{:S(2)}) collective-permute-start(bf16[128,1024]{1,0:T(8,128)(2,1)} %fusion.53), channel_id=1, source_target_pairs={{0,24},{8,0},{16,8},{24,16},{1,25},{9,1},{17,9},{25,17},{2,26},{10... | collective-permute-start | bytes 786440 | tf_op jit(solution)/shard_map/cond/branch_0_fun/ppermute | solution.py:18
  178.0 92.2 %collective-permute-start.8 = (bf16[128,1024]{1,0:T(8,128)(2,1)}, bf16[128,1024]{1,0:T(8,128)(2,1)S(1)}, u32[]{:S(2)}, u32[]{:S(2)}) collective-permute-start(bf16[128,1024]{1,0:T(8,128)(2,1)} %fusion.53), channel_id=1, source_target_pairs={{0,8},{8,16},{16,24},{24,0},{1,9},{9,17},{17,25},{25,1},{2,10},{10... | collective-permute-start | bytes 786440 | tf_op jit(solution)/shard_map/cond/branch_0_fun/ppermute | solution.py:18
  178.2 99.0 %collective-permute-start.17 = (bf16[128,1024]{1,0:T(8,128)(2,1)S(1)}, bf16[128,1024]{1,0:T(8,128)(2,1)S(1)}, u32[]{:S(2)}, u32[]{:S(2)}) collective-permute-start(bf16[128,1024]{1,0:T(8,128)(2,1)S(1)} %fusion.54), channel_id=1, source_target_pairs={{0,24},{8,0},{16,8},{24,16},{1,25},{9,1},{17,9},{25,17},{2,26},{10... | collective-permute-start | bytes 786440 | tf_op jit(solution)/shard_map/cond/branch_0_fun/ppermute | solution.py:18
  270.3 55.0 %collective-permute-start.11 = (bf16[256,1024]{1,0:T(8,128)(2,1)S(1)}, bf16[256,1024]{1,0:T(8,128)(2,1)S(1)}, u32[]{:S(2)}, u32[]{:S(2)}) collective-permute-start(bf16[256,1024]{1,0:T(8,128)(2,1)S(1)} %copy-done.32), channel_id=1, source_target_pairs={{0,24},{8,0},{16,8},{24,16},{1,25},{9,1},{17,9},{25,17},{2,26},{10... | collective-permute-start | bytes 1572872 | tf_op jit(solution)/shard_map/cond/branch_0_fun/ppermute | solution.py:18
  325.3 146.8 %collective-permute-start.15 = (bf16[896,1024]{1,0:T(8,128)(2,1)S(1)}, bf16[896,1024]{1,0:T(8,128)(2,1)S(1)}, u32[]{:S(2)}, u32[]{:S(2)}) collective-permute-start(bf16[896,1024]{1,0:T(8,128)(2,1)S(1)} %copy-done.11), channel_id=1, source_target_pairs={{0,24},{8,0},{16,8},{24,16},{1,25},{9,1},{17,9},{25,17},{2,26},{10... | collective-permute-start | bytes 5505032 | tf_op jit(solution)/shard_map/cond/branch_0_fun/ppermute | solution.py:18
  329.0 140.7 %collective-permute-start.13 = (bf16[512,1024]{1,0:T(8,128)(2,1)S(1)}, bf16[512,1024]{1,0:T(8,128)(2,1)S(1)}, u32[]{:S(2)}, u32[]{:S(2)}) collective-permute-start(bf16[512,1024]{1,0:T(8,128)(2,1)S(1)} %copy-done.13), channel_id=1, source_target_pairs={{0,24},{8,0},{16,8},{24,16},{1,25},{9,1},{17,9},{25,17},{2,26},{10... | collective-permute-start | bytes 3145736 | tf_op jit(solution)/shard_map/cond/branch_0_fun/ppermute | solution.py:18
  337.3 132.7 %collective-permute-start.12 = (bf16[512,1024]{1,0:T(8,128)(2,1)S(1)}, bf16[512,1024]{1,0:T(8,128)(2,1)S(1)}, u32[]{:S(2)}, u32[]{:S(2)}) collective-permute-start(bf16[512,1024]{1,0:T(8,128)(2,1)S(1)} %copy-done.13), channel_id=1, source_target_pairs={{0,8},{8,16},{16,24},{24,0},{1,9},{9,17},{17,25},{25,1},{2,10},{10... | collective-permute-start | bytes 3145736 | tf_op jit(solution)/shard_map/cond/branch_0_fun/ppermute | solution.py:18
  337.3 135.7 %collective-permute-start.14 = (bf16[896,1024]{1,0:T(8,128)(2,1)S(1)}, bf16[896,1024]{1,0:T(8,128)(2,1)S(1)}, u32[]{:S(2)}, u32[]{:S(2)}) collective-permute-start(bf16[896,1024]{1,0:T(8,128)(2,1)S(1)} %copy-done.11), channel_id=1, source_target_pairs={{0,8},{8,16},{16,24},{24,0},{1,9},{9,17},{17,25},{25,1},{2,10},{10... | collective-permute-start | bytes 5505032 | tf_op jit(solution)/shard_map/cond/branch_0_fun/ppermute | solution.py:18
  337.4 126.8 %collective-permute-start.18 = (bf16[256,1024]{1,0:T(8,128)(2,1)S(1)}, bf16[256,1024]{1,0:T(8,128)(2,1)S(1)}, u32[]{:S(2)}, u32[]{:S(2)}) collective-permute-start(bf16[256,1024]{1,0:T(8,128)(2,1)S(1)} %copy-done.29), channel_id=1, source_target_pairs={{0,8},{8,16},{16,24},{24,0},{1,9},{9,17},{17,25},{25,1},{2,10},{10... | collective-permute-start | bytes 1572872 | tf_op jit(solution)/shard_map/cond/branch_0_fun/ppermute | solution.py:18
  464.2 147.9 %collective-permute-start.23 = (bf16[896,1024]{1,0:T(8,128)(2,1)S(1)}, bf16[896,1024]{1,0:T(8,128)(2,1)S(1)}, u32[]{:S(2)}, u32[]{:S(2)}) collective-permute-start(bf16[896,1024]{1,0:T(8,128)(2,1)S(1)} %copy-done.10), channel_id=1, source_target_pairs={{0,24},{8,0},{16,8},{24,16},{1,25},{9,1},{17,9},{25,17},{2,26},{10... | collective-permute-start | bytes 5505032 | tf_op jit(solution)/shard_map/cond/branch_0_fun/ppermute | solution.py:18
  469.7 138.2 %collective-permute-start.21 = (bf16[512,1024]{1,0:T(8,128)(2,1)S(1)}, bf16[512,1024]{1,0:T(8,128)(2,1)S(1)}, u32[]{:S(2)}, u32[]{:S(2)}) collective-permute-start(bf16[512,1024]{1,0:T(8,128)(2,1)S(1)} %fusion.9), channel_id=1, source_target_pairs={{0,24},{8,0},{16,8},{24,16},{1,25},{9,1},{17,9},{25,17},{2,26},{10... | collective-permute-start | bytes 3145736 | tf_op jit(solution)/shard_map/cond/branch_0_fun/ppermute | solution.py:18
  470.0 142.9 %collective-permute-start.22 = (bf16[896,1024]{1,0:T(8,128)(2,1)S(1)}, bf16[896,1024]{1,0:T(8,128)(2,1)S(1)}, u32[]{:S(2)}, u32[]{:S(2)}) collective-permute-start(bf16[896,1024]{1,0:T(8,128)(2,1)S(1)} %copy-done.10), channel_id=1, source_target_pairs={{0,8},{8,16},{16,24},{24,0},{1,9},{9,17},{17,25},{25,1},{2,10},{10... | collective-permute-start | bytes 5505032 | tf_op jit(solution)/shard_map/cond/branch_0_fun/ppermute | solution.py:18
  472.1 136.1 %collective-permute-start.20 = (bf16[512,1024]{1,0:T(8,128)(2,1)S(1)}, bf16[512,1024]{1,0:T(8,128)(2,1)S(1)}, u32[]{:S(2)}, u32[]{:S(2)}) collective-permute-start(bf16[512,1024]{1,0:T(8,128)(2,1)S(1)} %fusion.9), channel_id=1, source_target_pairs={{0,8},{8,16},{16,24},{24,0},{1,9},{9,17},{17,25},{25,1},{2,10},{10... | collective-permute-start | bytes 3145736 | tf_op jit(solution)/shard_map/cond/branch_0_fun/ppermute | solution.py:18
  473.1 130.5 %collective-permute-start.27 = (bf16[256,1024]{1,0:T(8,128)(2,1)S(1)}, bf16[256,1024]{1,0:T(8,128)(2,1)S(1)}, u32[]{:S(2)}, u32[]{:S(2)}) collective-permute-start(bf16[256,1024]{1,0:T(8,128)(2,1)S(1)} %copy-done.31), channel_id=1, source_target_pairs={{0,24},{8,0},{16,8},{24,16},{1,25},{9,1},{17,9},{25,17},{2,26},{10... | collective-permute-start | bytes 1572872 | tf_op jit(solution)/shard_map/cond/branch_0_fun/ppermute | solution.py:18
  603.6 140.3 %collective-permute-start.31 = (bf16[896,1024]{1,0:T(8,128)(2,1)S(1)}, bf16[896,1024]{1,0:T(8,128)(2,1)S(1)}, u32[]{:S(2)}, u32[]{:S(2)}) collective-permute-start(bf16[896,1024]{1,0:T(8,128)(2,1)S(1)} %fusion), channel_id=1, source_target_pairs={{0,24},{8,0},{16,8},{24,16},{1,25},{9,1},{17,9},{25,17},{2,26},{10... | collective-permute-start | bytes 5505032 | tf_op jit(solution)/shard_map/cond/branch_0_fun/ppermute | solution.py:18
  607.9 136.0 %collective-permute-start.30 = (bf16[896,1024]{1,0:T(8,128)(2,1)S(1)}, bf16[896,1024]{1,0:T(8,128)(2,1)S(1)}, u32[]{:S(2)}, u32[]{:S(2)}) collective-permute-start(bf16[896,1024]{1,0:T(8,128)(2,1)S(1)} %fusion), channel_id=1, source_target_pairs={{0,8},{8,16},{16,24},{24,0},{1,9},{9,17},{17,25},{25,1},{2,10},{10... | collective-permute-start | bytes 5505032 | tf_op jit(solution)/shard_map/cond/branch_0_fun/ppermute | solution.py:18
  608.2 134.9 %collective-permute-start.29 = (bf16[512,1024]{1,0:T(8,128)(2,1)S(1)}, bf16[512,1024]{1,0:T(8,128)(2,1)S(1)}, u32[]{:S(2)}, u32[]{:S(2)}) collective-permute-start(bf16[512,1024]{1,0:T(8,128)(2,1)S(1)} %fusion.8), channel_id=1, source_target_pairs={{0,24},{8,0},{16,8},{24,16},{1,25},{9,1},{17,9},{25,17},{2,26},{10... | collective-permute-start | bytes 3145736 | tf_op jit(solution)/shard_map/cond/branch_0_fun/ppermute | solution.py:18
  612.1 131.1 %collective-permute-start.28 = (bf16[512,1024]{1,0:T(8,128)(2,1)S(1)}, bf16[512,1024]{1,0:T(8,128)(2,1)S(1)}, u32[]{:S(2)}, u32[]{:S(2)}) collective-permute-start(bf16[512,1024]{1,0:T(8,128)(2,1)S(1)} %fusion.8), channel_id=1, source_target_pairs={{0,8},{8,16},{16,24},{24,0},{1,9},{9,17},{17,25},{25,1},{2,10},{10... | collective-permute-start | bytes 3145736 | tf_op jit(solution)/shard_map/cond/branch_0_fun/ppermute | solution.py:18
  612.8 130.0 %collective-permute-start.26 = (bf16[256,1024]{1,0:T(8,128)(2,1)S(1)}, bf16[256,1024]{1,0:T(8,128)(2,1)S(1)}, u32[]{:S(2)}, u32[]{:S(2)}) collective-permute-start(bf16[256,1024]{1,0:T(8,128)(2,1)S(1)} %copy-done.31), channel_id=1, source_target_pairs={{0,8},{8,16},{16,24},{24,0},{1,9},{9,17},{17,25},{25,1},{2,10},{10... | collective-permute-start | bytes 1572872 | tf_op jit(solution)/shard_map/cond/branch_0_fun/ppermute | solution.py:18
  (54 other events, 1674.1 us)
Sparse Core Ops, SparseCore 0:
  13.8 30.5 all-gather.8
  46.3 32.1 all-gather.10
  80.3 41.0 all-gather.12
  123.2 28.6 all-gather.14
where the time goes:
time: 777 us; the launch traced here: 769 us
  waiting for transfers between devices  524 us (67%)
  starting transfers between devices  96.6 us (12%)
  matrix products  61.6 us (8%)
  local copies, waits for them, and re-layouts  35.9 us (5%)
  other arithmetic  19.9 us (3%)
  between operations  17.9 us (2%)
  loops' own time  12.2 us (2%)
    ppermute x34, waiting for transfers between devices, shifted(): return lax.ppermute(value, axis, pairs)  492 us
    ppermute x34, starting transfers between devices, shifted(): return lax.ppermute(value, axis, pairs)  80.6 us
    dot_general x16, matrix products, pipeline(): lax.dot_general(cols, cot, tokens_axis, preferred_element_type=jnp.float32)  61.6 us
    all_to_all x4, waiting for transfers between devices, pipeline(): lax.all_to_all(piece, 'node', split_axis=1, concat_axis=0, tiled=True)  21.6 us
    dynamic_update_slice x15, other arithmetic, pipeline(): lax.dynamic_update_slice(mixed, total.astype(jnp.bfloat16), (start, b * c...  18.6 us
    all_to_all x4, starting transfers between devices, pipeline(): lax.all_to_all(piece, 'node', split_axis=1, concat_axis=0, tiled=True)  15.8 us
  transfers between devices with their start and end apart: 42, of which 14 were waited for; matrix products, arithmetic and copies ran while one was open for 14% of the time, Pallas kernels for 0%

commit v1 on v0

--- a/solution.py
+++ b/solution.py
@@ -8,7 +8,7 @@
 keep_share = 0.5
 back_share = 0.3
 front_share = 0.2
-tokens_axis = (((0,), (0,)), ((), ()))
+rows_by_tokens = (((1,), (0,)), ((), ()))
 col_blocks = 4
 
 
@@ -53,6 +53,7 @@
     sizes = row_sizes(rows_total)
     starts = [sum(sizes[:i]) for i in range(len(sizes))]
     columns = [None] * len(sizes)
+    weight_sent = None
     last = None
     for b in range(n_cols):
         span = slice(b * col_size, (b + 1) * col_size)
@@ -62,17 +63,20 @@
                 if last is not None:
                     piece, last = lax.optimization_barrier((piece, last))
                 cols = lax.all_to_all(piece, "node", split_axis=1, concat_axis=0, tiled=True)
-                columns[a] = cols.reshape(-1, size)
+                columns[a] = cols.reshape(-1, size).T
             cols, cot = columns[a], cots[b]
             if last is not None:
                 cols, cot, last = lax.optimization_barrier((cols, cot, last))
-            tok_group = cols.shape[0]
+            tok_group = cols.shape[1]
             rows = slice(start, start + size)
-            grad = lax.dot_general(cols, cot, tokens_axis, preferred_element_type=jnp.float32)
+            grad = lax.dot_general(cols, cot, rows_by_tokens, preferred_element_type=jnp.float32)
             grad = grad / tok_group
             renewed = moment_decay * momentum[0, rows, span].astype(jnp.float32) + grad
             half = (params[0, rows, span].astype(jnp.float32) - rate * renewed).astype(jnp.bfloat16)
             last = half
+            if weight_sent is None and b == 0 and a == len(sizes) - 1:
+                weight, last = lax.optimization_barrier((push_weight, last))
+                weight_sent = (shifted(weight, "grp", amount), shifted(weight, "grp", groups - amount))
             minus = shifted(half, "grp", amount)
             if paired:
                 peers = (back_share * minus.astype(jnp.float32)) + front_share * minus.astype(jnp.float32)
@@ -81,8 +85,7 @@
                 peers = w_minus * minus.astype(jnp.float32) + w_plus * plus.astype(jnp.float32)
             total = keep_share * half.astype(jnp.float32) + peers
             mixed = lax.dynamic_update_slice(mixed, total.astype(jnp.bfloat16), (start, b * col_size))
-    weight_minus = shifted(push_weight, "grp", amount)
-    weight_plus = shifted(push_weight, "grp", groups - amount)
+    weight_minus, weight_plus = weight_sent
     new_weight = keep_share * push_weight + w_minus * weight_minus + w_plus * weight_plus
     return mixed[None], new_weight
 

time: 777 us -> 756 us (0.973)
  starting transfers between devices: 96.6 us -> 67.3 us
  waiting for transfers between devices: 524 us -> 537 us
    ppermute x34, starting transfers between devices: 80.6 us -> 50.8 us  [shifted(): return lax.ppermute(value, axis, pairs)]
    ppermute x34, waiting for transfers between devices: 492 us -> 509 us  [shifted(): return lax.ppermute(value, axis, pairs)]
  transfers between devices with their start and end apart: 42 -> 42, of which waited for: 14 -> 16; matrix products, arithmetic and copies ran while one was open for 14% -> 14% of each run, Pallas kernels for 0% -> 0%
where the time goes in v1:
time: 756 us; the launch traced here: 748 us
  waiting for transfers between devices  537 us (71%)
  starting transfers between devices  67.3 us (9%)
  matrix products  60.4 us (8%)
  local copies, waits for them, and re-layouts  35.8 us (5%)
  other arithmetic  18.2 us (2%)
  between operations  17.7 us (2%)
  loops' own time  12.2 us (2%)
    ppermute x34, waiting for transfers between devices, shifted(): return lax.ppermute(value, axis, pairs)  509 us
    dot_general x16, matrix products, pipeline(): lax.dot_general(cols, cot, rows_by_tokens, preferred_element_type=jnp.flo...  60.4 us
    ppermute x34, starting transfers between devices, shifted(): return lax.ppermute(value, axis, pairs)  50.8 us
    dynamic_update_slice x15, other arithmetic, pipeline(): lax.dynamic_update_slice(mixed, total.astype(jnp.bfloat16), (start, b * c...  18.1 us
    all_to_all x4, starting transfers between devices, pipeline(): lax.all_to_all(piece, 'node', split_axis=1, concat_axis=0, tiled=True)  16.4 us
    all_to_all x4, waiting for transfers between devices, pipeline(): lax.all_to_all(piece, 'node', split_axis=1, concat_axis=0, tiled=True)  15.2 us
  transfers between devices with their start and end apart: 42, of which 16 were waited for; matrix products, arithmetic and copies ran while one was open for 14% of the time, Pallas kernels for 0%

profile of v1, /device:TPU:0, one launch (start us, length us, event | category | flops | bytes accessed | tf_op | source)
XLA Modules:
  0.0 748.1 jit_solution(4136827962681498814)
XLA Ops:
  11.0 729.2 %conditional.1 = (bf16[1,1792,4096]{2,1,0:T(8,128)(2,1)}, f32[1]{0:T(128)}) conditional(s32[]{:T(128)} %clamp.3, (bf16[1,1792,4096]{2,1,0:T(8,128)(2,1)}, f32[]{:T(128)}, bf16[1,1792,4096]{2,1,0:T(8,128)(2,1)}, bf16[1,128,14336]{2,1,0:T(8,128)(2,1)}, bf16[128,4096]{1,0:T(8,128)(2,1)}, /*index=5*/pred[]{:T(512)}, f32[1]{0:T(128)}) %tuple.93, ...), branch_computations={%region_0.1_spmd, %region_1.2_spmd} | conditional | flops 15157166080 | bytes 533467264 | solution.py:105
  14.8 6.1 copy.21
  22.5 5.2 all-to-all-start
  29.6 5.0 all-to-all-done
  34.8 9.6 %all-gather.9.cloned.1.call-done = bf16[1024,1024]{1,0:T(8,128)(2,1)} async-done(((bf16[128,1024]{1,0:T(8,128)(2,1)}), bf16[1024,1024]{1,0:T(8,128)(2,1)}) %all-gather.9.cloned.1.call-update) | async-done | bytes 2097168 | tf_op jit(solution)/shard_map/cond/branch_0_fun/all_gather | solution.py:49
  52.4 10.1 %all-to-all-done.1 = bf16[128,8,256]{0,2,1:T(8,128)(2,1)S(1)} async-done(((bf16[128,8,256]{0,2,1:T(8,128)(2,1)}), bf16[128,8,256]{0,2,1:T(8,128)(2,1)S(1)}, u32[]{:S(2)}, u32[]{:S(2)}) %all-to-all-start.1) | async-done | bytes 524320 | tf_op jit(solution)/shard_map/cond/branch_0_fun/all_to_all | solution.py:65
  84.7 6.2 collective-permute-done
  98.4 4.1 all-to-all-start.3
  102.5 7.3 pad_bitcast_fusion
  128.9 12.5 %collective-permute-done.5 = bf16[512,1024]{1,0:T(8,128)(2,1)S(1)} collective-permute-done((bf16[512,1024]{1,0:T(8,128)(2,1)S(1)}, bf16[512,1024]{1,0:T(8,128)(2,1)S(1)}, u32[]{:S(2)}, u32[]{:S(2)}) %collective-permute-start.5) | collective-permute-done | bytes 1048608 | tf_op jit(solution)/shard_map/cond/branch_0_fun/ppermute | solution.py:18
  144.8 19.3 %collective-permute-done.4 = bf16[512,1024]{1,0:T(8,128)(2,1)S(1)} collective-permute-done((bf16[512,1024]{1,0:T(8,128)(2,1)S(1)}, bf16[512,1024]{1,0:T(8,128)(2,1)S(1)}, u32[]{:S(2)}, u32[]{:S(2)}) %collective-permute-start.4) | collective-permute-done | bytes 1048608 | tf_op jit(solution)/shard_map/cond/branch_0_fun/ppermute | solution.py:18
  170.3 7.1 fusion.2
  186.2 6.0 fusion.3
  192.1 6.0 fusion.1
  206.7 30.3 %collective-permute-done.10 = bf16[256,1024]{1,0:T(8,128)(2,1)S(1)} collective-permute-done((bf16[256,1024]{1,0:T(8,128)(2,1)}, bf16[256,1024]{1,0:T(8,128)(2,1)S(1)}, u32[]{:S(2)}, u32[]{:S(2)}) %collective-permute-start.10) | collective-permute-done | bytes 524320 | tf_op jit(solution)/shard_map/cond/branch_0_fun/ppermute | solution.py:18
  242.3 117.9 %collective-permute-done.32 = f32[1]{0:T(128)} collective-permute-done((f32[1]{0:T(128)}, f32[1]{0:T(128)}, u32[]{:S(2)}, u32[]{:S(2)}) %collective-permute-start.32) | collective-permute-done | bytes 36 | tf_op jit(solution)/shard_map/cond/branch_0_fun/ppermute | solution.py:18
  368.8 5.0 collective-permute-done.16
  373.8 4.8 fusion
  379.8 37.3 %collective-permute-done.25 = bf16[128,1024]{1,0:T(8,128)(2,1)S(1)} collective-permute-done((bf16[128,1024]{1,0:T(8,128)(2,1)S(1)}, bf16[128,1024]{1,0:T(8,128)(2,1)S(1)}, u32[]{:S(2)}, u32[]{:S(2)}) %collective-permute-start.25) | collective-permute-done | bytes 262176 | tf_op jit(solution)/shard_map/cond/branch_0_fun/ppermute | solution.py:18
  421.1 25.8 %collective-permute-done.24 = bf16[128,1024]{1,0:T(8,128)(2,1)S(1)} collective-permute-done((bf16[128,1024]{1,0:T(8,128)(2,1)S(1)}, bf16[128,1024]{1,0:T(8,128)(2,1)S(1)}, u32[]{:S(2)}, u32[]{:S(2)}) %collective-permute-start.24) | collective-permute-done | bytes 262176 | tf_op jit(solution)/shard_map/cond/branch_0_fun/ppermute | solution.py:18
  463.0 120.4 %collective-permute-done.27 = bf16[256,1024]{1,0:T(8,128)(2,1)S(1)} collective-permute-done((bf16[256,1024]{1,0:T(8,128)(2,1)S(1)}, bf16[256,1024]{1,0:T(8,128)(2,1)S(1)}, u32[]{:S(2)}, u32[]{:S(2)}) %collective-permute-start.27) | collective-permute-done | bytes 524320 | tf_op jit(solution)/shard_map/cond/branch_0_fun/ppermute | solution.py:18
  583.4 4.3 collective-permute-start.31
  594.2 128.4 %collective-permute-done.26 = bf16[256,1024]{1,0:T(8,128)(2,1)S(1)} collective-permute-done((bf16[256,1024]{1,0:T(8,128)(2,1)S(1)}, bf16[256,1024]{1,0:T(8,128)(2,1)S(1)}, u32[]{:S(2)}, u32[]{:S(2)}) %collective-permute-start.26) | collective-permute-done | bytes 524320 | tf_op jit(solution)/shard_map/cond/branch_0_fun/ppermute | solution.py:18
  725.0 5.5 copy-done
  (150 shorter events, 134.0 us)
Async XLA Ops:
  14.0 163.4 %all-gather.13.cloned.1.call-start = ((), (), s32[]{:S(2)}) async-start(), calls=%async_computation.10 | async-start | bytes 2359296 | tf_op jit(solution)/shard_map/cond/branch_0_fun/all_gather | solution.py:49
  70.0 128.2 %all-gather.15.cloned.1.call-start = ((), (), s32[]{:S(2)}) async-start(), calls=%async_computation.11 | async-start | bytes 2359296 | tf_op jit(solution)/shard_map/cond/branch_0_fun/all_gather | solution.py:49
  81.3 116.8 %collective-permute-start.9 = (bf16[128,1024]{1,0:T(8,128)(2,1)}, bf16[128,1024]{1,0:T(8,128)(2,1)}, u32[]{:S(2)}, u32[]{:S(2)}) collective-permute-start(bf16[128,1024]{1,0:T(8,128)(2,1)} %fusion.53), channel_id=1, source_target_pairs={{0,24},{8,0},{16,8},{24,16},{1,25},{9,1},{17,9},{25,17},{2,26},{10... | collective-permute-start | bytes 786440 | tf_op jit(solution)/shard_map/cond/branch_0_fun/ppermute | solution.py:18
  98.4 69.3 %all-to-all-start.3 = ((bf16[128,8,896]{0,2,1:T(8,128)(2,1)}), bf16[128,8,896]{0,2,1:T(8,128)(2,1)S(1)}, u32[]{:S(2)}, u32[]{:S(2)}) async-start(bf16[128,8,896]{0,2,1:T(8,128)(2,1)} %slice.243), calls=%async_computation.3 | async-start | bytes 3670016 | tf_op jit(solution)/shard_map/cond/branch_0_fun/all_to_all | solution.py:65
  116.3 82.9 %collective-permute-start.8 = (bf16[128,1024]{1,0:T(8,128)(2,1)}, bf16[128,1024]{1,0:T(8,128)(2,1)}, u32[]{:S(2)}, u32[]{:S(2)}) collective-permute-start(bf16[128,1024]{1,0:T(8,128)(2,1)} %fusion.53), channel_id=1, source_target_pairs={{0,8},{8,16},{16,24},{24,0},{1,9},{9,17},{17,25},{25,1},{2,10},{10... | collective-permute-start | bytes 786440 | tf_op jit(solution)/shard_map/cond/branch_0_fun/ppermute | solution.py:18
  119.1 83.0 %collective-permute-start.11 = (bf16[256,1024]{1,0:T(8,128)(2,1)}, bf16[256,1024]{1,0:T(8,128)(2,1)}, u32[]{:S(2)}, u32[]{:S(2)}) collective-permute-start(bf16[256,1024]{1,0:T(8,128)(2,1)} %fusion.37), channel_id=1, source_target_pairs={{0,24},{8,0},{16,8},{24,16},{1,25},{9,1},{17,9},{25,17},{2,26},{10... | collective-permute-start | bytes 1572872 | tf_op jit(solution)/shard_map/cond/branch_0_fun/ppermute | solution.py:18
  141.4 98.8 %collective-permute-start.13 = (bf16[512,1024]{1,0:T(8,128)(2,1)}, bf16[512,1024]{1,0:T(8,128)(2,1)}, u32[]{:S(2)}, u32[]{:S(2)}) collective-permute-start(bf16[512,1024]{1,0:T(8,128)(2,1)} %fusion.10), channel_id=1, source_target_pairs={{0,24},{8,0},{16,8},{24,16},{1,25},{9,1},{17,9},{25,17},{2,26},{10... | collective-permute-start | bytes 3145736 | tf_op jit(solution)/shard_map/cond/branch_0_fun/ppermute | solution.py:18
  164.1 76.7 %collective-permute-start.12 = (bf16[512,1024]{1,0:T(8,128)(2,1)}, bf16[512,1024]{1,0:T(8,128)(2,1)}, u32[]{:S(2)}, u32[]{:S(2)}) collective-permute-start(bf16[512,1024]{1,0:T(8,128)(2,1)} %fusion.10), channel_id=1, source_target_pairs={{0,8},{8,16},{16,24},{24,0},{1,9},{9,17},{17,25},{25,1},{2,10},{10... | collective-permute-start | bytes 3145736 | tf_op jit(solution)/shard_map/cond/branch_0_fun/ppermute | solution.py:18
  199.2 219.4 %collective-permute-start.7 = (bf16[896,1024]{1,0:T(8,128)(2,1)}, bf16[896,1024]{1,0:T(8,128)(2,1)S(1)}, u32[]{:S(2)}, u32[]{:S(2)}) collective-permute-start(bf16[896,1024]{1,0:T(8,128)(2,1)} %fusion.3), channel_id=1, source_target_pairs={{0,24},{8,0},{16,8},{24,16},{1,25},{9,1},{17,9},{25,17},{2,26},{10... | collective-permute-start | bytes 5505032 | tf_op jit(solution)/shard_map/cond/branch_0_fun/ppermute | solution.py:18
  202.1 217.1 %collective-permute-start.6 = (bf16[896,1024]{1,0:T(8,128)(2,1)}, bf16[896,1024]{1,0:T(8,128)(2,1)S(1)}, u32[]{:S(2)}, u32[]{:S(2)}) collective-permute-start(bf16[896,1024]{1,0:T(8,128)(2,1)} %fusion.3), channel_id=1, source_target_pairs={{0,8},{8,16},{16,24},{24,0},{1,9},{9,17},{17,25},{25,1},{2,10},{10... | collective-permute-start | bytes 5505032 | tf_op jit(solution)/shard_map/cond/branch_0_fun/ppermute | solution.py:18
  237.0 217.1 %collective-permute-start.15 = (bf16[896,1024]{1,0:T(8,128)(2,1)S(1)}, bf16[896,1024]{1,0:T(8,128)(2,1)S(1)}, u32[]{:S(2)}, u32[]{:S(2)}) collective-permute-start(bf16[896,1024]{1,0:T(8,128)(2,1)S(1)} %copy-done.13), channel_id=1, source_target_pairs={{0,24},{8,0},{16,8},{24,16},{1,25},{9,1},{17,9},{25,17},{2,26},{10... | collective-permute-start | bytes 5505032 | tf_op jit(solution)/shard_map/cond/branch_0_fun/ppermute | solution.py:18
  240.3 128.5 %collective-permute-start.17 = (bf16[128,1024]{1,0:T(8,128)(2,1)S(1)}, bf16[128,1024]{1,0:T(8,128)(2,1)S(1)}, u32[]{:S(2)}, u32[]{:S(2)}) collective-permute-start(bf16[128,1024]{1,0:T(8,128)(2,1)S(1)} %fusion.54), channel_id=1, source_target_pairs={{0,24},{8,0},{16,8},{24,16},{1,25},{9,1},{17,9},{25,17},{2,26},{10... | collective-permute-start | bytes 786440 | tf_op jit(solution)/shard_map/cond/branch_0_fun/ppermute | solution.py:18
  240.8 119.4 %collective-permute-start.32 = (f32[1]{0:T(128)}, f32[1]{0:T(128)}, u32[]{:S(2)}, u32[]{:S(2)}) collective-permute-start(f32[1]{0:T(128)} %get-tuple-element.68), channel_id=1, source_target_pairs={{0,8},{8,16},{16,24},{24,0},{1,9},{9,17},{17,25},{25,1},{2,10},{10... | collective-permute-start | bytes 20 | tf_op jit(solution)/shard_map/cond/branch_0_fun/ppermute | solution.py:18
  368.7 88.0 %collective-permute-start.14 = (bf16[896,1024]{1,0:T(8,128)(2,1)S(1)}, bf16[896,1024]{1,0:T(8,128)(2,1)S(1)}, u32[]{:S(2)}, u32[]{:S(2)}) collective-permute-start(bf16[896,1024]{1,0:T(8,128)(2,1)S(1)} %copy-done.13), channel_id=1, source_target_pairs={{0,8},{8,16},{16,24},{24,0},{1,9},{9,17},{17,25},{25,1},{2,10},{10... | collective-permute-start | bytes 5505032 | tf_op jit(solution)/shard_map/cond/branch_0_fun/ppermute | solution.py:18
  446.9 145.0 %collective-permute-start.23 = (bf16[896,1024]{1,0:T(8,128)(2,1)S(1)}, bf16[896,1024]{1,0:T(8,128)(2,1)S(1)}, u32[]{:S(2)}, u32[]{:S(2)}) collective-permute-start(bf16[896,1024]{1,0:T(8,128)(2,1)S(1)} %copy-done.12), channel_id=1, source_target_pairs={{0,24},{8,0},{16,8},{24,16},{1,25},{9,1},{17,9},{25,17},{2,26},{10... | collective-permute-start | bytes 5505032 | tf_op jit(solution)/shard_map/cond/branch_0_fun/ppermute | solution.py:18
  450.5 137.2 %collective-permute-start.21 = (bf16[512,1024]{1,0:T(8,128)(2,1)S(1)}, bf16[512,1024]{1,0:T(8,128)(2,1)S(1)}, u32[]{:S(2)}, u32[]{:S(2)}) collective-permute-start(bf16[512,1024]{1,0:T(8,128)(2,1)S(1)} %fusion.9), channel_id=1, source_target_pairs={{0,24},{8,0},{16,8},{24,16},{1,25},{9,1},{17,9},{25,17},{2,26},{10... | collective-permute-start | bytes 3145736 | tf_op jit(solution)/shard_map/cond/branch_0_fun/ppermute | solution.py:18
  451.8 140.8 %collective-permute-start.22 = (bf16[896,1024]{1,0:T(8,128)(2,1)S(1)}, bf16[896,1024]{1,0:T(8,128)(2,1)S(1)}, u32[]{:S(2)}, u32[]{:S(2)}) collective-permute-start(bf16[896,1024]{1,0:T(8,128)(2,1)S(1)} %copy-done.12), channel_id=1, source_target_pairs={{0,8},{8,16},{16,24},{24,0},{1,9},{9,17},{17,25},{25,1},{2,10},{10... | collective-permute-start | bytes 5505032 | tf_op jit(solution)/shard_map/cond/branch_0_fun/ppermute | solution.py:18
  454.1 133.9 %collective-permute-start.20 = (bf16[512,1024]{1,0:T(8,128)(2,1)S(1)}, bf16[512,1024]{1,0:T(8,128)(2,1)S(1)}, u32[]{:S(2)}, u32[]{:S(2)}) collective-permute-start(bf16[512,1024]{1,0:T(8,128)(2,1)S(1)} %fusion.9), channel_id=1, source_target_pairs={{0,8},{8,16},{16,24},{24,0},{1,9},{9,17},{17,25},{25,1},{2,10},{10... | collective-permute-start | bytes 3145736 | tf_op jit(solution)/shard_map/cond/branch_0_fun/ppermute | solution.py:18
  456.7 126.7 %collective-permute-start.27 = (bf16[256,1024]{1,0:T(8,128)(2,1)S(1)}, bf16[256,1024]{1,0:T(8,128)(2,1)S(1)}, u32[]{:S(2)}, u32[]{:S(2)}) collective-permute-start(bf16[256,1024]{1,0:T(8,128)(2,1)S(1)} %fusion.39), channel_id=1, source_target_pairs={{0,24},{8,0},{16,8},{24,16},{1,25},{9,1},{17,9},{25,17},{2,26},{10... | collective-permute-start | bytes 1572872 | tf_op jit(solution)/shard_map/cond/branch_0_fun/ppermute | solution.py:18
  583.4 140.2 %collective-permute-start.31 = (bf16[896,1024]{1,0:T(8,128)(2,1)S(1)}, bf16[896,1024]{1,0:T(8,128)(2,1)S(1)}, u32[]{:S(2)}, u32[]{:S(2)}) collective-permute-start(bf16[896,1024]{1,0:T(8,128)(2,1)S(1)} %fusion), channel_id=1, source_target_pairs={{0,24},{8,0},{16,8},{24,16},{1,25},{9,1},{17,9},{25,17},{2,26},{10... | collective-permute-start | bytes 5505032 | tf_op jit(solution)/shard_map/cond/branch_0_fun/ppermute | solution.py:18
  587.7 135.9 %collective-permute-start.30 = (bf16[896,1024]{1,0:T(8,128)(2,1)S(1)}, bf16[896,1024]{1,0:T(8,128)(2,1)S(1)}, u32[]{:S(2)}, u32[]{:S(2)}) collective-permute-start(bf16[896,1024]{1,0:T(8,128)(2,1)S(1)} %fusion), channel_id=1, source_target_pairs={{0,8},{8,16},{16,24},{24,0},{1,9},{9,17},{17,25},{25,1},{2,10},{10... | collective-permute-start | bytes 5505032 | tf_op jit(solution)/shard_map/cond/branch_0_fun/ppermute | solution.py:18
  588.0 134.9 %collective-permute-start.29 = (bf16[512,1024]{1,0:T(8,128)(2,1)S(1)}, bf16[512,1024]{1,0:T(8,128)(2,1)S(1)}, u32[]{:S(2)}, u32[]{:S(2)}) collective-permute-start(bf16[512,1024]{1,0:T(8,128)(2,1)S(1)} %fusion.8), channel_id=1, source_target_pairs={{0,24},{8,0},{16,8},{24,16},{1,25},{9,1},{17,9},{25,17},{2,26},{10... | collective-permute-start | bytes 3145736 | tf_op jit(solution)/shard_map/cond/branch_0_fun/ppermute | solution.py:18
  591.9 131.0 %collective-permute-start.28 = (bf16[512,1024]{1,0:T(8,128)(2,1)S(1)}, bf16[512,1024]{1,0:T(8,128)(2,1)S(1)}, u32[]{:S(2)}, u32[]{:S(2)}) collective-permute-start(bf16[512,1024]{1,0:T(8,128)(2,1)S(1)} %fusion.8), channel_id=1, source_target_pairs={{0,8},{8,16},{16,24},{24,0},{1,9},{9,17},{17,25},{25,1},{2,10},{10... | collective-permute-start | bytes 3145736 | tf_op jit(solution)/shard_map/cond/branch_0_fun/ppermute | solution.py:18
  592.6 130.0 %collective-permute-start.26 = (bf16[256,1024]{1,0:T(8,128)(2,1)S(1)}, bf16[256,1024]{1,0:T(8,128)(2,1)S(1)}, u32[]{:S(2)}, u32[]{:S(2)}) collective-permute-start(bf16[256,1024]{1,0:T(8,128)(2,1)S(1)} %fusion.39), channel_id=1, source_target_pairs={{0,8},{8,16},{16,24},{24,0},{1,9},{9,17},{17,25},{25,1},{2,10},{10... | collective-permute-start | bytes 1572872 | tf_op jit(solution)/shard_map/cond/branch_0_fun/ppermute | solution.py:18
  (38 other events, 1129.8 us)
Sparse Core Ops, SparseCore 0:
  13.8 30.5 all-gather.8
  46.3 32.1 all-gather.10
  80.3 34.8 all-gather.12
  116.9 38.4 all-gather.14

commit v2 on v1

--- a/solution.py
+++ b/solution.py
@@ -59,11 +59,17 @@
         span = slice(b * col_size, (b + 1) * col_size)
         for a, (start, size) in enumerate(zip(starts, sizes)):
             if columns[a] is None:
-                piece = acts[:, :, start:start + size]
+                members = [0, 1][:len(sizes)] if a == 0 else [a]
+                width_a = sum(sizes[m] for m in members)
+                piece = acts[:, :, start:start + width_a]
                 if last is not None:
                     piece, last = lax.optimization_barrier((piece, last))
                 cols = lax.all_to_all(piece, "node", split_axis=1, concat_axis=0, tiled=True)
-                columns[a] = cols.reshape(-1, size).T
+                cols = cols.reshape(-1, width_a).T
+                offset_a = 0
+                for m in members:
+                    columns[m] = cols[offset_a:offset_a + sizes[m]]
+                    offset_a += sizes[m]
             cols, cot = columns[a], cots[b]
             if last is not None:
                 cols, cot, last = lax.optimization_barrier((cols, cot, last))

time: 756 us -> 742 us (0.981)
  waiting for transfers between devices: 537 us -> 527 us
    ppermute x34, waiting for transfers between devices: 509 us -> 494 us  [shifted(): return lax.ppermute(value, axis, pairs)]
    all_gather x4, waiting for transfers between devices: 10.4 us -> 18.3 us  [pipeline(): lax.all_gather(cotangent[:, b * col_size:(b + 1) * col_size], 'node', axi...]
    all_to_all x4 -> x3, starting transfers between devices: 16.4 us -> 12.3 us  [pipeline(): lax.all_to_all(piece, 'node', split_axis=1, concat_axis=0, tiled=True)]
    all_to_all x4 -> x3, waiting for transfers between devices: 15.2 us -> 13.3 us  [pipeline(): lax.all_to_all(piece, 'node', split_axis=1, concat_axis=0, tiled=True)]
  transfers between devices with their start and end apart: 42 -> 41, of which waited for: 16 -> 13; matrix products, arithmetic and copies ran while one was open for 14% -> 14% of each run, Pallas kernels for 0% -> 0%
where the time goes in v2:
time: 742 us; the launch traced here: 734 us
  waiting for transfers between devices  527 us (71%)
  starting transfers between devices  64.5 us (9%)
  matrix products  59.3 us (8%)
  local copies, waits for them, and re-layouts  34.3 us (5%)
  other arithmetic  18.7 us (3%)
  between operations  17.7 us (2%)
  loops' own time  12.3 us (2%)
    ppermute x34, waiting for transfers between devices, shifted(): return lax.ppermute(value, axis, pairs)  494 us
    dot_general x16, matrix products, pipeline(): lax.dot_general(cols, cot, rows_by_tokens, preferred_element_type=jnp.flo...  59.3 us
    ppermute x34, starting transfers between devices, shifted(): return lax.ppermute(value, axis, pairs)  52 us
    dynamic_update_slice x15, other arithmetic, pipeline(): lax.dynamic_update_slice(mixed, total.astype(jnp.bfloat16), (start, b * c...  18.5 us
    all_gather x4, waiting for transfers between devices, pipeline(): lax.all_gather(cotangent[:, b * col_size:(b + 1) * col_size], 'node', axi...  18.3 us
  transfers between devices with their start and end apart: 41, of which 13 were waited for; matrix products, arithmetic and copies ran while one was open for 14% of the time, Pallas kernels for 0%

profile of v2, /device:TPU:0, one launch (start us, length us, event | category | flops | bytes accessed | tf_op | source)
XLA Modules:
  0.0 734.1 jit_solution(13898739717720220064)
XLA Ops:
  11.0 715.2 %conditional.1 = (bf16[1,1792,4096]{2,1,0:T(8,128)(2,1)}, f32[1]{0:T(128)}) conditional(s32[]{:T(128)} %clamp.3, (bf16[1,1792,4096]{2,1,0:T(8,128)(2,1)}, f32[]{:T(128)}, bf16[1,1792,4096]{2,1,0:T(8,128)(2,1)}, bf16[1,128,14336]{2,1,0:T(8,128)(2,1)}, bf16[128,4096]{1,0:T(8,128)(2,1)}, /*index=5*/pred[]{:T(512)}, f32[1]{0:T(128)}) %tuple.89, ...), branch_computations={%region_0.1_spmd, %region_1.2_spmd} | conditional | flops 15157166080 | bytes 549720256 | solution.py:111
  14.8 6.1 copy.19
  22.9 5.2 all-to-all-start
  30.4 13.3 %all-to-all-done = bf16[128,8,384]{0,2,1:T(8,128)(2,1)S(1)} async-done(((bf16[128,8,384]{0,2,1:T(8,128)(2,1)}), bf16[128,8,384]{0,2,1:T(8,128)(2,1)S(1)}, u32[]{:S(2)}, u32[]{:S(2)}) %all-to-all-start) | async-done | bytes 786464 | tf_op jit(solution)/shard_map/cond/branch_0_fun/all_to_all | solution.py:67
  67.5 15.4 %all-gather.11.cloned.1.call-done = bf16[1024,1024]{1,0:T(8,128)(2,1)} async-done(((bf16[128,1024]{1,0:T(8,128)(2,1)}), bf16[1024,1024]{1,0:T(8,128)(2,1)}) %all-gather.11.cloned.1.call-update) | async-done | bytes 2097168 | tf_op jit(solution)/shard_map/cond/branch_0_fun/all_gather | solution.py:49
  93.6 4.0 fusion.11
  103.3 7.3 pad_bitcast_fusion
  116.9 4.3 fusion.10
  121.2 6.3 collective-permute-done.5
  131.0 19.1 %collective-permute-done.4 = bf16[512,1024]{1,0:T(8,128)(2,1)} collective-permute-done((bf16[512,1024]{1,0:T(8,128)(2,1)S(1)}, bf16[512,1024]{1,0:T(8,128)(2,1)}, u32[]{:S(2)}, u32[]{:S(2)}) %collective-permute-start.4) | collective-permute-done | bytes 1048608 | tf_op jit(solution)/shard_map/cond/branch_0_fun/ppermute | solution.py:18
  158.1 7.2 fusion.2
  173.9 6.0 fusion.3
  179.9 6.0 fusion.1
  194.4 28.6 %collective-permute-done.10 = bf16[256,1024]{1,0:T(8,128)(2,1)S(1)} collective-permute-done((bf16[256,1024]{1,0:T(8,128)(2,1)}, bf16[256,1024]{1,0:T(8,128)(2,1)S(1)}, u32[]{:S(2)}, u32[]{:S(2)}) %collective-permute-start.10) | collective-permute-done | bytes 524320 | tf_op jit(solution)/shard_map/cond/branch_0_fun/ppermute | solution.py:18
  228.1 118.2 %collective-permute-done.32 = f32[1]{0:T(128)} collective-permute-done((f32[1]{0:T(128)}, f32[1]{0:T(128)}, u32[]{:S(2)}, u32[]{:S(2)}) %collective-permute-start.32) | collective-permute-done | bytes 36 | tf_op jit(solution)/shard_map/cond/branch_0_fun/ppermute | solution.py:18
  354.8 4.5 collective-permute-done.16
  359.3 4.8 fusion
  365.4 37.7 %collective-permute-done.25 = bf16[128,1024]{1,0:T(8,128)(2,1)S(1)} collective-permute-done((bf16[128,1024]{1,0:T(8,128)(2,1)S(1)}, bf16[128,1024]{1,0:T(8,128)(2,1)S(1)}, u32[]{:S(2)}, u32[]{:S(2)}) %collective-permute-start.25) | collective-permute-done | bytes 262176 | tf_op jit(solution)/shard_map/cond/branch_0_fun/ppermute | solution.py:18
  407.0 25.8 %collective-permute-done.24 = bf16[128,1024]{1,0:T(8,128)(2,1)S(1)} collective-permute-done((bf16[128,1024]{1,0:T(8,128)(2,1)S(1)}, bf16[128,1024]{1,0:T(8,128)(2,1)S(1)}, u32[]{:S(2)}, u32[]{:S(2)}) %collective-permute-start.24) | collective-permute-done | bytes 262176 | tf_op jit(solution)/shard_map/cond/branch_0_fun/ppermute | solution.py:18
  447.9 121.5 %collective-permute-done.27 = bf16[256,1024]{1,0:T(8,128)(2,1)S(1)} collective-permute-done((bf16[256,1024]{1,0:T(8,128)(2,1)S(1)}, bf16[256,1024]{1,0:T(8,128)(2,1)S(1)}, u32[]{:S(2)}, u32[]{:S(2)}) %collective-permute-start.27) | collective-permute-done | bytes 524320 | tf_op jit(solution)/shard_map/cond/branch_0_fun/ppermute | solution.py:18
  569.4 4.3 collective-permute-start.31
  574.0 3.9 collective-permute-start.29
  580.2 128.4 %collective-permute-done.26 = bf16[256,1024]{1,0:T(8,128)(2,1)S(1)} collective-permute-done((bf16[256,1024]{1,0:T(8,128)(2,1)S(1)}, bf16[256,1024]{1,0:T(8,128)(2,1)S(1)}, u32[]{:S(2)}, u32[]{:S(2)}) %collective-permute-start.26) | collective-permute-done | bytes 524320 | tf_op jit(solution)/shard_map/cond/branch_0_fun/ppermute | solution.py:18
  711.0 5.5 copy-done
  (152 shorter events, 120.9 us)
Async XLA Ops:
  13.3 69.6 %all-gather.11.cloned.1.call-start = ((), (), s32[]{:S(2)}) async-start(), calls=%async_computation.7 | async-start | bytes 2359296 | tf_op jit(solution)/shard_map/cond/branch_0_fun/all_gather | solution.py:49
  14.0 151.2 %all-gather.13.cloned.1.call-start = ((), (), s32[]{:S(2)}) async-start(), calls=%async_computation.8 | async-start | bytes 2359296 | tf_op jit(solution)/shard_map/cond/branch_0_fun/all_gather | solution.py:49
  55.7 130.2 %all-gather.15.cloned.1.call-start = ((), (), s32[]{:S(2)}) async-start(), calls=%async_computation.9 | async-start | bytes 2359296 | tf_op jit(solution)/shard_map/cond/branch_0_fun/all_gather | solution.py:49
  85.9 100.0 %collective-permute-start.9 = (bf16[128,1024]{1,0:T(8,128)(2,1)}, bf16[128,1024]{1,0:T(8,128)(2,1)}, u32[]{:S(2)}, u32[]{:S(2)}) collective-permute-start(bf16[128,1024]{1,0:T(8,128)(2,1)} %fusion.53), channel_id=1, source_target_pairs={{0,24},{8,0},{16,8},{24,16},{1,25},{9,1},{17,9},{25,17},{2,26},{10... | collective-permute-start | bytes 786440 | tf_op jit(solution)/shard_map/cond/branch_0_fun/ppermute | solution.py:18
  110.6 76.3 %collective-permute-start.8 = (bf16[128,1024]{1,0:T(8,128)(2,1)}, bf16[128,1024]{1,0:T(8,128)(2,1)}, u32[]{:S(2)}, u32[]{:S(2)}) collective-permute-start(bf16[128,1024]{1,0:T(8,128)(2,1)} %fusion.53), channel_id=1, source_target_pairs={{0,8},{8,16},{16,24},{24,0},{1,9},{9,17},{17,25},{25,1},{2,10},{10... | collective-permute-start | bytes 786440 | tf_op jit(solution)/shard_map/cond/branch_0_fun/ppermute | solution.py:18
  110.6 79.2 %collective-permute-start.11 = (bf16[256,1024]{1,0:T(8,128)(2,1)}, bf16[256,1024]{1,0:T(8,128)(2,1)}, u32[]{:S(2)}, u32[]{:S(2)}) collective-permute-start(bf16[256,1024]{1,0:T(8,128)(2,1)} %fusion.37), channel_id=1, source_target_pairs={{0,24},{8,0},{16,8},{24,16},{1,25},{9,1},{17,9},{25,17},{2,26},{10... | collective-permute-start | bytes 1572872 | tf_op jit(solution)/shard_map/cond/branch_0_fun/ppermute | solution.py:18
  127.6 98.5 %collective-permute-start.13 = (bf16[512,1024]{1,0:T(8,128)(2,1)}, bf16[512,1024]{1,0:T(8,128)(2,1)}, u32[]{:S(2)}, u32[]{:S(2)}) collective-permute-start(bf16[512,1024]{1,0:T(8,128)(2,1)} %fusion.10), channel_id=1, source_target_pairs={{0,24},{8,0},{16,8},{24,16},{1,25},{9,1},{17,9},{25,17},{2,26},{10... | collective-permute-start | bytes 3145736 | tf_op jit(solution)/shard_map/cond/branch_0_fun/ppermute | solution.py:18
  150.1 76.9 %collective-permute-start.12 = (bf16[512,1024]{1,0:T(8,128)(2,1)}, bf16[512,1024]{1,0:T(8,128)(2,1)}, u32[]{:S(2)}, u32[]{:S(2)}) collective-permute-start(bf16[512,1024]{1,0:T(8,128)(2,1)} %fusion.10), channel_id=1, source_target_pairs={{0,8},{8,16},{16,24},{24,0},{1,9},{9,17},{17,25},{25,1},{2,10},{10... | collective-permute-start | bytes 3145736 | tf_op jit(solution)/shard_map/cond/branch_0_fun/ppermute | solution.py:18
  187.0 217.6 %collective-permute-start.7 = (bf16[896,1024]{1,0:T(8,128)(2,1)}, bf16[896,1024]{1,0:T(8,128)(2,1)S(1)}, u32[]{:S(2)}, u32[]{:S(2)}) collective-permute-start(bf16[896,1024]{1,0:T(8,128)(2,1)} %fusion.3), channel_id=1, source_target_pairs={{0,24},{8,0},{16,8},{24,16},{1,25},{9,1},{17,9},{25,17},{2,26},{10... | collective-permute-start | bytes 5505032 | tf_op jit(solution)/shard_map/cond/branch_0_fun/ppermute | solution.py:18
  189.8 215.3 %collective-permute-start.6 = (bf16[896,1024]{1,0:T(8,128)(2,1)}, bf16[896,1024]{1,0:T(8,128)(2,1)S(1)}, u32[]{:S(2)}, u32[]{:S(2)}) collective-permute-start(bf16[896,1024]{1,0:T(8,128)(2,1)} %fusion.3), channel_id=1, source_target_pairs={{0,8},{8,16},{16,24},{24,0},{1,9},{9,17},{17,25},{25,1},{2,10},{10... | collective-permute-start | bytes 5505032 | tf_op jit(solution)/shard_map/cond/branch_0_fun/ppermute | solution.py:18
  223.0 216.9 %collective-permute-start.15 = (bf16[896,1024]{1,0:T(8,128)(2,1)S(1)}, bf16[896,1024]{1,0:T(8,128)(2,1)S(1)}, u32[]{:S(2)}, u32[]{:S(2)}) collective-permute-start(bf16[896,1024]{1,0:T(8,128)(2,1)S(1)} %copy-done.16), channel_id=1, source_target_pairs={{0,24},{8,0},{16,8},{24,16},{1,25},{9,1},{17,9},{25,17},{2,26},{10... | collective-permute-start | bytes 5505032 | tf_op jit(solution)/shard_map/cond/branch_0_fun/ppermute | solution.py:18
  226.0 128.7 %collective-permute-start.17 = (bf16[128,1024]{1,0:T(8,128)(2,1)S(1)}, bf16[128,1024]{1,0:T(8,128)(2,1)S(1)}, u32[]{:S(2)}, u32[]{:S(2)}) collective-permute-start(bf16[128,1024]{1,0:T(8,128)(2,1)S(1)} %fusion.54), channel_id=1, source_target_pairs={{0,24},{8,0},{16,8},{24,16},{1,25},{9,1},{17,9},{25,17},{2,26},{10... | collective-permute-start | bytes 786440 | tf_op jit(solution)/shard_map/cond/branch_0_fun/ppermute | solution.py:18
  227.0 119.2 %collective-permute-start.32 = (f32[1]{0:T(128)}, f32[1]{0:T(128)}, u32[]{:S(2)}, u32[]{:S(2)}) collective-permute-start(f32[1]{0:T(128)} %get-tuple-element.67), channel_id=1, source_target_pairs={{0,8},{8,16},{16,24},{24,0},{1,9},{9,17},{17,25},{25,1},{2,10},{10... | collective-permute-start | bytes 20 | tf_op jit(solution)/shard_map/cond/branch_0_fun/ppermute | solution.py:18
  354.7 87.8 %collective-permute-start.14 = (bf16[896,1024]{1,0:T(8,128)(2,1)S(1)}, bf16[896,1024]{1,0:T(8,128)(2,1)S(1)}, u32[]{:S(2)}, u32[]{:S(2)}) collective-permute-start(bf16[896,1024]{1,0:T(8,128)(2,1)S(1)} %copy-done.16), channel_id=1, source_target_pairs={{0,8},{8,16},{16,24},{24,0},{1,9},{9,17},{17,25},{25,1},{2,10},{10... | collective-permute-start | bytes 5505032 | tf_op jit(solution)/shard_map/cond/branch_0_fun/ppermute | solution.py:18
  432.9 145.0 %collective-permute-start.23 = (bf16[896,1024]{1,0:T(8,128)(2,1)S(1)}, bf16[896,1024]{1,0:T(8,128)(2,1)S(1)}, u32[]{:S(2)}, u32[]{:S(2)}) collective-permute-start(bf16[896,1024]{1,0:T(8,128)(2,1)S(1)} %copy-done.15), channel_id=1, source_target_pairs={{0,24},{8,0},{16,8},{24,16},{1,25},{9,1},{17,9},{25,17},{2,26},{10... | collective-permute-start | bytes 5505032 | tf_op jit(solution)/shard_map/cond/branch_0_fun/ppermute | solution.py:18
  436.5 137.2 %collective-permute-start.21 = (bf16[512,1024]{1,0:T(8,128)(2,1)S(1)}, bf16[512,1024]{1,0:T(8,128)(2,1)S(1)}, u32[]{:S(2)}, u32[]{:S(2)}) collective-permute-start(bf16[512,1024]{1,0:T(8,128)(2,1)S(1)} %fusion.9), channel_id=1, source_target_pairs={{0,24},{8,0},{16,8},{24,16},{1,25},{9,1},{17,9},{25,17},{2,26},{10... | collective-permute-start | bytes 3145736 | tf_op jit(solution)/shard_map/cond/branch_0_fun/ppermute | solution.py:18
  437.8 140.8 %collective-permute-start.22 = (bf16[896,1024]{1,0:T(8,128)(2,1)S(1)}, bf16[896,1024]{1,0:T(8,128)(2,1)S(1)}, u32[]{:S(2)}, u32[]{:S(2)}) collective-permute-start(bf16[896,1024]{1,0:T(8,128)(2,1)S(1)} %copy-done.15), channel_id=1, source_target_pairs={{0,8},{8,16},{16,24},{24,0},{1,9},{9,17},{17,25},{25,1},{2,10},{10... | collective-permute-start | bytes 5505032 | tf_op jit(solution)/shard_map/cond/branch_0_fun/ppermute | solution.py:18
  439.9 134.1 %collective-permute-start.20 = (bf16[512,1024]{1,0:T(8,128)(2,1)S(1)}, bf16[512,1024]{1,0:T(8,128)(2,1)S(1)}, u32[]{:S(2)}, u32[]{:S(2)}) collective-permute-start(bf16[512,1024]{1,0:T(8,128)(2,1)S(1)} %fusion.9), channel_id=1, source_target_pairs={{0,8},{8,16},{16,24},{24,0},{1,9},{9,17},{17,25},{25,1},{2,10},{10... | collective-permute-start | bytes 3145736 | tf_op jit(solution)/shard_map/cond/branch_0_fun/ppermute | solution.py:18
  442.5 126.8 %collective-permute-start.27 = (bf16[256,1024]{1,0:T(8,128)(2,1)S(1)}, bf16[256,1024]{1,0:T(8,128)(2,1)S(1)}, u32[]{:S(2)}, u32[]{:S(2)}) collective-permute-start(bf16[256,1024]{1,0:T(8,128)(2,1)S(1)} %fusion.39), channel_id=1, source_target_pairs={{0,24},{8,0},{16,8},{24,16},{1,25},{9,1},{17,9},{25,17},{2,26},{10... | collective-permute-start | bytes 1572872 | tf_op jit(solution)/shard_map/cond/branch_0_fun/ppermute | solution.py:18
  569.4 140.2 %collective-permute-start.31 = (bf16[896,1024]{1,0:T(8,128)(2,1)S(1)}, bf16[896,1024]{1,0:T(8,128)(2,1)S(1)}, u32[]{:S(2)}, u32[]{:S(2)}) collective-permute-start(bf16[896,1024]{1,0:T(8,128)(2,1)S(1)} %fusion), channel_id=1, source_target_pairs={{0,24},{8,0},{16,8},{24,16},{1,25},{9,1},{17,9},{25,17},{2,26},{10... | collective-permute-start | bytes 5505032 | tf_op jit(solution)/shard_map/cond/branch_0_fun/ppermute | solution.py:18
  573.7 135.9 %collective-permute-start.30 = (bf16[896,1024]{1,0:T(8,128)(2,1)S(1)}, bf16[896,1024]{1,0:T(8,128)(2,1)S(1)}, u32[]{:S(2)}, u32[]{:S(2)}) collective-permute-start(bf16[896,1024]{1,0:T(8,128)(2,1)S(1)} %fusion), channel_id=1, source_target_pairs={{0,8},{8,16},{16,24},{24,0},{1,9},{9,17},{17,25},{25,1},{2,10},{10... | collective-permute-start | bytes 5505032 | tf_op jit(solution)/shard_map/cond/branch_0_fun/ppermute | solution.py:18
  574.0 134.9 %collective-permute-start.29 = (bf16[512,1024]{1,0:T(8,128)(2,1)S(1)}, bf16[512,1024]{1,0:T(8,128)(2,1)S(1)}, u32[]{:S(2)}, u32[]{:S(2)}) collective-permute-start(bf16[512,1024]{1,0:T(8,128)(2,1)S(1)} %fusion.8), channel_id=1, source_target_pairs={{0,24},{8,0},{16,8},{24,16},{1,25},{9,1},{17,9},{25,17},{2,26},{10... | collective-permute-start | bytes 3145736 | tf_op jit(solution)/shard_map/cond/branch_0_fun/ppermute | solution.py:18
  577.9 131.0 %collective-permute-start.28 = (bf16[512,1024]{1,0:T(8,128)(2,1)S(1)}, bf16[512,1024]{1,0:T(8,128)(2,1)S(1)}, u32[]{:S(2)}, u32[]{:S(2)}) collective-permute-start(bf16[512,1024]{1,0:T(8,128)(2,1)S(1)} %fusion.8), channel_id=1, source_target_pairs={{0,8},{8,16},{16,24},{24,0},{1,9},{9,17},{17,25},{25,1},{2,10},{10... | collective-permute-start | bytes 3145736 | tf_op jit(solution)/shard_map/cond/branch_0_fun/ppermute | solution.py:18
  578.6 130.0 %collective-permute-start.26 = (bf16[256,1024]{1,0:T(8,128)(2,1)S(1)}, bf16[256,1024]{1,0:T(8,128)(2,1)S(1)}, u32[]{:S(2)}, u32[]{:S(2)}) collective-permute-start(bf16[256,1024]{1,0:T(8,128)(2,1)S(1)} %fusion.39), channel_id=1, source_target_pairs={{0,8},{8,16},{16,24},{24,0},{1,9},{9,17},{17,25},{25,1},{2,10},{10... | collective-permute-start | bytes 1572872 | tf_op jit(solution)/shard_map/cond/branch_0_fun/ppermute | solution.py:18
  (39 other events, 1305.9 us)
Sparse Core Ops, SparseCore 0:
  13.8 33.1 all-gather.8
  48.9 33.9 all-gather.10
  84.8 32.8 all-gather.12
  119.4 38.3 all-gather.14

commit v3 on v2

--- a/solution.py
+++ b/solution.py
@@ -31,7 +31,8 @@
         take = left if (left - size < size or size % quantum) else size
         sizes.append(take)
         left -= take
-        size *= 2
+        if len(sizes) > 1:
+            size *= 4 if len(sizes) == 2 else 2
     return sizes
 
 

time: 742 us -> 747 us (level)
  waiting for transfers between devices: 527 us -> 495 us
  starting transfers between devices: 64.5 us -> 90.9 us
    ppermute x34, waiting for transfers between devices: 494 us -> 462 us  [shifted(): return lax.ppermute(value, axis, pairs)]
    ppermute x34, starting transfers between devices: 52 us -> 77.6 us  [shifted(): return lax.ppermute(value, axis, pairs)]
  transfers between devices with their start and end apart: 41 -> 41, of which waited for: 13 -> 13; matrix products, arithmetic and copies ran while one was open for 14% -> 15% of each run, Pallas kernels for 0% -> 0%
where the time goes in v3:
time: 747 us; the launch traced here: 739 us
  waiting for transfers between devices  495 us (66%)
  starting transfers between devices  90.9 us (12%)
  matrix products  60.4 us (8%)
  local copies, waits for them, and re-layouts  37.3 us (5%)
  other arithmetic  25.8 us (3%)
  between operations  17.9 us (2%)
  loops' own time  12.1 us (2%)
    ppermute x34, waiting for transfers between devices, shifted(): return lax.ppermute(value, axis, pairs)  462 us
    ppermute x34, starting transfers between devices, shifted(): return lax.ppermute(value, axis, pairs)  77.6 us
    dot_general x16, matrix products, pipeline(): lax.dot_general(cols, cot, rows_by_tokens, preferred_element_type=jnp.flo...  60.4 us
    dynamic_update_slice x15, other arithmetic, pipeline(): lax.dynamic_update_slice(mixed, total.astype(jnp.bfloat16), (start, b * c...  23.8 us
    all_gather x4, waiting for transfers between devices, pipeline(): lax.all_gather(cotangent[:, b * col_size:(b + 1) * col_size], 'node', axi...  23.1 us
  transfers between devices with their start and end apart: 41, of which 13 were waited for; matrix products, arithmetic and copies ran while one was open for 15% of the time, Pallas kernels for 0%

profile of v3, /device:TPU:0, one launch (start us, length us, event | category | flops | bytes accessed | tf_op | source)
XLA Modules:
  0.0 739.0 jit_solution(12793783118549027952)
XLA Ops:
  11.0 719.8 %conditional.1 = (bf16[1,1792,4096]{2,1,0:T(8,128)(2,1)}, f32[1]{0:T(128)}) conditional(s32[]{:T(128)} %clamp.3, (bf16[1,1792,4096]{2,1,0:T(8,128)(2,1)}, f32[]{:T(128)}, bf16[1,1792,4096]{2,1,0:T(8,128)(2,1)}, bf16[1,128,14336]{2,1,0:T(8,128)(2,1)}, bf16[128,4096]{1,0:T(8,128)(2,1)}, /*index=5*/pred[]{:T(512)}, f32[1]{0:T(128)}) %tuple.91, ...), branch_computations={%region_0.1_spmd, %region_1.2_spmd} | conditional | flops 15157166080 | bytes 535564608 | solution.py:112
  14.8 6.1 copy.19
  22.8 5.2 all-to-all-start
  30.2 7.5 %all-to-all-done = bf16[128,8,256]{0,2,1:T(8,128)(2,1)S(1)} async-done(((bf16[128,8,256]{0,2,1:T(8,128)(2,1)}), bf16[128,8,256]{0,2,1:T(8,128)(2,1)S(1)}, u32[]{:S(2)}, u32[]{:S(2)}) %all-to-all-start) | async-done | bytes 524320 | tf_op jit(solution)/shard_map/cond/branch_0_fun/all_to_all | solution.py:68
  38.7 6.2 all-gather.9.cloned.1.call-done
  65.7 16.9 %all-gather.11.cloned.1.call-done = bf16[1024,1024]{1,0:T(8,128)(2,1)} async-done(((bf16[128,1024]{1,0:T(8,128)(2,1)}), bf16[1024,1024]{1,0:T(8,128)(2,1)}) %all-gather.11.cloned.1.call-update) | async-done | bytes 2097168 | tf_op jit(solution)/shard_map/cond/branch_0_fun/all_gather | solution.py:50
  94.6 4.4 fusion.19
  105.3 7.3 pad_bitcast_fusion
  118.5 5.0 fusion.18
  123.4 29.9 %collective-permute-done.5 = bf16[512,1024]{1,0:T(8,128)(2,1)} collective-permute-done((bf16[512,1024]{1,0:T(8,128)(2,1)}, bf16[512,1024]{1,0:T(8,128)(2,1)}, u32[]{:S(2)}, u32[]{:S(2)}) %collective-permute-start.5) | collective-permute-done | bytes 1048608 | tf_op jit(solution)/shard_map/cond/branch_0_fun/ppermute | solution.py:18
  163.1 7.9 %fusion.2 = bf16[1024,1024]{1,0:T(8,128)(2,1)} fusion(bf16[1024,1024]{0,1:T(8,128)(2,1)} %bitcast.477, bf16[1024,1024]{1,0:T(8,128)(2,1)} %all-gather.11.cloned.1.call-done, bf16[1,1792,4096]{2,1,0:T(8,128)(2,1)} %get-tuple-element.30, bf16[1,1792,4096]{2,1,0:T(8,128)(2,1)} %get-tuple-element.28, f32[]{:T(128)} %get-tuple-element.29), kind=kOutput, calls=%fused_computation.6 | convolution fusion | flops 2155872256 | bytes 10485764 | tf_op jit(solution)/shard_map/cond/branch_0_fun/dot_general | solution.py:79
  175.1 6.8 fusion.3
  188.3 5.4 fusion.1
  196.2 101.5 %collective-permute-done.10 = bf16[128,1024]{1,0:T(8,128)(2,1)S(1)} collective-permute-done((bf16[128,1024]{1,0:T(8,128)(2,1)S(1)}, bf16[128,1024]{1,0:T(8,128)(2,1)S(1)}, u32[]{:S(2)}, u32[]{:S(2)}) %collective-permute-start.10) | collective-permute-done | bytes 262176 | tf_op jit(solution)/shard_map/cond/branch_0_fun/ppermute | solution.py:18
  303.0 49.4 %collective-permute-done.32 = f32[1]{0:T(128)} collective-permute-done((f32[1]{0:T(128)}, f32[1]{0:T(128)}, u32[]{:S(2)}, u32[]{:S(2)}) %collective-permute-start.32) | collective-permute-done | bytes 36 | tf_op jit(solution)/shard_map/cond/branch_0_fun/ppermute | solution.py:18
  371.5 5.4 fusion
  378.1 44.4 %collective-permute-done.18 = bf16[128,1024]{1,0:T(8,128)(2,1)S(1)} collective-permute-done((bf16[128,1024]{1,0:T(8,128)(2,1)S(1)}, bf16[128,1024]{1,0:T(8,128)(2,1)S(1)}, u32[]{:S(2)}, u32[]{:S(2)}) %collective-permute-start.18) | collective-permute-done | bytes 262176 | tf_op jit(solution)/shard_map/cond/branch_0_fun/ppermute | solution.py:18
  424.6 4.4 fusion.9
  429.1 71.1 %collective-permute-done.25 = bf16[128,1024]{1,0:T(8,128)(2,1)S(1)} collective-permute-done((bf16[128,1024]{1,0:T(8,128)(2,1)S(1)}, bf16[128,1024]{1,0:T(8,128)(2,1)S(1)}, u32[]{:S(2)}, u32[]{:S(2)}) %collective-permute-start.25) | collective-permute-done | bytes 262176 | tf_op jit(solution)/shard_map/cond/branch_0_fun/ppermute | solution.py:18
  514.8 66.7 %collective-permute-done.27 = bf16[128,1024]{1,0:T(8,128)(2,1)} collective-permute-done((bf16[128,1024]{1,0:T(8,128)(2,1)S(1)}, bf16[128,1024]{1,0:T(8,128)(2,1)}, u32[]{:S(2)}, u32[]{:S(2)}) %collective-permute-start.27) | collective-permute-done | bytes 262176 | tf_op jit(solution)/shard_map/cond/branch_0_fun/ppermute | solution.py:18
  581.5 4.5 collective-permute-start.31
  587.4 33.1 %collective-permute-start.29 = (bf16[512,1024]{1,0:T(8,128)(2,1)S(1)}, bf16[512,1024]{1,0:T(8,128)(2,1)S(1)}, u32[]{:S(2)}, u32[]{:S(2)}) collective-permute-start(bf16[512,1024]{1,0:T(8,128)(2,1)S(1)} %fusion.16), channel_id=1, source_target_pairs={{0,24},{8,0},{16,8},{24,16},{1,25},{9,1},{17,9},{25,17},{2,26},{10... | collective-permute-start | bytes 3145736 | tf_op jit(solution)/shard_map/cond/branch_0_fun/ppermute | solution.py:18
  623.1 89.2 %collective-permute-done.26 = bf16[128,1024]{1,0:T(8,128)(2,1)S(1)} collective-permute-done((bf16[128,1024]{1,0:T(8,128)(2,1)S(1)}, bf16[128,1024]{1,0:T(8,128)(2,1)S(1)}, u32[]{:S(2)}, u32[]{:S(2)}) %collective-permute-start.26) | collective-permute-done | bytes 262176 | tf_op jit(solution)/shard_map/cond/branch_0_fun/ppermute | solution.py:18
  715.8 5.5 copy-done
  (163 shorter events, 125.2 us)
Async XLA Ops:
  14.0 157.0 %all-gather.13.cloned.1.call-start = ((), (), s32[]{:S(2)}) async-start(), calls=%async_computation.8 | async-start | bytes 2359296 | tf_op jit(solution)/shard_map/cond/branch_0_fun/all_gather | solution.py:50
  53.8 140.0 %all-gather.15.cloned.1.call-start = ((), (), s32[]{:S(2)}) async-start(), calls=%async_computation.9 | async-start | bytes 2359296 | tf_op jit(solution)/shard_map/cond/branch_0_fun/all_gather | solution.py:50
  85.7 100.3 %collective-permute-start.9 = (bf16[128,1024]{1,0:T(8,128)(2,1)}, bf16[128,1024]{1,0:T(8,128)(2,1)}, u32[]{:S(2)}, u32[]{:S(2)}) collective-permute-start(bf16[128,1024]{1,0:T(8,128)(2,1)} %fusion.50), channel_id=1, source_target_pairs={{0,24},{8,0},{16,8},{24,16},{1,25},{9,1},{17,9},{25,17},{2,26},{10... | collective-permute-start | bytes 786440 | tf_op jit(solution)/shard_map/cond/branch_0_fun/ppermute | solution.py:18
  112.7 75.1 %collective-permute-start.8 = (bf16[128,1024]{1,0:T(8,128)(2,1)}, bf16[128,1024]{1,0:T(8,128)(2,1)}, u32[]{:S(2)}, u32[]{:S(2)}) collective-permute-start(bf16[128,1024]{1,0:T(8,128)(2,1)} %fusion.50), channel_id=1, source_target_pairs={{0,8},{8,16},{16,24},{24,0},{1,9},{9,17},{17,25},{25,1},{2,10},{10... | collective-permute-start | bytes 786440 | tf_op jit(solution)/shard_map/cond/branch_0_fun/ppermute | solution.py:18
  112.7 81.1 %collective-permute-start.11 = (bf16[128,1024]{1,0:T(8,128)(2,1)S(1)}, bf16[128,1024]{1,0:T(8,128)(2,1)}, u32[]{:S(2)}, u32[]{:S(2)}) collective-permute-start(bf16[128,1024]{1,0:T(8,128)(2,1)S(1)} %copy-done.27), channel_id=1, source_target_pairs={{0,24},{8,0},{16,8},{24,16},{1,25},{9,1},{17,9},{25,17},{2,26},{10... | collective-permute-start | bytes 786440 | tf_op jit(solution)/shard_map/cond/branch_0_fun/ppermute | solution.py:18
  153.4 147.5 %collective-permute-start.13 = (bf16[512,1024]{1,0:T(8,128)(2,1)}, bf16[512,1024]{1,0:T(8,128)(2,1)}, u32[]{:S(2)}, u32[]{:S(2)}) collective-permute-start(bf16[512,1024]{1,0:T(8,128)(2,1)} %fusion.18), channel_id=1, source_target_pairs={{0,24},{8,0},{16,8},{24,16},{1,25},{9,1},{17,9},{25,17},{2,26},{10... | collective-permute-start | bytes 3145736 | tf_op jit(solution)/shard_map/cond/branch_0_fun/ppermute | solution.py:18
  153.4 149.6 %collective-permute-start.12 = (bf16[512,1024]{1,0:T(8,128)(2,1)}, bf16[512,1024]{1,0:T(8,128)(2,1)}, u32[]{:S(2)}, u32[]{:S(2)}) collective-permute-start(bf16[512,1024]{1,0:T(8,128)(2,1)} %fusion.18), channel_id=1, source_target_pairs={{0,8},{8,16},{16,24},{24,0},{1,9},{9,17},{17,25},{25,1},{2,10},{10... | collective-permute-start | bytes 3145736 | tf_op jit(solution)/shard_map/cond/branch_0_fun/ppermute | solution.py:18
  185.9 236.6 %collective-permute-start.7 = (bf16[1024,1024]{1,0:T(8,128)(2,1)}, bf16[1024,1024]{1,0:T(8,128)(2,1)}, u32[]{:S(2)}, u32[]{:S(2)}) collective-permute-start(bf16[1024,1024]{1,0:T(8,128)(2,1)} %fusion.3), channel_id=1, source_target_pairs={{0,24},{8,0},{16,8},{24,16},{1,25},{9,1},{17,9},{25,17},{2,26},{10... | collective-permute-start | bytes 6291464 | tf_op jit(solution)/shard_map/cond/branch_0_fun/ppermute | solution.py:18
  187.7 235.5 %collective-permute-start.6 = (bf16[1024,1024]{1,0:T(8,128)(2,1)}, bf16[1024,1024]{1,0:T(8,128)(2,1)}, u32[]{:S(2)}, u32[]{:S(2)}) collective-permute-start(bf16[1024,1024]{1,0:T(8,128)(2,1)} %fusion.3), channel_id=1, source_target_pairs={{0,8},{8,16},{16,24},{24,0},{1,9},{9,17},{17,25},{25,1},{2,10},{10... | collective-permute-start | bytes 6291464 | tf_op jit(solution)/shard_map/cond/branch_0_fun/ppermute | solution.py:18
  193.7 103.9 %collective-permute-start.10 = (bf16[128,1024]{1,0:T(8,128)(2,1)S(1)}, bf16[128,1024]{1,0:T(8,128)(2,1)S(1)}, u32[]{:S(2)}, u32[]{:S(2)}) collective-permute-start(bf16[128,1024]{1,0:T(8,128)(2,1)S(1)} %copy-done.27), channel_id=1, source_target_pairs={{0,8},{8,16},{16,24},{24,0},{1,9},{9,17},{17,25},{25,1},{2,10},{10... | collective-permute-start | bytes 786440 | tf_op jit(solution)/shard_map/cond/branch_0_fun/ppermute | solution.py:18
  300.8 205.6 %collective-permute-start.15 = (bf16[1024,1024]{1,0:T(8,128)(2,1)S(1)}, bf16[1024,1024]{1,0:T(8,128)(2,1)S(1)}, u32[]{:S(2)}, u32[]{:S(2)}) collective-permute-start(bf16[1024,1024]{1,0:T(8,128)(2,1)S(1)} %copy-done.13), channel_id=1, source_target_pairs={{0,24},{8,0},{16,8},{24,16},{1,25},{9,1},{17,9},{25,17},{2,26},{10... | collective-permute-start | bytes 6291464 | tf_op jit(solution)/shard_map/cond/branch_0_fun/ppermute | solution.py:18
  367.2 142.1 %collective-permute-start.14 = (bf16[1024,1024]{1,0:T(8,128)(2,1)S(1)}, bf16[1024,1024]{1,0:T(8,128)(2,1)S(1)}, u32[]{:S(2)}, u32[]{:S(2)}) collective-permute-start(bf16[1024,1024]{1,0:T(8,128)(2,1)S(1)} %copy-done.13), channel_id=1, source_target_pairs={{0,8},{8,16},{16,24},{24,0},{1,9},{9,17},{17,25},{25,1},{2,10},{10... | collective-permute-start | bytes 6291464 | tf_op jit(solution)/shard_map/cond/branch_0_fun/ppermute | solution.py:18
  422.5 198.0 %collective-permute-start.23 = (bf16[1024,1024]{1,0:T(8,128)(2,1)S(1)}, bf16[1024,1024]{1,0:T(8,128)(2,1)S(1)}, u32[]{:S(2)}, u32[]{:S(2)}) collective-permute-start(bf16[1024,1024]{1,0:T(8,128)(2,1)S(1)} %fusion.1), channel_id=1, source_target_pairs={{0,24},{8,0},{16,8},{24,16},{1,25},{9,1},{17,9},{25,17},{2,26},{10... | collective-permute-start | bytes 6291464 | tf_op jit(solution)/shard_map/cond/branch_0_fun/ppermute | solution.py:18
  422.5 77.7 %collective-permute-start.25 = (bf16[128,1024]{1,0:T(8,128)(2,1)S(1)}, bf16[128,1024]{1,0:T(8,128)(2,1)S(1)}, u32[]{:S(2)}, u32[]{:S(2)}) collective-permute-start(bf16[128,1024]{1,0:T(8,128)(2,1)S(1)} %fusion.54), channel_id=1, source_target_pairs={{0,24},{8,0},{16,8},{24,16},{1,25},{9,1},{17,9},{25,17},{2,26},{10... | collective-permute-start | bytes 786440 | tf_op jit(solution)/shard_map/cond/branch_0_fun/ppermute | solution.py:18
  423.2 78.3 %collective-permute-start.24 = (bf16[128,1024]{1,0:T(8,128)(2,1)S(1)}, bf16[128,1024]{1,0:T(8,128)(2,1)S(1)}, u32[]{:S(2)}, u32[]{:S(2)}) collective-permute-start(bf16[128,1024]{1,0:T(8,128)(2,1)S(1)} %fusion.54), channel_id=1, source_target_pairs={{0,8},{8,16},{16,24},{24,0},{1,9},{9,17},{17,25},{25,1},{2,10},{10... | collective-permute-start | bytes 786440 | tf_op jit(solution)/shard_map/cond/branch_0_fun/ppermute | solution.py:18
  500.2 121.0 %collective-permute-start.22 = (bf16[1024,1024]{1,0:T(8,128)(2,1)S(1)}, bf16[1024,1024]{1,0:T(8,128)(2,1)S(1)}, u32[]{:S(2)}, u32[]{:S(2)}) collective-permute-start(bf16[1024,1024]{1,0:T(8,128)(2,1)S(1)} %fusion.1), channel_id=1, source_target_pairs={{0,8},{8,16},{16,24},{24,0},{1,9},{9,17},{17,25},{25,1},{2,10},{10... | collective-permute-start | bytes 6291464 | tf_op jit(solution)/shard_map/cond/branch_0_fun/ppermute | solution.py:18
  501.6 84.4 %collective-permute-start.21 = (bf16[512,1024]{1,0:T(8,128)(2,1)S(1)}, bf16[512,1024]{1,0:T(8,128)(2,1)S(1)}, u32[]{:S(2)}, u32[]{:S(2)}) collective-permute-start(bf16[512,1024]{1,0:T(8,128)(2,1)S(1)} %copy-done.22), channel_id=1, source_target_pairs={{0,24},{8,0},{16,8},{24,16},{1,25},{9,1},{17,9},{25,17},{2,26},{10... | collective-permute-start | bytes 3145736 | tf_op jit(solution)/shard_map/cond/branch_0_fun/ppermute | solution.py:18
  506.5 80.9 %collective-permute-start.20 = (bf16[512,1024]{1,0:T(8,128)(2,1)S(1)}, bf16[512,1024]{1,0:T(8,128)(2,1)S(1)}, u32[]{:S(2)}, u32[]{:S(2)}) collective-permute-start(bf16[512,1024]{1,0:T(8,128)(2,1)S(1)} %copy-done.22), channel_id=1, source_target_pairs={{0,8},{8,16},{16,24},{24,0},{1,9},{9,17},{17,25},{25,1},{2,10},{10... | collective-permute-start | bytes 3145736 | tf_op jit(solution)/shard_map/cond/branch_0_fun/ppermute | solution.py:18
  509.3 72.1 %collective-permute-start.27 = (bf16[128,1024]{1,0:T(8,128)(2,1)S(1)}, bf16[128,1024]{1,0:T(8,128)(2,1)}, u32[]{:S(2)}, u32[]{:S(2)}) collective-permute-start(bf16[128,1024]{1,0:T(8,128)(2,1)S(1)} %fusion.55), channel_id=1, source_target_pairs={{0,24},{8,0},{16,8},{24,16},{1,25},{9,1},{17,9},{25,17},{2,26},{10... | collective-permute-start | bytes 786440 | tf_op jit(solution)/shard_map/cond/branch_0_fun/ppermute | solution.py:18
  581.5 132.6 %collective-permute-start.31 = (bf16[1024,1024]{1,0:T(8,128)(2,1)S(1)}, bf16[1024,1024]{1,0:T(8,128)(2,1)S(1)}, u32[]{:S(2)}, u32[]{:S(2)}) collective-permute-start(bf16[1024,1024]{1,0:T(8,128)(2,1)S(1)} %fusion), channel_id=1, source_target_pairs={{0,24},{8,0},{16,8},{24,16},{1,25},{9,1},{17,9},{25,17},{2,26},{10... | collective-permute-start | bytes 6291464 | tf_op jit(solution)/shard_map/cond/branch_0_fun/ppermute | solution.py:18
  586.0 128.2 %collective-permute-start.30 = (bf16[1024,1024]{1,0:T(8,128)(2,1)S(1)}, bf16[1024,1024]{1,0:T(8,128)(2,1)S(1)}, u32[]{:S(2)}, u32[]{:S(2)}) collective-permute-start(bf16[1024,1024]{1,0:T(8,128)(2,1)S(1)} %fusion), channel_id=1, source_target_pairs={{0,8},{8,16},{16,24},{24,0},{1,9},{9,17},{17,25},{25,1},{2,10},{10... | collective-permute-start | bytes 6291464 | tf_op jit(solution)/shard_map/cond/branch_0_fun/ppermute | solution.py:18
  587.4 126.0 %collective-permute-start.29 = (bf16[512,1024]{1,0:T(8,128)(2,1)S(1)}, bf16[512,1024]{1,0:T(8,128)(2,1)S(1)}, u32[]{:S(2)}, u32[]{:S(2)}) collective-permute-start(bf16[512,1024]{1,0:T(8,128)(2,1)S(1)} %fusion.16), channel_id=1, source_target_pairs={{0,24},{8,0},{16,8},{24,16},{1,25},{9,1},{17,9},{25,17},{2,26},{10... | collective-permute-start | bytes 3145736 | tf_op jit(solution)/shard_map/cond/branch_0_fun/ppermute | solution.py:18
  620.5 92.9 %collective-permute-start.28 = (bf16[512,1024]{1,0:T(8,128)(2,1)S(1)}, bf16[512,1024]{1,0:T(8,128)(2,1)S(1)}, u32[]{:S(2)}, u32[]{:S(2)}) collective-permute-start(bf16[512,1024]{1,0:T(8,128)(2,1)S(1)} %fusion.16), channel_id=1, source_target_pairs={{0,8},{8,16},{16,24},{24,0},{1,9},{9,17},{17,25},{25,1},{2,10},{10... | collective-permute-start | bytes 3145736 | tf_op jit(solution)/shard_map/cond/branch_0_fun/ppermute | solution.py:18
  621.2 91.0 %collective-permute-start.26 = (bf16[128,1024]{1,0:T(8,128)(2,1)S(1)}, bf16[128,1024]{1,0:T(8,128)(2,1)S(1)}, u32[]{:S(2)}, u32[]{:S(2)}) collective-permute-start(bf16[128,1024]{1,0:T(8,128)(2,1)S(1)} %fusion.55), channel_id=1, source_target_pairs={{0,8},{8,16},{16,24},{24,0},{1,9},{9,17},{17,25},{25,1},{2,10},{10... | collective-permute-start | bytes 786440 | tf_op jit(solution)/shard_map/cond/branch_0_fun/ppermute | solution.py:18
  (45 other events, 1730.8 us)
Sparse Core Ops, SparseCore 0:
  13.8 31.1 all-gather.8
  46.8 35.7 all-gather.10
  84.5 30.2 all-gather.12
  116.6 35.7 all-gather.14

commit v4 on v2

--- a/solution.py
+++ b/solution.py
@@ -35,16 +35,61 @@
     return sizes
 
 
-def pipeline(amount, groups, params, momentum, hidden, cotangent, push_weight, rate, direct):
+def switched_sends(amount, groups, direct):
+    paired = (2 * amount) % groups == 0
+    w_minus = jnp.where(direct, back_share, front_share).astype(jnp.float32)
+    w_plus = jnp.where(direct, front_share, back_share).astype(jnp.float32)
+
+    def send_tile(half):
+        minus = shifted(half, "grp", amount)
+        if paired:
+            return (back_share * minus.astype(jnp.float32)) + front_share * minus.astype(jnp.float32)
+        plus = shifted(half, "grp", groups - amount)
+        return w_minus * minus.astype(jnp.float32) + w_plus * plus.astype(jnp.float32)
+
+    def send_weight(weight):
+        return w_minus * shifted(weight, "grp", amount) + w_plus * shifted(weight, "grp", groups - amount)
+
+    return send_tile, send_weight
+
+
+def relayed_sends(groups, offset):
+    far = offset * 2 == groups
+    direct = offset == 1
+    w_minus = jnp.where(direct, back_share, front_share).astype(jnp.float32)
+    w_plus = jnp.where(direct, front_share, back_share).astype(jnp.float32)
+
+    def send_tile(half):
+        cut = half.shape[0] // 2
+        top, bottom = half[:cut], half[cut:]
+        up_1 = shifted(top, "grp", 1)
+        down_1 = shifted(jnp.where(far, bottom, top), "grp", groups - 1)
+        up_2 = shifted(jnp.where(far, up_1, bottom), "grp", 1)
+        down_2 = shifted(jnp.where(far, down_1, bottom), "grp", groups - 1)
+        minus = jnp.concatenate([up_1, up_2], axis=0).astype(jnp.float32)
+        plus = jnp.concatenate([down_1, down_2], axis=0).astype(jnp.float32)
+        other = jnp.concatenate([up_2, down_2], axis=0).astype(jnp.float32)
+        near = w_minus * minus + w_plus * plus
+        return jnp.where(far, back_share * other + front_share * other, near)
+
+    def send_weight(weight):
+        up_1 = shifted(weight, "grp", 1)
+        down_1 = shifted(weight, "grp", groups - 1)
+        up_2 = shifted(up_1, "grp", 1)
+        near = w_minus * up_1 + w_plus * down_1
+        return jnp.where(far, back_share * up_2 + front_share * up_2, near)
+
+    return send_tile, send_weight
+
+
+def pipeline(sends, params, momentum, hidden, cotangent, push_weight, rate):
+    send_tile, send_weight = sends
     nodes = lax.axis_size("node")
     rows_total = params.shape[1]
     acts = hidden.reshape(hidden.shape[0], nodes, rows_total)
     width = cotangent.shape[1]
     n_cols = block_count(width, col_blocks, 128)
     col_size = width // n_cols
-    paired = (2 * amount) % groups == 0
-    w_minus = jnp.where(direct, back_share, front_share).astype(jnp.float32)
-    w_plus = jnp.where(direct, front_share, back_share).astype(jnp.float32)
     cots = [
         lax.all_gather(cotangent[:, b * col_size:(b + 1) * col_size], "node", axis=0, tiled=True)
         for b in range(n_cols)
@@ -82,17 +127,11 @@
             last = half
             if weight_sent is None and b == 0 and a == len(sizes) - 1:
                 weight, last = lax.optimization_barrier((push_weight, last))
-                weight_sent = (shifted(weight, "grp", amount), shifted(weight, "grp", groups - amount))
-            minus = shifted(half, "grp", amount)
-            if paired:
-                peers = (back_share * minus.astype(jnp.float32)) + front_share * minus.astype(jnp.float32)
-            else:
-                plus = shifted(half, "grp", groups - amount)
-                peers = w_minus * minus.astype(jnp.float32) + w_plus * plus.astype(jnp.float32)
+                weight_sent = send_weight(weight)
+            peers = send_tile(half)
             total = keep_share * half.astype(jnp.float32) + peers
             mixed = lax.dynamic_update_slice(mixed, total.astype(jnp.bfloat16), (start, b * col_size))
-    weight_minus, weight_plus = weight_sent
-    new_weight = keep_share * push_weight + w_minus * weight_minus + w_plus * weight_plus
+    new_weight = keep_share * push_weight + weight_sent
     return mixed[None], new_weight
 
 
@@ -101,16 +140,17 @@
     position = step[0]
     offset = offsets[position]
     rate = base_rate * (1.0 - 0.5 * position.astype(jnp.float32) / offsets.shape[0])
+    args = (params, momentum, hidden[0], cotangent[0], push_weight, rate)
+    if groups == 4:
+        return pipeline(relayed_sends(groups, offset), *args)
     amounts = list(range(1, groups // 2 + 1))
     direct = offset <= groups // 2
     index = jnp.where(direct, offset, groups - offset) - 1
     branches = [
-        (lambda *a, amount=amount: pipeline(amount, groups, *a))
+        (lambda *a, amount=amount: pipeline(switched_sends(amount, groups, direct), *a))
         for amount in amounts
     ]
-    return lax.switch(
-        index, branches, params, momentum, hidden[0], cotangent[0], push_weight, rate, direct
-    )
+    return lax.switch(index, branches, *args)
 
 
 def solution(mesh):

time: 742 us -> 757 us (1.020)
  waiting for transfers between devices: 527 us -> 421 us
  starting transfers between devices: 64.5 us -> 155 us
  other arithmetic: 18.7 us -> 56.7 us
  loops' own time: 12.3 us -> 0 us
  local copies, waits for them, and re-layouts: 34.3 us -> 42.6 us
  matrix products: 59.3 us -> 51.5 us
    ppermute x34 -> x67, waiting for transfers between devices: 494 us -> 387 us  [shifted(): return lax.ppermute(value, axis, pairs)]
    ppermute x34 -> x67, starting transfers between devices: 52 us -> 142 us  [shifted(): return lax.ppermute(value, axis, pairs)]
    select_n x0 -> x47, other arithmetic: none -> 32.9 us  [the longest x16 14.4 us: send_tile(): down_2 = shifted(jnp.where(far, down_1, bottom), 'grp', groups - 1)]
    unnamed x0 -> x147, local copies, waits for them, and re-layouts: none -> 18.1 us
    another operation x1 -> x0, loops' own time: 12.3 us -> none  [per_device(): lax.switch(index, branches, params, momentum, hidden[0], cotangent[0], pu...]
    dot_general x16, matrix products: 59.3 us -> 51.5 us  [pipeline(): lax.dot_general(cols, cot, rows_by_tokens, preferred_element_type=jnp.flo...]
  transfers between devices with their start and end apart: 41 -> 74, of which waited for: 13 -> 36; matrix products, arithmetic and copies ran while one was open for 14% -> 18% of each run, Pallas kernels for 0% -> 0%
where the time goes in v4:
time: 757 us; the launch traced here: 748 us
  waiting for transfers between devices  421 us (56%)
  starting transfers between devices  155 us (20%)
  other arithmetic  56.7 us (7%)
  matrix products  51.5 us (7%)
  local copies, waits for them, and re-layouts  42.6 us (6%)
  between operations  20.8 us (3%)
    ppermute x67, waiting for transfers between devices, shifted(): return lax.ppermute(value, axis, pairs)  387 us
    ppermute x67, starting transfers between devices, shifted(): return lax.ppermute(value, axis, pairs)  142 us
    dot_general x16, matrix products, pipeline(): lax.dot_general(cols, cot, rows_by_tokens, preferred_element_type=jnp.flo...  51.5 us
    all_gather x4, waiting for transfers between devices, pipeline(): lax.all_gather(cotangent[:, b * col_size:(b + 1) * col_size], 'node', axi...  25.4 us
    dynamic_update_slice x15, other arithmetic, pipeline(): lax.dynamic_update_slice(mixed, total.astype(jnp.bfloat16), (start, b * c...  22.9 us
    unnamed x147, local copies, waits for them, and re-layouts  18.1 us
  transfers between devices with their start and end apart: 74, of which 36 were waited for; matrix products, arithmetic and copies ran while one was open for 18% of the time, Pallas kernels for 0%

profile of v4, /device:TPU:0, one launch (start us, length us, event | category | flops | bytes accessed | tf_op | source)
XLA Modules:
  0.0 747.7 jit_solution(13639119414269544540)
XLA Ops:
  56.3 22.6 %all-gather.7.cloned.1.call-done = bf16[1024,1024]{1,0:T(8,128)(2,1)} async-done(((bf16[128,1024]{1,0:T(8,128)(2,1)}), bf16[1024,1024]{1,0:T(8,128)(2,1)}) %all-gather.7.cloned.1.call-update) | async-done | bytes 2097168 | tf_op jit(solution)/shard_map/all_gather | solution.py:94
  90.4 12.1 %collective-permute-done.2 = bf16[64,1024]{1,0:T(8,128)(2,1)S(1)} collective-permute-done((bf16[64,1024]{1,0:T(8,128)(2,1)S(1)}, bf16[64,1024]{1,0:T(8,128)(2,1)S(1)}, u32[]{:S(2)}, u32[]{:S(2)}) %collective-permute-start.2) | collective-permute-done | bytes 131104 | tf_op jit(solution)/shard_map/ppermute | solution.py:18
  125.4 11.4 %collective-permute-done.10 = bf16[256,1024]{1,0:T(8,128)(2,1)S(1)} collective-permute-done((bf16[256,1024]{1,0:T(8,128)(2,1)S(1)}, bf16[256,1024]{1,0:T(8,128)(2,1)S(1)}, u32[]{:S(2)}, u32[]{:S(2)}) %collective-permute-start.10) | collective-permute-done | bytes 524320 | tf_op jit(solution)/shard_map/ppermute | solution.py:18
  138.7 8.3 %pad_bitcast_fusion = bf16[1,1792,4096]{2,1,0:T(8,128)(2,1)} fusion(bf16[128,1024]{1,0:T(8,128)(2,1)} %fusion.79), kind=kLoop, calls=%fused_computation | loop fusion | bytes 14942208 | tf_op jit(solution)/shard_map/broadcast_in_dim | solution.py:135
  170.9 14.4 %collective-permute-done.24 = bf16[256,1024]{1,0:T(8,128)(2,1)S(1)} collective-permute-done((bf16[256,1024]{1,0:T(8,128)(2,1)S(1)}, bf16[256,1024]{1,0:T(8,128)(2,1)S(1)}, u32[]{:S(2)}, u32[]{:S(2)}) %collective-permute-start.24) | collective-permute-done | bytes 524320 | tf_op jit(solution)/shard_map/ppermute | solution.py:18
  187.0 7.8 %collective-permute-done.11 = bf16[256,1024]{1,0:T(8,128)(2,1)S(1)} collective-permute-done((bf16[256,1024]{1,0:T(8,128)(2,1)}, bf16[256,1024]{1,0:T(8,128)(2,1)S(1)}, u32[]{:S(2)}, u32[]{:S(2)}) %collective-permute-start.11) | collective-permute-done | bytes 524320 | tf_op jit(solution)/shard_map/ppermute | solution.py:18
  265.3 11.1 %collective-permute-done.50 = bf16[64,1024]{1,0:T(8,128)(2,1)S(1)} collective-permute-done((bf16[64,1024]{1,0:T(8,128)(2,1)S(1)}, bf16[64,1024]{1,0:T(8,128)(2,1)S(1)}, u32[]{:S(2)}, u32[]{:S(2)}) %collective-permute-start.50) | collective-permute-done | bytes 131104 | tf_op jit(solution)/shard_map/ppermute | solution.py:18
  284.8 7.5 %collective-permute-done.48 = bf16[64,1024]{1,0:T(8,128)(2,1)S(1)} collective-permute-done((bf16[64,1024]{1,0:T(8,128)(2,1)S(1)}, bf16[64,1024]{1,0:T(8,128)(2,1)S(1)}, u32[]{:S(2)}, u32[]{:S(2)}) %collective-permute-start.48) | collective-permute-done | bytes 131104 | tf_op jit(solution)/shard_map/ppermute | solution.py:18
  301.9 14.1 %collective-permute-done.36 = bf16[128,1024]{1,0:T(8,128)(2,1)S(1)} collective-permute-done((bf16[128,1024]{1,0:T(8,128)(2,1)S(1)}, bf16[128,1024]{1,0:T(8,128)(2,1)S(1)}, u32[]{:S(2)}, u32[]{:S(2)}) %collective-permute-start.36) | collective-permute-done | bytes 262176 | tf_op jit(solution)/shard_map/ppermute | solution.py:18
  332.4 8.9 %collective-permute-done.46 = bf16[448,1024]{1,0:T(8,128)(2,1)S(1)} collective-permute-done((bf16[448,1024]{1,0:T(8,128)(2,1)S(1)}, bf16[448,1024]{1,0:T(8,128)(2,1)S(1)}, u32[]{:S(2)}, u32[]{:S(2)}) %collective-permute-start.46) | collective-permute-done | bytes 917536 | tf_op jit(solution)/shard_map/ppermute | solution.py:18
  345.9 55.3 %collective-permute-done.62 = bf16[448,1024]{1,0:T(8,128)(2,1)S(1)} collective-permute-done((bf16[448,1024]{1,0:T(8,128)(2,1)S(1)}, bf16[448,1024]{1,0:T(8,128)(2,1)S(1)}, u32[]{:S(2)}, u32[]{:S(2)}) %collective-permute-start.62) | collective-permute-done | bytes 917536 | tf_op jit(solution)/shard_map/ppermute | solution.py:18
  408.3 34.6 %collective-permute-done.28 = bf16[448,1024]{1,0:T(8,128)(2,1)S(1)} collective-permute-done((bf16[448,1024]{1,0:T(8,128)(2,1)S(1)}, bf16[448,1024]{1,0:T(8,128)(2,1)S(1)}, u32[]{:S(2)}, u32[]{:S(2)}) %collective-permute-start.28) | collective-permute-done | bytes 917536 | tf_op jit(solution)/shard_map/ppermute | solution.py:18
  443.1 19.5 %collective-permute-done.44 = bf16[448,1024]{1,0:T(8,128)(2,1)S(1)} collective-permute-done((bf16[448,1024]{1,0:T(8,128)(2,1)S(1)}, bf16[448,1024]{1,0:T(8,128)(2,1)S(1)}, u32[]{:S(2)}, u32[]{:S(2)}) %collective-permute-start.44) | collective-permute-done | bytes 917536 | tf_op jit(solution)/shard_map/ppermute | solution.py:18
  464.7 17.5 %collective-permute-done.60 = bf16[448,1024]{1,0:T(8,128)(2,1)S(1)} collective-permute-done((bf16[448,1024]{1,0:T(8,128)(2,1)S(1)}, bf16[448,1024]{1,0:T(8,128)(2,1)S(1)}, u32[]{:S(2)}, u32[]{:S(2)}) %collective-permute-start.60) | collective-permute-done | bytes 917536 | tf_op jit(solution)/shard_map/ppermute | solution.py:18
  482.4 21.6 %collective-permute-done.19 = bf16[64,1024]{1,0:T(8,128)(2,1)S(1)} collective-permute-done((bf16[64,1024]{1,0:T(8,128)(2,1)S(1)}, bf16[64,1024]{1,0:T(8,128)(2,1)S(1)}, u32[]{:S(2)}, u32[]{:S(2)}) %collective-permute-start.19) | collective-permute-done | bytes 131104 | tf_op jit(solution)/shard_map/ppermute | solution.py:18
  519.9 8.7 %collective-permute-start.35 = (bf16[64,1024]{1,0:T(8,128)(2,1)}, bf16[64,1024]{1,0:T(8,128)(2,1)S(1)}, u32[]{:S(2)}, u32[]{:S(2)}) collective-permute-start(bf16[64,1024]{1,0:T(8,128)(2,1)} %get-tuple-element.98), channel_id=1, source_target_pairs={{0,24},{8,0},{16,8},{24,16},{1,25},{9,1},{17,9},{25,17},{2,26},{10... | collective-permute-start | bytes 393224 | tf_op jit(solution)/shard_map/ppermute | solution.py:18
  539.1 20.2 %collective-permute-start.39 = (bf16[128,1024]{1,0:T(8,128)(2,1)S(1)}, bf16[128,1024]{1,0:T(8,128)(2,1)S(1)}, u32[]{:S(2)}, u32[]{:S(2)}) collective-permute-start(bf16[128,1024]{1,0:T(8,128)(2,1)S(1)} %copy-done.55), channel_id=1, source_target_pairs={{0,24},{8,0},{16,8},{24,16},{1,25},{9,1},{17,9},{25,17},{2,26},{10... | collective-permute-start | bytes 786440 | tf_op jit(solution)/shard_map/ppermute | solution.py:18
  561.2 19.4 %collective-permute-done.35 = bf16[64,1024]{1,0:T(8,128)(2,1)S(1)} collective-permute-done((bf16[64,1024]{1,0:T(8,128)(2,1)}, bf16[64,1024]{1,0:T(8,128)(2,1)S(1)}, u32[]{:S(2)}, u32[]{:S(2)}) %collective-permute-start.35) | collective-permute-done | bytes 131104 | tf_op jit(solution)/shard_map/ppermute | solution.py:18
  599.5 26.6 %collective-permute-start.51 = (bf16[64,1024]{1,0:T(8,128)(2,1)}, bf16[64,1024]{1,0:T(8,128)(2,1)S(1)}, u32[]{:S(2)}, u32[]{:S(2)}) collective-permute-start(bf16[64,1024]{1,0:T(8,128)(2,1)} %get-tuple-element.96), channel_id=1, source_target_pairs={{0,24},{8,0},{16,8},{24,16},{1,25},{9,1},{17,9},{25,17},{2,26},{10... | collective-permute-start | bytes 393224 | tf_op jit(solution)/shard_map/ppermute | solution.py:18
  626.6 10.1 %collective-permute-done.41 = bf16[256,1024]{1,0:T(8,128)(2,1)S(1)} collective-permute-done((bf16[256,1024]{1,0:T(8,128)(2,1)S(1)}, bf16[256,1024]{1,0:T(8,128)(2,1)S(1)}, u32[]{:S(2)}, u32[]{:S(2)}) %collective-permute-start.41) | collective-permute-done | bytes 524320 | tf_op jit(solution)/shard_map/ppermute | solution.py:18
  640.0 19.2 %collective-permute-done.51 = bf16[64,1024]{1,0:T(8,128)(2,1)S(1)} collective-permute-done((bf16[64,1024]{1,0:T(8,128)(2,1)}, bf16[64,1024]{1,0:T(8,128)(2,1)S(1)}, u32[]{:S(2)}, u32[]{:S(2)}) %collective-permute-start.51) | collective-permute-done | bytes 131104 | tf_op jit(solution)/shard_map/ppermute | solution.py:18
  676.1 8.4 %collective-permute-done.59 = bf16[256,1024]{1,0:T(8,128)(2,1)S(1)} collective-permute-done((bf16[256,1024]{1,0:T(8,128)(2,1)S(1)}, bf16[256,1024]{1,0:T(8,128)(2,1)S(1)}, u32[]{:S(2)}, u32[]{:S(2)}) %collective-permute-start.59) | collective-permute-done | bytes 524320 | tf_op jit(solution)/shard_map/ppermute | solution.py:18
  684.5 30.9 %collective-permute-done.57 = bf16[256,1024]{1,0:T(8,128)(2,1)S(1)} collective-permute-done((bf16[256,1024]{1,0:T(8,128)(2,1)S(1)}, bf16[256,1024]{1,0:T(8,128)(2,1)S(1)}, u32[]{:S(2)}, u32[]{:S(2)}) %collective-permute-start.57) | collective-permute-done | bytes 524320 | tf_op jit(solution)/shard_map/ppermute | solution.py:18
  716.2 16.0 %collective-permute-done.63 = bf16[448,1024]{1,0:T(8,128)(2,1)S(1)} collective-permute-done((bf16[448,1024]{1,0:T(8,128)(2,1)S(1)}, bf16[448,1024]{1,0:T(8,128)(2,1)S(1)}, u32[]{:S(2)}, u32[]{:S(2)}) %collective-permute-start.63) | collective-permute-done | bytes 917536 | tf_op jit(solution)/shard_map/ppermute | solution.py:18
  (367 shorter events, 300.5 us)
Async XLA Ops:
  9.4 69.4 %all-gather.7.cloned.1.call-start = ((), (), s32[]{:S(2)}) async-start(), calls=%async_computation.4 | async-start | bytes 2359296 | tf_op jit(solution)/shard_map/all_gather | solution.py:94
  10.2 210.9 %all-gather.9.cloned.1.call-start = ((), (), s32[]{:S(2)}) async-start(), calls=%async_computation.5 | async-start | bytes 2359296 | tf_op jit(solution)/shard_map/all_gather | solution.py:94
  24.3 213.8 %all-gather.11.cloned.1.call-start = ((), (), s32[]{:S(2)}) async-start(), calls=%async_computation.6 | async-start | bytes 2359296 | tf_op jit(solution)/shard_map/all_gather | solution.py:94
  52.8 63.1 %all-to-all-start.1 = ((bf16[128,8,512]{0,2,1:T(8,128)(2,1)}), bf16[128,8,512]{0,2,1:T(8,128)(2,1)S(1)}, u32[]{:S(2)}, u32[]{:S(2)}) async-start(bf16[128,8,512]{0,2,1:T(8,128)(2,1)} %slice.300), calls=%async_computation.1 | async-start | bytes 2097152 | tf_op jit(solution)/shard_map/all_to_all | solution.py:112
  105.5 63.0 %collective-permute-start.7 = (bf16[128,1024]{1,0:T(8,128)(2,1)}, bf16[128,1024]{1,0:T(8,128)(2,1)}, u32[]{:S(2)}, u32[]{:S(2)}) collective-permute-start(bf16[128,1024]{1,0:T(8,128)(2,1)} %get-tuple-element.94), channel_id=1, source_target_pairs={{0,24},{8,0},{16,8},{24,16},{1,25},{9,1},{17,9},{25,17},{2,26},{10... | collective-permute-start | bytes 786440 | tf_op jit(solution)/shard_map/ppermute | solution.py:18
  212.4 115.2 %collective-permute-start.14 = (bf16[448,1024]{1,0:T(8,128)(2,1)}, bf16[448,1024]{1,0:T(8,128)(2,1)}, u32[]{:S(2)}, u32[]{:S(2)}) collective-permute-start(bf16[448,1024]{1,0:T(8,128)(2,1)} %broadcast_select_fusion.10), channel_id=1, source_target_pairs={{0,24},{8,0},{16,8},{24,16},{1,25},{9,1},{17,9},{25,17},{2,26},{10... | collective-permute-start | bytes 2752520 | tf_op jit(solution)/shard_map/ppermute | solution.py:18
  220.6 108.8 %collective-permute-start.30 = (bf16[448,1024]{1,0:T(8,128)(2,1)}, bf16[448,1024]{1,0:T(8,128)(2,1)}, u32[]{:S(2)}, u32[]{:S(2)}) collective-permute-start(bf16[448,1024]{1,0:T(8,128)(2,1)} %broadcast_select_fusion.7), channel_id=1, source_target_pairs={{0,24},{8,0},{16,8},{24,16},{1,25},{9,1},{17,9},{25,17},{2,26},{10... | collective-permute-start | bytes 2752520 | tf_op jit(solution)/shard_map/ppermute | solution.py:18
  321.6 79.6 %collective-permute-start.62 = (bf16[448,1024]{1,0:T(8,128)(2,1)S(1)}, bf16[448,1024]{1,0:T(8,128)(2,1)S(1)}, u32[]{:S(2)}, u32[]{:S(2)}) collective-permute-start(bf16[448,1024]{1,0:T(8,128)(2,1)S(1)} %broadcast_select_fusion.1), channel_id=1, source_target_pairs={{0,24},{8,0},{16,8},{24,16},{1,25},{9,1},{17,9},{25,17},{2,26},{10... | collective-permute-start | bytes 2752520 | tf_op jit(solution)/shard_map/ppermute | solution.py:18
  326.8 76.7 %collective-permute-start.40 = (bf16[256,1024]{1,0:T(8,128)(2,1)S(1)}, bf16[256,1024]{1,0:T(8,128)(2,1)S(1)}, u32[]{:S(2)}, u32[]{:S(2)}) collective-permute-start(bf16[256,1024]{1,0:T(8,128)(2,1)S(1)} %get-tuple-element.83), channel_id=1, source_target_pairs={{0,8},{8,16},{16,24},{24,0},{1,9},{9,17},{17,25},{25,1},{2,10},{10... | collective-permute-start | bytes 1572872 | tf_op jit(solution)/shard_map/ppermute | solution.py:18
  327.7 78.0 %collective-permute-start.56 = (bf16[256,1024]{1,0:T(8,128)(2,1)S(1)}, bf16[256,1024]{1,0:T(8,128)(2,1)S(1)}, u32[]{:S(2)}, u32[]{:S(2)}) collective-permute-start(bf16[256,1024]{1,0:T(8,128)(2,1)S(1)} %get-tuple-element.77), channel_id=1, source_target_pairs={{0,8},{8,16},{16,24},{24,0},{1,9},{9,17},{17,25},{25,1},{2,10},{10... | collective-permute-start | bytes 1572872 | tf_op jit(solution)/shard_map/ppermute | solution.py:18
  329.4 75.0 %collective-permute-start.12 = (bf16[448,1024]{1,0:T(8,128)(2,1)S(1)}, bf16[448,1024]{1,0:T(8,128)(2,1)S(1)}, u32[]{:S(2)}, u32[]{:S(2)}) collective-permute-start(bf16[448,1024]{1,0:T(8,128)(2,1)S(1)} %get-tuple-element.75), channel_id=1, source_target_pairs={{0,8},{8,16},{16,24},{24,0},{1,9},{9,17},{17,25},{25,1},{2,10},{10... | collective-permute-start | bytes 2752520 | tf_op jit(solution)/shard_map/ppermute | solution.py:18
  341.3 169.4 %collective-permute-start.15 = (bf16[448,1024]{1,0:T(8,128)(2,1)S(1)}, bf16[448,1024]{1,0:T(8,128)(2,1)}, u32[]{:S(2)}, u32[]{:S(2)}) collective-permute-start(bf16[448,1024]{1,0:T(8,128)(2,1)S(1)} %get-tuple-element.74), channel_id=1, source_target_pairs={{0,24},{8,0},{16,8},{24,16},{1,25},{9,1},{17,9},{25,17},{2,26},{10... | collective-permute-start | bytes 2752520 | tf_op jit(solution)/shard_map/ppermute | solution.py:18
  403.4 59.2 %collective-permute-start.44 = (bf16[448,1024]{1,0:T(8,128)(2,1)S(1)}, bf16[448,1024]{1,0:T(8,128)(2,1)S(1)}, u32[]{:S(2)}, u32[]{:S(2)}) collective-permute-start(bf16[448,1024]{1,0:T(8,128)(2,1)S(1)} %get-tuple-element.71), channel_id=1, source_target_pairs={{0,8},{8,16},{16,24},{24,0},{1,9},{9,17},{17,25},{25,1},{2,10},{10... | collective-permute-start | bytes 2752520 | tf_op jit(solution)/shard_map/ppermute | solution.py:18
  404.4 77.9 %collective-permute-start.60 = (bf16[448,1024]{1,0:T(8,128)(2,1)S(1)}, bf16[448,1024]{1,0:T(8,128)(2,1)S(1)}, u32[]{:S(2)}, u32[]{:S(2)}) collective-permute-start(bf16[448,1024]{1,0:T(8,128)(2,1)S(1)} %get-tuple-element.69), channel_id=1, source_target_pairs={{0,8},{8,16},{16,24},{24,0},{1,9},{9,17},{17,25},{25,1},{2,10},{10... | collective-permute-start | bytes 2752520 | tf_op jit(solution)/shard_map/ppermute | solution.py:18
  405.7 108.9 %collective-permute-start.13 = (bf16[448,1024]{1,0:T(8,128)(2,1)S(1)}, bf16[448,1024]{1,0:T(8,128)(2,1)S(1)}, u32[]{:S(2)}, u32[]{:S(2)}) collective-permute-start(bf16[448,1024]{1,0:T(8,128)(2,1)S(1)} %broadcast_select_fusion.11), channel_id=1, source_target_pairs={{0,8},{8,16},{16,24},{24,0},{1,9},{9,17},{17,25},{25,1},{2,10},{10... | collective-permute-start | bytes 2752520 | tf_op jit(solution)/shard_map/ppermute | solution.py:18
  443.0 61.0 %collective-permute-start.19 = (bf16[64,1024]{1,0:T(8,128)(2,1)S(1)}, bf16[64,1024]{1,0:T(8,128)(2,1)S(1)}, u32[]{:S(2)}, u32[]{:S(2)}) collective-permute-start(bf16[64,1024]{1,0:T(8,128)(2,1)S(1)} %copy-done.67), channel_id=1, source_target_pairs={{0,24},{8,0},{16,8},{24,16},{1,25},{9,1},{17,9},{25,17},{2,26},{10... | collective-permute-start | bytes 393224 | tf_op jit(solution)/shard_map/ppermute | solution.py:18
  510.7 83.3 %collective-permute-start.31 = (bf16[448,1024]{1,0:T(8,128)(2,1)S(1)}, bf16[448,1024]{1,0:T(8,128)(2,1)}, u32[]{:S(2)}, u32[]{:S(2)}) collective-permute-start(bf16[448,1024]{1,0:T(8,128)(2,1)S(1)} %get-tuple-element.72), channel_id=1, source_target_pairs={{0,24},{8,0},{16,8},{24,16},{1,25},{9,1},{17,9},{25,17},{2,26},{10... | collective-permute-start | bytes 2752520 | tf_op jit(solution)/shard_map/ppermute | solution.py:18
  515.6 78.4 %collective-permute-start.29 = (bf16[448,1024]{1,0:T(8,128)(2,1)S(1)}, bf16[448,1024]{1,0:T(8,128)(2,1)S(1)}, u32[]{:S(2)}, u32[]{:S(2)}) collective-permute-start(bf16[448,1024]{1,0:T(8,128)(2,1)S(1)} %broadcast_select_fusion.8), channel_id=1, source_target_pairs={{0,8},{8,16},{16,24},{24,0},{1,9},{9,17},{17,25},{25,1},{2,10},{10... | collective-permute-start | bytes 2752520 | tf_op jit(solution)/shard_map/ppermute | solution.py:18
  519.9 60.7 %collective-permute-start.35 = (bf16[64,1024]{1,0:T(8,128)(2,1)}, bf16[64,1024]{1,0:T(8,128)(2,1)S(1)}, u32[]{:S(2)}, u32[]{:S(2)}) collective-permute-start(bf16[64,1024]{1,0:T(8,128)(2,1)} %get-tuple-element.98), channel_id=1, source_target_pairs={{0,24},{8,0},{16,8},{24,16},{1,25},{9,1},{17,9},{25,17},{2,26},{10... | collective-permute-start | bytes 393224 | tf_op jit(solution)/shard_map/ppermute | solution.py:18
  591.2 80.9 %collective-permute-start.47 = (bf16[448,1024]{1,0:T(8,128)(2,1)S(1)}, bf16[448,1024]{1,0:T(8,128)(2,1)S(1)}, u32[]{:S(2)}, u32[]{:S(2)}) collective-permute-start(bf16[448,1024]{1,0:T(8,128)(2,1)S(1)} %get-tuple-element.70), channel_id=1, source_target_pairs={{0,24},{8,0},{16,8},{24,16},{1,25},{9,1},{17,9},{25,17},{2,26},{10... | collective-permute-start | bytes 2752520 | tf_op jit(solution)/shard_map/ppermute | solution.py:18
  594.0 78.0 %collective-permute-start.45 = (bf16[448,1024]{1,0:T(8,128)(2,1)S(1)}, bf16[448,1024]{1,0:T(8,128)(2,1)S(1)}, u32[]{:S(2)}, u32[]{:S(2)}) collective-permute-start(bf16[448,1024]{1,0:T(8,128)(2,1)S(1)} %broadcast_select_fusion.5), channel_id=1, source_target_pairs={{0,8},{8,16},{16,24},{24,0},{1,9},{9,17},{17,25},{25,1},{2,10},{10... | collective-permute-start | bytes 2752520 | tf_op jit(solution)/shard_map/ppermute | solution.py:18
  599.5 59.8 %collective-permute-start.51 = (bf16[64,1024]{1,0:T(8,128)(2,1)}, bf16[64,1024]{1,0:T(8,128)(2,1)S(1)}, u32[]{:S(2)}, u32[]{:S(2)}) collective-permute-start(bf16[64,1024]{1,0:T(8,128)(2,1)} %get-tuple-element.96), channel_id=1, source_target_pairs={{0,24},{8,0},{16,8},{24,16},{1,25},{9,1},{17,9},{25,17},{2,26},{10... | collective-permute-start | bytes 393224 | tf_op jit(solution)/shard_map/ppermute | solution.py:18
  669.1 63.2 %collective-permute-start.63 = (bf16[448,1024]{1,0:T(8,128)(2,1)S(1)}, bf16[448,1024]{1,0:T(8,128)(2,1)S(1)}, u32[]{:S(2)}, u32[]{:S(2)}) collective-permute-start(bf16[448,1024]{1,0:T(8,128)(2,1)S(1)} %get-tuple-element.68), channel_id=1, source_target_pairs={{0,24},{8,0},{16,8},{24,16},{1,25},{9,1},{17,9},{25,17},{2,26},{10... | collective-permute-start | bytes 2752520 | tf_op jit(solution)/shard_map/ppermute | solution.py:18
  672.1 60.2 %collective-permute-start.61 = (bf16[448,1024]{1,0:T(8,128)(2,1)S(1)}, bf16[448,1024]{1,0:T(8,128)(2,1)S(1)}, u32[]{:S(2)}, u32[]{:S(2)}) collective-permute-start(bf16[448,1024]{1,0:T(8,128)(2,1)S(1)} %broadcast_select_fusion.2), channel_id=1, source_target_pairs={{0,8},{8,16},{16,24},{24,0},{1,9},{9,17},{17,25},{25,1},{2,10},{10... | collective-permute-start | bytes 2752520 | tf_op jit(solution)/shard_map/ppermute | solution.py:18
  (123 other events, 3170.9 us)
Sparse Core Ops, SparseCore 0:
  9.9 33.2 all-gather.4
  45.0 33.8 all-gather.6
  80.8 25.8 all-gather.8
  108.4 27.8 all-gather.10

commit v5 on v2

--- a/solution.py
+++ b/solution.py
@@ -54,6 +54,7 @@
     starts = [sum(sizes[:i]) for i in range(len(sizes))]
     columns = [None] * len(sizes)
     weight_sent = None
+    first_total = None
     last = None
     for b in range(n_cols):
         span = slice(b * col_size, (b + 1) * col_size)
@@ -62,7 +63,9 @@
                 members = [0, 1][:len(sizes)] if a == 0 else [a]
                 width_a = sum(sizes[m] for m in members)
                 piece = acts[:, :, start:start + width_a]
-                if last is not None:
+                if last is not None and first_total is not None:
+                    piece, last, first_total = lax.optimization_barrier((piece, last, first_total))
+                elif last is not None:
                     piece, last = lax.optimization_barrier((piece, last))
                 cols = lax.all_to_all(piece, "node", split_axis=1, concat_axis=0, tiled=True)
                 cols = cols.reshape(-1, width_a).T
@@ -90,6 +93,8 @@
                 plus = shifted(half, "grp", groups - amount)
                 peers = w_minus * minus.astype(jnp.float32) + w_plus * plus.astype(jnp.float32)
             total = keep_share * half.astype(jnp.float32) + peers
+            if first_total is None:
+                first_total = total
             mixed = lax.dynamic_update_slice(mixed, total.astype(jnp.bfloat16), (start, b * col_size))
     weight_minus, weight_plus = weight_sent
     new_weight = keep_share * push_weight + w_minus * weight_minus + w_plus * weight_plus

time: 742 us -> 742 us (level)
    all_gather x4, waiting for transfers between devices: 18.3 us -> 7.61 us  [pipeline(): lax.all_gather(cotangent[:, b * col_size:(b + 1) * col_size], 'node', axi...]
    ppermute x34, waiting for transfers between devices: 494 us -> 502 us  [shifted(): return lax.ppermute(value, axis, pairs)]
  transfers between devices with their start and end apart: 41 -> 41, of which waited for: 13 -> 14; matrix products, arithmetic and copies ran while one was open for 14% -> 14% of each run, Pallas kernels for 0% -> 0%
where the time goes in v5:
time: 742 us; the launch traced here: 735 us
  waiting for transfers between devices  525 us (71%)
  starting transfers between devices  67.3 us (9%)
  matrix products  59.5 us (8%)
  local copies, waits for them, and re-layouts  34.2 us (5%)
  other arithmetic  18.7 us (3%)
  between operations  17.7 us (2%)
  loops' own time  12.3 us (2%)
    ppermute x34, waiting for transfers between devices, shifted(): return lax.ppermute(value, axis, pairs)  502 us
    dot_general x16, matrix products, pipeline(): lax.dot_general(cols, cot, rows_by_tokens, preferred_element_type=jnp.flo...  59.5 us
    ppermute x34, starting transfers between devices, shifted(): return lax.ppermute(value, axis, pairs)  52.7 us
    dynamic_update_slice x15, other arithmetic, pipeline(): lax.dynamic_update_slice(mixed, total.astype(jnp.bfloat16), (start, b * c...  18.5 us
  transfers between devices with their start and end apart: 41, of which 14 were waited for; matrix products, arithmetic and copies ran while one was open for 14% of the time, Pallas kernels for 0%

profile of v5, /device:TPU:0, one launch (start us, length us, event | category | flops | bytes accessed | tf_op | source)
XLA Modules:
  0.0 734.7 jit_solution(3768519186325098886)
XLA Ops:
  11.0 715.8 %conditional.1 = (bf16[1,1792,4096]{2,1,0:T(8,128)(2,1)}, f32[1]{0:T(128)}) conditional(s32[]{:T(128)} %clamp.3, (bf16[1,1792,4096]{2,1,0:T(8,128)(2,1)}, f32[]{:T(128)}, bf16[1,1792,4096]{2,1,0:T(8,128)(2,1)}, bf16[1,128,14336]{2,1,0:T(8,128)(2,1)}, bf16[128,4096]{1,0:T(8,128)(2,1)}, /*index=5*/pred[]{:T(512)}, f32[1]{0:T(128)}) %tuple.92, ...), branch_computations={%region_0.1_spmd, %region_1.2_spmd} | conditional | flops 15157166080 | bytes 549720256 | solution.py:116
  14.8 6.1 copy.19
  23.0 5.2 all-to-all-start
  30.4 13.3 %all-to-all-done = bf16[128,8,384]{0,2,1:T(8,128)(2,1)S(1)} async-done(((bf16[128,8,384]{0,2,1:T(8,128)(2,1)}), bf16[128,8,384]{0,2,1:T(8,128)(2,1)S(1)}, u32[]{:S(2)}, u32[]{:S(2)}) %all-to-all-start) | async-done | bytes 786464 | tf_op jit(solution)/shard_map/cond/branch_0_fun/all_to_all | solution.py:70
  59.7 5.8 collective-permute-done
  75.5 4.8 all-gather.11.cloned.1.call-done
  83.3 8.0 %collective-permute-start.9 = (bf16[128,1024]{1,0:T(8,128)(2,1)}, bf16[128,1024]{1,0:T(8,128)(2,1)}, u32[]{:S(2)}, u32[]{:S(2)}) collective-permute-start(bf16[128,1024]{1,0:T(8,128)(2,1)} %fusion.53), channel_id=1, source_target_pairs={{0,24},{8,0},{16,8},{24,16},{1,25},{9,1},{17,9},{25,17},{2,26},{10... | collective-permute-start | bytes 786440 | tf_op jit(solution)/shard_map/cond/branch_0_fun/ppermute | solution.py:18
  101.8 5.7 all-to-all-start.2
  107.4 7.3 pad_bitcast_fusion
  121.0 4.3 fusion.10
  125.4 30.3 %collective-permute-done.5 = bf16[512,1024]{1,0:T(8,128)(2,1)} collective-permute-done((bf16[512,1024]{1,0:T(8,128)(2,1)S(1)}, bf16[512,1024]{1,0:T(8,128)(2,1)}, u32[]{:S(2)}, u32[]{:S(2)}) %collective-permute-start.5) | collective-permute-done | bytes 1048608 | tf_op jit(solution)/shard_map/cond/branch_0_fun/ppermute | solution.py:18
  164.1 7.2 fusion.2
  179.9 6.0 fusion.3
  185.9 6.0 fusion.1
  200.6 23.0 %collective-permute-done.10 = bf16[256,1024]{1,0:T(8,128)(2,1)S(1)} collective-permute-done((bf16[256,1024]{1,0:T(8,128)(2,1)}, bf16[256,1024]{1,0:T(8,128)(2,1)S(1)}, u32[]{:S(2)}, u32[]{:S(2)}) %collective-permute-start.10) | collective-permute-done | bytes 524320 | tf_op jit(solution)/shard_map/cond/branch_0_fun/ppermute | solution.py:18
  229.2 117.6 %collective-permute-done.32 = f32[1]{0:T(128)} collective-permute-done((f32[1]{0:T(128)}, f32[1]{0:T(128)}, u32[]{:S(2)}, u32[]{:S(2)}) %collective-permute-start.32) | collective-permute-done | bytes 36 | tf_op jit(solution)/shard_map/cond/branch_0_fun/ppermute | solution.py:18
  355.3 4.3 collective-permute-done.16
  359.6 4.8 fusion
  365.8 37.9 %collective-permute-done.25 = bf16[128,1024]{1,0:T(8,128)(2,1)S(1)} collective-permute-done((bf16[128,1024]{1,0:T(8,128)(2,1)S(1)}, bf16[128,1024]{1,0:T(8,128)(2,1)S(1)}, u32[]{:S(2)}, u32[]{:S(2)}) %collective-permute-start.25) | collective-permute-done | bytes 262176 | tf_op jit(solution)/shard_map/cond/branch_0_fun/ppermute | solution.py:18
  407.7 25.9 %collective-permute-done.24 = bf16[128,1024]{1,0:T(8,128)(2,1)S(1)} collective-permute-done((bf16[128,1024]{1,0:T(8,128)(2,1)S(1)}, bf16[128,1024]{1,0:T(8,128)(2,1)S(1)}, u32[]{:S(2)}, u32[]{:S(2)}) %collective-permute-start.24) | collective-permute-done | bytes 262176 | tf_op jit(solution)/shard_map/cond/branch_0_fun/ppermute | solution.py:18
  448.6 121.6 %collective-permute-done.27 = bf16[256,1024]{1,0:T(8,128)(2,1)S(1)} collective-permute-done((bf16[256,1024]{1,0:T(8,128)(2,1)S(1)}, bf16[256,1024]{1,0:T(8,128)(2,1)S(1)}, u32[]{:S(2)}, u32[]{:S(2)}) %collective-permute-start.27) | collective-permute-done | bytes 524320 | tf_op jit(solution)/shard_map/cond/branch_0_fun/ppermute | solution.py:18
  570.1 4.3 collective-permute-start.31
  580.9 128.2 %collective-permute-done.26 = bf16[256,1024]{1,0:T(8,128)(2,1)S(1)} collective-permute-done((bf16[256,1024]{1,0:T(8,128)(2,1)S(1)}, bf16[256,1024]{1,0:T(8,128)(2,1)S(1)}, u32[]{:S(2)}, u32[]{:S(2)}) %collective-permute-start.26) | collective-permute-done | bytes 524320 | tf_op jit(solution)/shard_map/cond/branch_0_fun/ppermute | solution.py:18
  711.5 5.5 copy-done
  (152 shorter events, 121.7 us)
Async XLA Ops:
  13.3 66.9 %all-gather.11.cloned.1.call-start = ((), (), s32[]{:S(2)}) async-start(), calls=%async_computation.7 | async-start | bytes 2359296 | tf_op jit(solution)/shard_map/cond/branch_0_fun/all_gather | solution.py:49
  14.1 157.1 %all-gather.13.cloned.1.call-start = ((), (), s32[]{:S(2)}) async-start(), calls=%async_computation.8 | async-start | bytes 2359296 | tf_op jit(solution)/shard_map/cond/branch_0_fun/all_gather | solution.py:49
  69.3 122.7 %all-gather.15.cloned.1.call-start = ((), (), s32[]{:S(2)}) async-start(), calls=%async_computation.9 | async-start | bytes 2359296 | tf_op jit(solution)/shard_map/cond/branch_0_fun/all_gather | solution.py:49
  83.3 108.7 %collective-permute-start.9 = (bf16[128,1024]{1,0:T(8,128)(2,1)}, bf16[128,1024]{1,0:T(8,128)(2,1)}, u32[]{:S(2)}, u32[]{:S(2)}) collective-permute-start(bf16[128,1024]{1,0:T(8,128)(2,1)} %fusion.53), channel_id=1, source_target_pairs={{0,24},{8,0},{16,8},{24,16},{1,25},{9,1},{17,9},{25,17},{2,26},{10... | collective-permute-start | bytes 786440 | tf_op jit(solution)/shard_map/cond/branch_0_fun/ppermute | solution.py:18
  114.7 79.3 %collective-permute-start.8 = (bf16[128,1024]{1,0:T(8,128)(2,1)}, bf16[128,1024]{1,0:T(8,128)(2,1)}, u32[]{:S(2)}, u32[]{:S(2)}) collective-permute-start(bf16[128,1024]{1,0:T(8,128)(2,1)} %fusion.53), channel_id=1, source_target_pairs={{0,8},{8,16},{16,24},{24,0},{1,9},{9,17},{17,25},{25,1},{2,10},{10... | collective-permute-start | bytes 786440 | tf_op jit(solution)/shard_map/cond/branch_0_fun/ppermute | solution.py:18
  114.8 81.1 %collective-permute-start.11 = (bf16[256,1024]{1,0:T(8,128)(2,1)}, bf16[256,1024]{1,0:T(8,128)(2,1)}, u32[]{:S(2)}, u32[]{:S(2)}) collective-permute-start(bf16[256,1024]{1,0:T(8,128)(2,1)} %fusion.37), channel_id=1, source_target_pairs={{0,24},{8,0},{16,8},{24,16},{1,25},{9,1},{17,9},{25,17},{2,26},{10... | collective-permute-start | bytes 1572872 | tf_op jit(solution)/shard_map/cond/branch_0_fun/ppermute | solution.py:18
  155.6 71.5 %collective-permute-start.13 = (bf16[512,1024]{1,0:T(8,128)(2,1)}, bf16[512,1024]{1,0:T(8,128)(2,1)}, u32[]{:S(2)}, u32[]{:S(2)}) collective-permute-start(bf16[512,1024]{1,0:T(8,128)(2,1)} %fusion.10), channel_id=1, source_target_pairs={{0,24},{8,0},{16,8},{24,16},{1,25},{9,1},{17,9},{25,17},{2,26},{10... | collective-permute-start | bytes 3145736 | tf_op jit(solution)/shard_map/cond/branch_0_fun/ppermute | solution.py:18
  155.6 72.0 %collective-permute-start.12 = (bf16[512,1024]{1,0:T(8,128)(2,1)}, bf16[512,1024]{1,0:T(8,128)(2,1)}, u32[]{:S(2)}, u32[]{:S(2)}) collective-permute-start(bf16[512,1024]{1,0:T(8,128)(2,1)} %fusion.10), channel_id=1, source_target_pairs={{0,8},{8,16},{16,24},{24,0},{1,9},{9,17},{17,25},{25,1},{2,10},{10... | collective-permute-start | bytes 3145736 | tf_op jit(solution)/shard_map/cond/branch_0_fun/ppermute | solution.py:18
  194.0 211.4 %collective-permute-start.7 = (bf16[896,1024]{1,0:T(8,128)(2,1)}, bf16[896,1024]{1,0:T(8,128)(2,1)S(1)}, u32[]{:S(2)}, u32[]{:S(2)}) collective-permute-start(bf16[896,1024]{1,0:T(8,128)(2,1)} %fusion.3), channel_id=1, source_target_pairs={{0,24},{8,0},{16,8},{24,16},{1,25},{9,1},{17,9},{25,17},{2,26},{10... | collective-permute-start | bytes 5505032 | tf_op jit(solution)/shard_map/cond/branch_0_fun/ppermute | solution.py:18
  195.9 209.9 %collective-permute-start.6 = (bf16[896,1024]{1,0:T(8,128)(2,1)}, bf16[896,1024]{1,0:T(8,128)(2,1)S(1)}, u32[]{:S(2)}, u32[]{:S(2)}) collective-permute-start(bf16[896,1024]{1,0:T(8,128)(2,1)} %fusion.3), channel_id=1, source_target_pairs={{0,8},{8,16},{16,24},{24,0},{1,9},{9,17},{17,25},{25,1},{2,10},{10... | collective-permute-start | bytes 5505032 | tf_op jit(solution)/shard_map/cond/branch_0_fun/ppermute | solution.py:18
  223.6 216.9 %collective-permute-start.15 = (bf16[896,1024]{1,0:T(8,128)(2,1)S(1)}, bf16[896,1024]{1,0:T(8,128)(2,1)S(1)}, u32[]{:S(2)}, u32[]{:S(2)}) collective-permute-start(bf16[896,1024]{1,0:T(8,128)(2,1)S(1)} %copy-done.16), channel_id=1, source_target_pairs={{0,24},{8,0},{16,8},{24,16},{1,25},{9,1},{17,9},{25,17},{2,26},{10... | collective-permute-start | bytes 5505032 | tf_op jit(solution)/shard_map/cond/branch_0_fun/ppermute | solution.py:18
  227.2 128.1 %collective-permute-start.17 = (bf16[128,1024]{1,0:T(8,128)(2,1)S(1)}, bf16[128,1024]{1,0:T(8,128)(2,1)S(1)}, u32[]{:S(2)}, u32[]{:S(2)}) collective-permute-start(bf16[128,1024]{1,0:T(8,128)(2,1)S(1)} %fusion.54), channel_id=1, source_target_pairs={{0,24},{8,0},{16,8},{24,16},{1,25},{9,1},{17,9},{25,17},{2,26},{10... | collective-permute-start | bytes 786440 | tf_op jit(solution)/shard_map/cond/branch_0_fun/ppermute | solution.py:18
  227.6 119.2 %collective-permute-start.32 = (f32[1]{0:T(128)}, f32[1]{0:T(128)}, u32[]{:S(2)}, u32[]{:S(2)}) collective-permute-start(f32[1]{0:T(128)} %get-tuple-element.67), channel_id=1, source_target_pairs={{0,8},{8,16},{16,24},{24,0},{1,9},{9,17},{17,25},{25,1},{2,10},{10... | collective-permute-start | bytes 20 | tf_op jit(solution)/shard_map/cond/branch_0_fun/ppermute | solution.py:18
  355.3 87.9 %collective-permute-start.14 = (bf16[896,1024]{1,0:T(8,128)(2,1)S(1)}, bf16[896,1024]{1,0:T(8,128)(2,1)S(1)}, u32[]{:S(2)}, u32[]{:S(2)}) collective-permute-start(bf16[896,1024]{1,0:T(8,128)(2,1)S(1)} %copy-done.16), channel_id=1, source_target_pairs={{0,8},{8,16},{16,24},{24,0},{1,9},{9,17},{17,25},{25,1},{2,10},{10... | collective-permute-start | bytes 5505032 | tf_op jit(solution)/shard_map/cond/branch_0_fun/ppermute | solution.py:18
  433.5 145.1 %collective-permute-start.23 = (bf16[896,1024]{1,0:T(8,128)(2,1)S(1)}, bf16[896,1024]{1,0:T(8,128)(2,1)S(1)}, u32[]{:S(2)}, u32[]{:S(2)}) collective-permute-start(bf16[896,1024]{1,0:T(8,128)(2,1)S(1)} %copy-done.15), channel_id=1, source_target_pairs={{0,24},{8,0},{16,8},{24,16},{1,25},{9,1},{17,9},{25,17},{2,26},{10... | collective-permute-start | bytes 5505032 | tf_op jit(solution)/shard_map/cond/branch_0_fun/ppermute | solution.py:18
  437.1 137.3 %collective-permute-start.21 = (bf16[512,1024]{1,0:T(8,128)(2,1)S(1)}, bf16[512,1024]{1,0:T(8,128)(2,1)S(1)}, u32[]{:S(2)}, u32[]{:S(2)}) collective-permute-start(bf16[512,1024]{1,0:T(8,128)(2,1)S(1)} %fusion.9), channel_id=1, source_target_pairs={{0,24},{8,0},{16,8},{24,16},{1,25},{9,1},{17,9},{25,17},{2,26},{10... | collective-permute-start | bytes 3145736 | tf_op jit(solution)/shard_map/cond/branch_0_fun/ppermute | solution.py:18
  438.4 140.9 %collective-permute-start.22 = (bf16[896,1024]{1,0:T(8,128)(2,1)S(1)}, bf16[896,1024]{1,0:T(8,128)(2,1)S(1)}, u32[]{:S(2)}, u32[]{:S(2)}) collective-permute-start(bf16[896,1024]{1,0:T(8,128)(2,1)S(1)} %copy-done.15), channel_id=1, source_target_pairs={{0,8},{8,16},{16,24},{24,0},{1,9},{9,17},{17,25},{25,1},{2,10},{10... | collective-permute-start | bytes 5505032 | tf_op jit(solution)/shard_map/cond/branch_0_fun/ppermute | solution.py:18
  440.6 134.2 %collective-permute-start.20 = (bf16[512,1024]{1,0:T(8,128)(2,1)S(1)}, bf16[512,1024]{1,0:T(8,128)(2,1)S(1)}, u32[]{:S(2)}, u32[]{:S(2)}) collective-permute-start(bf16[512,1024]{1,0:T(8,128)(2,1)S(1)} %fusion.9), channel_id=1, source_target_pairs={{0,8},{8,16},{16,24},{24,0},{1,9},{9,17},{17,25},{25,1},{2,10},{10... | collective-permute-start | bytes 3145736 | tf_op jit(solution)/shard_map/cond/branch_0_fun/ppermute | solution.py:18
  443.2 126.9 %collective-permute-start.27 = (bf16[256,1024]{1,0:T(8,128)(2,1)S(1)}, bf16[256,1024]{1,0:T(8,128)(2,1)S(1)}, u32[]{:S(2)}, u32[]{:S(2)}) collective-permute-start(bf16[256,1024]{1,0:T(8,128)(2,1)S(1)} %fusion.39), channel_id=1, source_target_pairs={{0,24},{8,0},{16,8},{24,16},{1,25},{9,1},{17,9},{25,17},{2,26},{10... | collective-permute-start | bytes 1572872 | tf_op jit(solution)/shard_map/cond/branch_0_fun/ppermute | solution.py:18
  570.1 140.0 %collective-permute-start.31 = (bf16[896,1024]{1,0:T(8,128)(2,1)S(1)}, bf16[896,1024]{1,0:T(8,128)(2,1)S(1)}, u32[]{:S(2)}, u32[]{:S(2)}) collective-permute-start(bf16[896,1024]{1,0:T(8,128)(2,1)S(1)} %fusion), channel_id=1, source_target_pairs={{0,24},{8,0},{16,8},{24,16},{1,25},{9,1},{17,9},{25,17},{2,26},{10... | collective-permute-start | bytes 5505032 | tf_op jit(solution)/shard_map/cond/branch_0_fun/ppermute | solution.py:18
  574.4 135.8 %collective-permute-start.30 = (bf16[896,1024]{1,0:T(8,128)(2,1)S(1)}, bf16[896,1024]{1,0:T(8,128)(2,1)S(1)}, u32[]{:S(2)}, u32[]{:S(2)}) collective-permute-start(bf16[896,1024]{1,0:T(8,128)(2,1)S(1)} %fusion), channel_id=1, source_target_pairs={{0,8},{8,16},{16,24},{24,0},{1,9},{9,17},{17,25},{25,1},{2,10},{10... | collective-permute-start | bytes 5505032 | tf_op jit(solution)/shard_map/cond/branch_0_fun/ppermute | solution.py:18
  574.7 134.7 %collective-permute-start.29 = (bf16[512,1024]{1,0:T(8,128)(2,1)S(1)}, bf16[512,1024]{1,0:T(8,128)(2,1)S(1)}, u32[]{:S(2)}, u32[]{:S(2)}) collective-permute-start(bf16[512,1024]{1,0:T(8,128)(2,1)S(1)} %fusion.8), channel_id=1, source_target_pairs={{0,24},{8,0},{16,8},{24,16},{1,25},{9,1},{17,9},{25,17},{2,26},{10... | collective-permute-start | bytes 3145736 | tf_op jit(solution)/shard_map/cond/branch_0_fun/ppermute | solution.py:18
  578.6 130.8 %collective-permute-start.28 = (bf16[512,1024]{1,0:T(8,128)(2,1)S(1)}, bf16[512,1024]{1,0:T(8,128)(2,1)S(1)}, u32[]{:S(2)}, u32[]{:S(2)}) collective-permute-start(bf16[512,1024]{1,0:T(8,128)(2,1)S(1)} %fusion.8), channel_id=1, source_target_pairs={{0,8},{8,16},{16,24},{24,0},{1,9},{9,17},{17,25},{25,1},{2,10},{10... | collective-permute-start | bytes 3145736 | tf_op jit(solution)/shard_map/cond/branch_0_fun/ppermute | solution.py:18
  579.3 129.8 %collective-permute-start.26 = (bf16[256,1024]{1,0:T(8,128)(2,1)S(1)}, bf16[256,1024]{1,0:T(8,128)(2,1)S(1)}, u32[]{:S(2)}, u32[]{:S(2)}) collective-permute-start(bf16[256,1024]{1,0:T(8,128)(2,1)S(1)} %fusion.39), channel_id=1, source_target_pairs={{0,8},{8,16},{16,24},{24,0},{1,9},{9,17},{17,25},{25,1},{2,10},{10... | collective-permute-start | bytes 1572872 | tf_op jit(solution)/shard_map/cond/branch_0_fun/ppermute | solution.py:18
  (39 other events, 1276.0 us)
Sparse Core Ops, SparseCore 0:
  13.8 33.2 all-gather.8
  48.9 31.3 all-gather.10
  82.2 41.6 all-gather.12
  125.7 36.5 all-gather.14

commit v6 on v2

--- a/solution.py
+++ b/solution.py
@@ -35,7 +35,36 @@
     return sizes
 
 
-def pipeline(amount, groups, params, momentum, hidden, cotangent, push_weight, rate, direct):
+def half_step(cols, cot, params, momentum, rate):
+    tok_group = cols.shape[1]
+    grad = lax.dot_general(cols, cot, rows_by_tokens, preferred_element_type=jnp.float32)
+    grad = grad / tok_group
+    renewed = moment_decay * momentum.astype(jnp.float32) + grad
+    return (params.astype(jnp.float32) - rate * renewed).astype(jnp.bfloat16)
+
+
+def head_tiles(params, momentum, hidden, cotangent, rate):
+    nodes = lax.axis_size("node")
+    rows_total = params.shape[1]
+    acts = hidden.reshape(hidden.shape[0], nodes, rows_total)
+    col_size = cotangent.shape[1] // block_count(cotangent.shape[1], col_blocks, 128)
+    sizes = row_sizes(rows_total)[:2]
+    width_a = sum(sizes)
+    first_cots = lax.all_gather(cotangent[:, :col_size], "node", axis=0, tiled=True)
+    cols = lax.all_to_all(acts[:, :, :width_a], "node", split_axis=1, concat_axis=0, tiled=True)
+    cols = cols.reshape(-1, width_a).T
+    columns, halves, start = [], [], 0
+    for size in sizes:
+        columns.append(cols[start:start + size])
+        rows = slice(start, start + size)
+        halves.append(
+            half_step(columns[-1], first_cots, params[0, rows, :col_size], momentum[0, rows, :col_size], rate)
+        )
+        start += size
+    return first_cots, tuple(columns), tuple(halves)
+
+
+def pipeline(amount, groups, params, momentum, hidden, cotangent, push_weight, rate, direct, head):
     nodes = lax.axis_size("node")
     rows_total = params.shape[1]
     acts = hidden.reshape(hidden.shape[0], nodes, rows_total)
@@ -45,14 +74,15 @@
     paired = (2 * amount) % groups == 0
     w_minus = jnp.where(direct, back_share, front_share).astype(jnp.float32)
     w_plus = jnp.where(direct, front_share, back_share).astype(jnp.float32)
-    cots = [
+    first_cots, first_columns, first_halves = head
+    cots = [first_cots] + [
         lax.all_gather(cotangent[:, b * col_size:(b + 1) * col_size], "node", axis=0, tiled=True)
-        for b in range(n_cols)
+        for b in range(1, n_cols)
     ]
     mixed = jnp.zeros(params.shape[1:], jnp.bfloat16)
     sizes = row_sizes(rows_total)
     starts = [sum(sizes[:i]) for i in range(len(sizes))]
-    columns = [None] * len(sizes)
+    columns = list(first_columns) + [None] * (len(sizes) - len(first_columns))
     weight_sent = None
     last = None
     for b in range(n_cols):
@@ -70,15 +100,14 @@
                 for m in members:
                     columns[m] = cols[offset_a:offset_a + sizes[m]]
                     offset_a += sizes[m]
-            cols, cot = columns[a], cots[b]
-            if last is not None:
-                cols, cot, last = lax.optimization_barrier((cols, cot, last))
-            tok_group = cols.shape[1]
             rows = slice(start, start + size)
-            grad = lax.dot_general(cols, cot, rows_by_tokens, preferred_element_type=jnp.float32)
-            grad = grad / tok_group
-            renewed = moment_decay * momentum[0, rows, span].astype(jnp.float32) + grad
-            half = (params[0, rows, span].astype(jnp.float32) - rate * renewed).astype(jnp.bfloat16)
+            if b == 0 and a < len(first_halves):
+                half = first_halves[a]
+            else:
+                cols, cot = columns[a], cots[b]
+                if last is not None:
+                    cols, cot, last = lax.optimization_barrier((cols, cot, last))
+                half = half_step(cols, cot, params[0, rows, span], momentum[0, rows, span], rate)
             last = half
             if weight_sent is None and b == 0 and a == len(sizes) - 1:
                 weight, last = lax.optimization_barrier((push_weight, last))
@@ -108,8 +137,9 @@
         (lambda *a, amount=amount: pipeline(amount, groups, *a))
         for amount in amounts
     ]
+    head = head_tiles(params, momentum, hidden[0], cotangent[0], rate)
     return lax.switch(
-        index, branches, params, momentum, hidden[0], cotangent[0], push_weight, rate, direct
+        index, branches, params, momentum, hidden[0], cotangent[0], push_weight, rate, direct, head
     )
 
 

time: 742 us -> 747 us (level)
  starting transfers between devices: 64.5 us -> 25 us
  waiting for transfers between devices: 527 us -> 566 us
    ppermute x34 -> x17, waiting for transfers between devices: 494 us -> 549 us  [shifted(): return lax.ppermute(value, axis, pairs)]
    ppermute x34 -> x17, starting transfers between devices: 52 us -> 12 us  [shifted(): return lax.ppermute(value, axis, pairs)]
    all_gather x4 -> x3, waiting for transfers between devices: 18.3 us -> 0.02 us  [pipeline(): lax.all_gather(cotangent[:, b * col_size:(b + 1) * col_size], 'node', axi...]
    all_to_all x3 -> x2, waiting for transfers between devices: 13.3 us -> 0.01 us  [pipeline(): lax.all_to_all(piece, 'node', split_axis=1, concat_axis=0, tiled=True)]
    all_to_all x0 -> x1, waiting for transfers between devices: none -> 9.44 us  [head_tiles(): lax.all_to_all(acts[:, :, :width_a], 'node', split_axis=1, concat_axis=0,...]
  transfers between devices with their start and end apart: 41 -> 24, of which waited for: 13 -> 16; matrix products, arithmetic and copies ran while one was open for 14% -> 14% of each run, Pallas kernels for 0% -> 0%
where the time goes in v6:
time: 747 us; the launch traced here: 738 us
  waiting for transfers between devices  566 us (76%)
  matrix products  61 us (8%)
  local copies, waits for them, and re-layouts  41.4 us (6%)
  starting transfers between devices  25 us (3%)
  other arithmetic  19.2 us (3%)
  between operations  18 us (2%)
    ppermute x17, waiting for transfers between devices, shifted(): return lax.ppermute(value, axis, pairs)  549 us
    dot_general x16, matrix products, half_step(): lax.dot_general(cols, cot, rows_by_tokens, preferred_element_type=jnp.flo...  61 us
    dynamic_update_slice x15, other arithmetic, pipeline(): lax.dynamic_update_slice(mixed, total.astype(jnp.bfloat16), (start, b * c...  18.2 us
  transfers between devices with their start and end apart: 24, of which 16 were waited for; matrix products, arithmetic and copies ran while one was open for 14% of the time, Pallas kernels for 0%

profile of v6, /device:TPU:0, one launch (start us, length us, event | category | flops | bytes accessed | tf_op | source)
XLA Modules:
  0.0 738.0 jit_solution(16481445858685874129)
XLA Ops:
  8.9 6.1 copy.33
  25.5 9.4 %all-to-all-done.4 = bf16[128,8,384]{0,2,1:T(8,128)(2,1)S(1)} async-done(((bf16[128,8,384]{0,2,1:T(8,128)(2,1)}), bf16[128,8,384]{0,2,1:T(8,128)(2,1)S(1)}, u32[]{:S(2)}, u32[]{:S(2)}) %all-to-all-start.4) | async-done | bytes 786464 | tf_op jit(solution)/shard_map/all_to_all | solution.py:54
  35.3 6.8 all-gather.20.cloned.1.call-done
  48.6 681.2 %conditional.1 = (bf16[1,1792,4096]{2,1,0:T(8,128)(2,1)}, f32[1]{0:T(128)}) conditional(s32[]{:T(128)} %clamp.3, (bf16[128,1024]{1,0:T(8,128)(2,1)}, pred[]{:T(512)}, bf16[256,1024]{1,0:T(8,128)(2,1)}, bf16[1,1792,4096]{2,1,0:T(8,128)(2,1)}, f32[]{:T(128)}, /*index=5*/bf16[1,1792,4096]{2,1,0:T(8,128)(2,1)}, bf16[1,128,14336]{2,1,0:T(8,128)(2,1)}, ...), branch_computations={%region_0.1_spmd, %region_1.2_spmd} | conditional | flops 14348713984 | bytes 519836096 | solution.py:141
  54.8 6.1 copy.38
  74.6 19.4 %collective-permute-done.34 = bf16[128,1024]{1,0:T(8,128)(2,1)S(1)} collective-permute-done((bf16[128,1024]{1,0:T(8,128)(2,1)}, bf16[128,1024]{1,0:T(8,128)(2,1)S(1)}, u32[]{:S(2)}, u32[]{:S(2)}) %collective-permute-start.34) | collective-permute-done | bytes 262176 | tf_op jit(solution)/shard_map/cond/branch_1_fun/ppermute | solution.py:18
  104.7 7.3 pad_bitcast_fusion.1
  112.0 15.8 %collective-permute-done.35 = bf16[256,1024]{1,0:T(8,128)(2,1)} collective-permute-done((bf16[256,1024]{1,0:T(8,128)(2,1)}, bf16[256,1024]{1,0:T(8,128)(2,1)}, u32[]{:S(2)}, u32[]{:S(2)}) %collective-permute-start.35) | collective-permute-done | bytes 524320 | tf_op jit(solution)/shard_map/cond/branch_1_fun/ppermute | solution.py:18
  130.0 19.6 %collective-permute-done.36 = bf16[512,1024]{1,0:T(8,128)(2,1)} collective-permute-done((bf16[512,1024]{1,0:T(8,128)(2,1)S(1)}, bf16[512,1024]{1,0:T(8,128)(2,1)}, u32[]{:S(2)}, u32[]{:S(2)}) %collective-permute-start.36) | collective-permute-done | bytes 1048608 | tf_op jit(solution)/shard_map/cond/branch_1_fun/ppermute | solution.py:18
  155.1 7.2 fusion.73
  165.2 79.1 %collective-permute-done.50 = f32[1]{0:T(128)} collective-permute-done((f32[1]{0:T(128)}, f32[1]{0:T(128)}, u32[]{:S(2)}, u32[]{:S(2)}) %collective-permute-start.50) | collective-permute-done | bytes 36 | tf_op jit(solution)/shard_map/cond/branch_1_fun/ppermute | solution.py:18
  258.7 6.1 fusion.72
  275.7 6.3 fusion.71
  298.3 42.6 %collective-permute-done.38 = bf16[128,1024]{1,0:T(8,128)(2,1)} collective-permute-done((bf16[128,1024]{1,0:T(8,128)(2,1)}, bf16[128,1024]{1,0:T(8,128)(2,1)}, u32[]{:S(2)}, u32[]{:S(2)}) %collective-permute-start.38) | collective-permute-done | bytes 262176 | tf_op jit(solution)/shard_map/cond/branch_1_fun/ppermute | solution.py:18
  342.1 49.4 %collective-permute-done.39 = bf16[256,1024]{1,0:T(8,128)(2,1)} collective-permute-done((bf16[256,1024]{1,0:T(8,128)(2,1)}, bf16[256,1024]{1,0:T(8,128)(2,1)}, u32[]{:S(2)}, u32[]{:S(2)}) %collective-permute-start.39) | collective-permute-done | bytes 524320 | tf_op jit(solution)/shard_map/cond/branch_1_fun/ppermute | solution.py:18
  392.9 32.3 %collective-permute-done.40 = bf16[512,1024]{1,0:T(8,128)(2,1)} collective-permute-done((bf16[512,1024]{1,0:T(8,128)(2,1)}, bf16[512,1024]{1,0:T(8,128)(2,1)}, u32[]{:S(2)}, u32[]{:S(2)}) %collective-permute-start.40) | collective-permute-done | bytes 1048608 | tf_op jit(solution)/shard_map/cond/branch_1_fun/ppermute | solution.py:18
  427.2 59.9 %collective-permute-done.41 = bf16[896,1024]{1,0:T(8,128)(2,1)} collective-permute-done((bf16[896,1024]{1,0:T(8,128)(2,1)}, bf16[896,1024]{1,0:T(8,128)(2,1)}, u32[]{:S(2)}, u32[]{:S(2)}) %collective-permute-start.41) | collective-permute-done | bytes 1835040 | tf_op jit(solution)/shard_map/cond/branch_1_fun/ppermute | solution.py:18
  489.9 8.3 %collective-permute-done.42 = bf16[128,1024]{1,0:T(8,128)(2,1)S(1)} collective-permute-done((bf16[128,1024]{1,0:T(8,128)(2,1)S(1)}, bf16[128,1024]{1,0:T(8,128)(2,1)S(1)}, u32[]{:S(2)}, u32[]{:S(2)}) %collective-permute-start.42) | collective-permute-done | bytes 262176 | tf_op jit(solution)/shard_map/cond/branch_1_fun/ppermute | solution.py:18
  498.3 89.8 %collective-permute-done.43 = bf16[256,1024]{1,0:T(8,128)(2,1)S(1)} collective-permute-done((bf16[256,1024]{1,0:T(8,128)(2,1)S(1)}, bf16[256,1024]{1,0:T(8,128)(2,1)S(1)}, u32[]{:S(2)}, u32[]{:S(2)}) %collective-permute-start.43) | collective-permute-done | bytes 524320 | tf_op jit(solution)/shard_map/cond/branch_1_fun/ppermute | solution.py:18
  588.2 33.5 %collective-permute-done.44 = bf16[512,1024]{1,0:T(8,128)(2,1)S(1)} collective-permute-done((bf16[512,1024]{1,0:T(8,128)(2,1)S(1)}, bf16[512,1024]{1,0:T(8,128)(2,1)S(1)}, u32[]{:S(2)}, u32[]{:S(2)}) %collective-permute-start.44) | collective-permute-done | bytes 1048608 | tf_op jit(solution)/shard_map/cond/branch_1_fun/ppermute | solution.py:18
  623.0 26.8 %collective-permute-done.46 = bf16[128,1024]{1,0:T(8,128)(2,1)S(1)} collective-permute-done((bf16[128,1024]{1,0:T(8,128)(2,1)S(1)}, bf16[128,1024]{1,0:T(8,128)(2,1)S(1)}, u32[]{:S(2)}, u32[]{:S(2)}) %collective-permute-start.46) | collective-permute-done | bytes 262176 | tf_op jit(solution)/shard_map/cond/branch_1_fun/ppermute | solution.py:18
  649.9 50.5 %collective-permute-done.47 = bf16[256,1024]{1,0:T(8,128)(2,1)S(1)} collective-permute-done((bf16[256,1024]{1,0:T(8,128)(2,1)S(1)}, bf16[256,1024]{1,0:T(8,128)(2,1)S(1)}, u32[]{:S(2)}, u32[]{:S(2)}) %collective-permute-start.47) | collective-permute-done | bytes 524320 | tf_op jit(solution)/shard_map/cond/branch_1_fun/ppermute | solution.py:18
  700.6 22.2 %collective-permute-done.48 = bf16[512,1024]{1,0:T(8,128)(2,1)S(1)} collective-permute-done((bf16[512,1024]{1,0:T(8,128)(2,1)S(1)}, bf16[512,1024]{1,0:T(8,128)(2,1)S(1)}, u32[]{:S(2)}, u32[]{:S(2)}) %collective-permute-start.48) | collective-permute-done | bytes 1048608 | tf_op jit(solution)/shard_map/cond/branch_1_fun/ppermute | solution.py:18
  724.1 5.5 copy-done.1
  (116 shorter events, 102.9 us)
Async XLA Ops:
  7.2 34.9 %all-gather.20.cloned.1.call-start = ((), (), s32[]{:S(2)}) async-start(), calls=%async_computation.11 | async-start | bytes 2359296 | tf_op jit(solution)/shard_map/all_gather | solution.py:53
  17.1 17.8 %all-to-all-start.4 = ((bf16[128,8,384]{0,2,1:T(8,128)(2,1)}), bf16[128,8,384]{0,2,1:T(8,128)(2,1)S(1)}, u32[]{:S(2)}, u32[]{:S(2)}) async-start(bf16[128,8,384]{0,2,1:T(8,128)(2,1)} %slice.234), calls=%async_computation.4 | async-start | bytes 1572864 | tf_op jit(solution)/shard_map/all_to_all | solution.py:54
  53.1 192.5 %all-gather.14.cloned.1.call-start = ((), (), s32[]{:S(2)}) async-start(), calls=%async_computation.8 | async-start | bytes 2359296 | tf_op jit(solution)/shard_map/cond/branch_1_fun/all_gather | solution.py:79
  54.1 213.4 %all-gather.16.cloned.1.call-start = ((), (), s32[]{:S(2)}) async-start(), calls=%async_computation.9 | async-start | bytes 2359296 | tf_op jit(solution)/shard_map/cond/branch_1_fun/all_gather | solution.py:79
  63.2 31.8 %all-to-all-start.2 = ((bf16[128,8,512]{0,2,1:T(8,128)(2,1)}), bf16[128,8,512]{0,2,1:T(8,128)(2,1)S(1)}, u32[]{:S(2)}, u32[]{:S(2)}) async-start(bf16[128,8,512]{0,2,1:T(8,128)(2,1)} %slice.232), calls=%async_computation.2 | async-start | bytes 2097152 | tf_op jit(solution)/shard_map/cond/branch_1_fun/all_to_all | solution.py:97
  66.8 215.2 %all-gather.18.cloned.1.call-start = ((), (), s32[]{:S(2)}) async-start(), calls=%async_computation.10 | async-start | bytes 2359296 | tf_op jit(solution)/shard_map/cond/branch_1_fun/all_gather | solution.py:79
  66.8 27.2 %collective-permute-start.34 = (bf16[128,1024]{1,0:T(8,128)(2,1)}, bf16[128,1024]{1,0:T(8,128)(2,1)S(1)}, u32[]{:S(2)}, u32[]{:S(2)}) collective-permute-start(bf16[128,1024]{1,0:T(8,128)(2,1)} %get-tuple-element.91), channel_id=1, source_target_pairs={{0,16},{8,24},{16,0},{24,8},{1,17},{9,25},{17,1},{25,9},{2,18},{10... | collective-permute-start | bytes 786440 | tf_op jit(solution)/shard_map/cond/branch_1_fun/ppermute | solution.py:18
  69.4 58.4 %collective-permute-start.35 = (bf16[256,1024]{1,0:T(8,128)(2,1)}, bf16[256,1024]{1,0:T(8,128)(2,1)}, u32[]{:S(2)}, u32[]{:S(2)}) collective-permute-start(bf16[256,1024]{1,0:T(8,128)(2,1)} %get-tuple-element.92), channel_id=1, source_target_pairs={{0,16},{8,24},{16,0},{24,8},{1,17},{9,25},{17,1},{25,9},{2,18},{10... | collective-permute-start | bytes 1572872 | tf_op jit(solution)/shard_map/cond/branch_1_fun/ppermute | solution.py:18
  100.5 49.1 %collective-permute-start.36 = (bf16[512,1024]{1,0:T(8,128)(2,1)S(1)}, bf16[512,1024]{1,0:T(8,128)(2,1)}, u32[]{:S(2)}, u32[]{:S(2)}) collective-permute-start(bf16[512,1024]{1,0:T(8,128)(2,1)S(1)} %fusion.81), channel_id=1, source_target_pairs={{0,16},{8,24},{16,0},{24,8},{1,17},{9,25},{17,1},{25,9},{2,18},{10... | collective-permute-start | bytes 3145736 | tf_op jit(solution)/shard_map/cond/branch_1_fun/ppermute | solution.py:18
  100.6 51.6 %all-to-all-start.3 = ((bf16[128,8,896]{0,2,1:T(8,128)(2,1)}), bf16[128,8,896]{0,2,1:T(8,128)(2,1)S(1)}, u32[]{:S(2)}, u32[]{:S(2)}) async-start(bf16[128,8,896]{0,2,1:T(8,128)(2,1)} %slice.233), calls=%async_computation.3 | async-start | bytes 3670016 | tf_op jit(solution)/shard_map/cond/branch_1_fun/all_to_all | solution.py:97
  162.3 132.7 %collective-permute-start.37 = (bf16[896,1024]{1,0:T(8,128)(2,1)}, bf16[896,1024]{1,0:T(8,128)(2,1)}, u32[]{:S(2)}, u32[]{:S(2)}) collective-permute-start(bf16[896,1024]{1,0:T(8,128)(2,1)} %fusion.73), channel_id=1, source_target_pairs={{0,16},{8,24},{16,0},{24,8},{1,17},{9,25},{17,1},{25,9},{2,18},{10... | collective-permute-start | bytes 5505032 | tf_op jit(solution)/shard_map/cond/branch_1_fun/ppermute | solution.py:18
  162.3 82.0 %collective-permute-start.50 = (f32[1]{0:T(128)}, f32[1]{0:T(128)}, u32[]{:S(2)}, u32[]{:S(2)}) collective-permute-start(f32[1]{0:T(128)} %get-tuple-element.133), channel_id=1, source_target_pairs={{0,16},{8,24},{16,0},{24,8},{1,17},{9,25},{17,1},{25,9},{2,18},{10... | collective-permute-start | bytes 20 | tf_op jit(solution)/shard_map/cond/branch_1_fun/ppermute | solution.py:18
  248.7 92.3 %collective-permute-start.38 = (bf16[128,1024]{1,0:T(8,128)(2,1)}, bf16[128,1024]{1,0:T(8,128)(2,1)}, u32[]{:S(2)}, u32[]{:S(2)}) collective-permute-start(bf16[128,1024]{1,0:T(8,128)(2,1)} %fusion.115), channel_id=1, source_target_pairs={{0,16},{8,24},{16,0},{24,8},{1,17},{9,25},{17,1},{25,9},{2,18},{10... | collective-permute-start | bytes 786440 | tf_op jit(solution)/shard_map/cond/branch_1_fun/ppermute | solution.py:18
  251.6 139.9 %collective-permute-start.39 = (bf16[256,1024]{1,0:T(8,128)(2,1)}, bf16[256,1024]{1,0:T(8,128)(2,1)}, u32[]{:S(2)}, u32[]{:S(2)}) collective-permute-start(bf16[256,1024]{1,0:T(8,128)(2,1)} %fusion.103), channel_id=1, source_target_pairs={{0,16},{8,24},{16,0},{24,8},{1,17},{9,25},{17,1},{25,9},{2,18},{10... | collective-permute-start | bytes 1572872 | tf_op jit(solution)/shard_map/cond/branch_1_fun/ppermute | solution.py:18
  258.5 166.8 %collective-permute-start.40 = (bf16[512,1024]{1,0:T(8,128)(2,1)}, bf16[512,1024]{1,0:T(8,128)(2,1)}, u32[]{:S(2)}, u32[]{:S(2)}) collective-permute-start(bf16[512,1024]{1,0:T(8,128)(2,1)} %fusion.80), channel_id=1, source_target_pairs={{0,16},{8,24},{16,0},{24,8},{1,17},{9,25},{17,1},{25,9},{2,18},{10... | collective-permute-start | bytes 3145736 | tf_op jit(solution)/shard_map/cond/branch_1_fun/ppermute | solution.py:18
  264.8 222.3 %collective-permute-start.41 = (bf16[896,1024]{1,0:T(8,128)(2,1)}, bf16[896,1024]{1,0:T(8,128)(2,1)}, u32[]{:S(2)}, u32[]{:S(2)}) collective-permute-start(bf16[896,1024]{1,0:T(8,128)(2,1)} %fusion.72), channel_id=1, source_target_pairs={{0,16},{8,24},{16,0},{24,8},{1,17},{9,25},{17,1},{25,9},{2,18},{10... | collective-permute-start | bytes 5505032 | tf_op jit(solution)/shard_map/cond/branch_1_fun/ppermute | solution.py:18
  295.0 203.2 %collective-permute-start.42 = (bf16[128,1024]{1,0:T(8,128)(2,1)S(1)}, bf16[128,1024]{1,0:T(8,128)(2,1)S(1)}, u32[]{:S(2)}, u32[]{:S(2)}) collective-permute-start(bf16[128,1024]{1,0:T(8,128)(2,1)S(1)} %copy-done.33), channel_id=1, source_target_pairs={{0,16},{8,24},{16,0},{24,8},{1,17},{9,25},{17,1},{25,9},{2,18},{10... | collective-permute-start | bytes 786440 | tf_op jit(solution)/shard_map/cond/branch_1_fun/ppermute | solution.py:18
  341.0 281.2 %collective-permute-start.45 = (bf16[896,1024]{1,0:T(8,128)(2,1)S(1)}, bf16[896,1024]{1,0:T(8,128)(2,1)S(1)}, u32[]{:S(2)}, u32[]{:S(2)}) collective-permute-start(bf16[896,1024]{1,0:T(8,128)(2,1)S(1)} %copy-done.7), channel_id=1, source_target_pairs={{0,16},{8,24},{16,0},{24,8},{1,17},{9,25},{17,1},{25,9},{2,18},{10... | collective-permute-start | bytes 5505032 | tf_op jit(solution)/shard_map/cond/branch_1_fun/ppermute | solution.py:18
  391.5 196.5 %collective-permute-start.43 = (bf16[256,1024]{1,0:T(8,128)(2,1)S(1)}, bf16[256,1024]{1,0:T(8,128)(2,1)S(1)}, u32[]{:S(2)}, u32[]{:S(2)}) collective-permute-start(bf16[256,1024]{1,0:T(8,128)(2,1)S(1)} %fusion.104), channel_id=1, source_target_pairs={{0,16},{8,24},{16,0},{24,8},{1,17},{9,25},{17,1},{25,9},{2,18},{10... | collective-permute-start | bytes 1572872 | tf_op jit(solution)/shard_map/cond/branch_1_fun/ppermute | solution.py:18
  425.2 196.5 %collective-permute-start.44 = (bf16[512,1024]{1,0:T(8,128)(2,1)S(1)}, bf16[512,1024]{1,0:T(8,128)(2,1)S(1)}, u32[]{:S(2)}, u32[]{:S(2)}) collective-permute-start(bf16[512,1024]{1,0:T(8,128)(2,1)S(1)} %fusion.79), channel_id=1, source_target_pairs={{0,16},{8,24},{16,0},{24,8},{1,17},{9,25},{17,1},{25,9},{2,18},{10... | collective-permute-start | bytes 3145736 | tf_op jit(solution)/shard_map/cond/branch_1_fun/ppermute | solution.py:18
  487.0 162.8 %collective-permute-start.46 = (bf16[128,1024]{1,0:T(8,128)(2,1)S(1)}, bf16[128,1024]{1,0:T(8,128)(2,1)S(1)}, u32[]{:S(2)}, u32[]{:S(2)}) collective-permute-start(bf16[128,1024]{1,0:T(8,128)(2,1)S(1)} %fusion.117), channel_id=1, source_target_pairs={{0,16},{8,24},{16,0},{24,8},{1,17},{9,25},{17,1},{25,9},{2,18},{10... | collective-permute-start | bytes 786440 | tf_op jit(solution)/shard_map/cond/branch_1_fun/ppermute | solution.py:18
  498.2 225.0 %collective-permute-start.49 = (bf16[896,1024]{1,0:T(8,128)(2,1)S(1)}, bf16[896,1024]{1,0:T(8,128)(2,1)S(1)}, u32[]{:S(2)}, u32[]{:S(2)}) collective-permute-start(bf16[896,1024]{1,0:T(8,128)(2,1)S(1)} %fusion.70), channel_id=1, source_target_pairs={{0,16},{8,24},{16,0},{24,8},{1,17},{9,25},{17,1},{25,9},{2,18},{10... | collective-permute-start | bytes 5505032 | tf_op jit(solution)/shard_map/cond/branch_1_fun/ppermute | solution.py:18
  588.0 112.4 %collective-permute-start.47 = (bf16[256,1024]{1,0:T(8,128)(2,1)S(1)}, bf16[256,1024]{1,0:T(8,128)(2,1)S(1)}, u32[]{:S(2)}, u32[]{:S(2)}) collective-permute-start(bf16[256,1024]{1,0:T(8,128)(2,1)S(1)} %fusion.105), channel_id=1, source_target_pairs={{0,16},{8,24},{16,0},{24,8},{1,17},{9,25},{17,1},{25,9},{2,18},{10... | collective-permute-start | bytes 1572872 | tf_op jit(solution)/shard_map/cond/branch_1_fun/ppermute | solution.py:18
  621.8 101.0 %collective-permute-start.48 = (bf16[512,1024]{1,0:T(8,128)(2,1)S(1)}, bf16[512,1024]{1,0:T(8,128)(2,1)S(1)}, u32[]{:S(2)}, u32[]{:S(2)}) collective-permute-start(bf16[512,1024]{1,0:T(8,128)(2,1)S(1)} %fusion.78), channel_id=1, source_target_pairs={{0,16},{8,24},{16,0},{24,8},{1,17},{9,25},{17,1},{25,9},{2,18},{10... | collective-permute-start | bytes 3145736 | tf_op jit(solution)/shard_map/cond/branch_1_fun/ppermute | solution.py:18
  (19 other events, 404.8 us)
Sparse Core Ops, SparseCore 0:
  9.9 32.1 all-gather.19
  55.8 32.4 all-gather.13
  90.2 38.7 all-gather.15
  130.8 29.3 all-gather.17

commit v7 on v2

--- a/solution.py
+++ b/solution.py
@@ -45,10 +45,11 @@
     paired = (2 * amount) % groups == 0
     w_minus = jnp.where(direct, back_share, front_share).astype(jnp.float32)
     w_plus = jnp.where(direct, front_share, back_share).astype(jnp.float32)
-    cots = [
-        lax.all_gather(cotangent[:, b * col_size:(b + 1) * col_size], "node", axis=0, tiled=True)
-        for b in range(n_cols)
-    ]
+    first = lax.all_gather(cotangent[:, :col_size], "node", axis=0, tiled=True)
+    cots = [first]
+    if n_cols > 1:
+        rest = lax.all_gather(cotangent[:, col_size:], "node", axis=0, tiled=True)
+        cots += [rest[:, (b - 1) * col_size:b * col_size] for b in range(1, n_cols)]
     mixed = jnp.zeros(params.shape[1:], jnp.bfloat16)
     sizes = row_sizes(rows_total)
     starts = [sum(sizes[:i]) for i in range(len(sizes))]

time: 742 us -> 762 us (1.027)
  waiting for transfers between devices: 527 us -> 596 us
  starting transfers between devices: 64.5 us -> 24.2 us
  matrix products: 59.3 us -> 48.6 us
    ppermute x34 -> x17, waiting for transfers between devices: 494 us -> 552 us  [shifted(): return lax.ppermute(value, axis, pairs)]
    ppermute x34 -> x17, starting transfers between devices: 52 us -> 11.8 us  [shifted(): return lax.ppermute(value, axis, pairs)]
    all_to_all x3, waiting for transfers between devices: 13.3 us -> 41.5 us  [pipeline(): lax.all_to_all(piece, 'node', split_axis=1, concat_axis=0, tiled=True)]
    all_gather x4 -> x2, waiting for transfers between devices: 18.3 us -> 2.7 us  [the longest x1 2.7 us: pipeline(): first = lax.all_gather(cotangent[:, :col_size], 'node', axis=0, tiled=True)]
    dot_general x16, matrix products: 59.3 us -> 48.6 us  [pipeline(): lax.dot_general(cols, cot, rows_by_tokens, preferred_element_type=jnp.flo...]
  transfers between devices with their start and end apart: 41 -> 22, of which waited for: 13 -> 18; matrix products, arithmetic and copies ran while one was open for 14% -> 13% of each run, Pallas kernels for 0% -> 0%
where the time goes in v7:
time: 762 us; the launch traced here: 752 us
  waiting for transfers between devices  596 us (78%)
  matrix products  48.6 us (6%)
  local copies, waits for them, and re-layouts  34.3 us (5%)
  starting transfers between devices  24.2 us (3%)
  other arithmetic  24.1 us (3%)
  between operations  18 us (2%)
    ppermute x17, waiting for transfers between devices, shifted(): return lax.ppermute(value, axis, pairs)  552 us
    dot_general x16, matrix products, pipeline(): lax.dot_general(cols, cot, rows_by_tokens, preferred_element_type=jnp.flo...  48.6 us
    all_to_all x3, waiting for transfers between devices, pipeline(): lax.all_to_all(piece, 'node', split_axis=1, concat_axis=0, tiled=True)  41.5 us
    dynamic_update_slice x15, other arithmetic, pipeline(): lax.dynamic_update_slice(mixed, total.astype(jnp.bfloat16), (start, b * c...  24 us
  transfers between devices with their start and end apart: 22, of which 18 were waited for; matrix products, arithmetic and copies ran while one was open for 13% of the time, Pallas kernels for 0%

profile of v7, /device:TPU:0, one launch (start us, length us, event | category | flops | bytes accessed | tf_op | source)
XLA Modules:
  0.0 751.8 jit_solution(3342555137326646142)
XLA Ops:
  11.0 732.5 %conditional.1 = (bf16[1,1792,4096]{2,1,0:T(8,128)(2,1)}, f32[1]{0:T(128)}) conditional(s32[]{:T(128)} %clamp.3, (bf16[1,1792,4096]{2,1,0:T(8,128)(2,1)}, f32[]{:T(128)}, bf16[1,1792,4096]{2,1,0:T(8,128)(2,1)}, bf16[1,128,14336]{2,1,0:T(8,128)(2,1)}, bf16[128,4096]{1,0:T(8,128)(2,1)}, /*index=5*/pred[]{:T(512)}, f32[1]{0:T(128)}) %tuple.79, ...), branch_computations={%region_0.1_spmd, %region_1.2_spmd} | conditional | flops 15157166080 | bytes 496242560 | solution.py:112
  19.1 6.1 copy.20
  27.2 5.2 all-to-all-start.3
  34.7 13.5 %all-to-all-done.3 = bf16[128,8,384]{0,2,1:T(8,128)(2,1)S(1)} async-done(((bf16[128,8,384]{0,2,1:T(8,128)(2,1)}), bf16[128,8,384]{0,2,1:T(8,128)(2,1)S(1)}, u32[]{:S(2)}, u32[]{:S(2)}) %all-to-all-start.3) | async-done | bytes 786464 | tf_op jit(solution)/shard_map/cond/branch_1_fun/all_to_all | solution.py:68
  63.2 20.6 %all-to-all-done.4 = bf16[128,8,512]{0,2,1:T(8,128)(2,1)S(1)} async-done(((bf16[128,8,512]{0,2,1:T(8,128)(2,1)}), bf16[128,8,512]{0,2,1:T(8,128)(2,1)S(1)}, u32[]{:S(2)}, u32[]{:S(2)}) %all-to-all-start.4) | async-done | bytes 1048608 | tf_op jit(solution)/shard_map/cond/branch_1_fun/all_to_all | solution.py:68
  85.1 5.0 fusion.90
  97.4 23.2 %collective-permute-done.34 = bf16[128,1024]{1,0:T(8,128)(2,1)S(1)} collective-permute-done((bf16[128,1024]{1,0:T(8,128)(2,1)S(1)}, bf16[128,1024]{1,0:T(8,128)(2,1)S(1)}, u32[]{:S(2)}, u32[]{:S(2)}) %collective-permute-start.34) | collective-permute-done | bytes 262176 | tf_op jit(solution)/shard_map/cond/branch_1_fun/ppermute | solution.py:18
  120.8 7.5 all-to-all-done.5
  131.3 5.9 fusion.82
  139.7 7.3 pad_bitcast_fusion.1
  147.1 46.7 %collective-permute-done.35 = bf16[256,1024]{1,0:T(8,128)(2,1)} collective-permute-done((bf16[256,1024]{1,0:T(8,128)(2,1)}, bf16[256,1024]{1,0:T(8,128)(2,1)}, u32[]{:S(2)}, u32[]{:S(2)}) %collective-permute-start.35) | collective-permute-done | bytes 524320 | tf_op jit(solution)/shard_map/cond/branch_1_fun/ppermute | solution.py:18
  195.8 20.4 %collective-permute-done.36 = bf16[512,1024]{1,0:T(8,128)(2,1)} collective-permute-done((bf16[512,1024]{1,0:T(8,128)(2,1)}, bf16[512,1024]{1,0:T(8,128)(2,1)}, u32[]{:S(2)}, u32[]{:S(2)}) %collective-permute-start.36) | collective-permute-done | bytes 1048608 | tf_op jit(solution)/shard_map/cond/branch_1_fun/ppermute | solution.py:18
  218.8 36.2 %collective-permute-done.50 = f32[1]{0:T(128)} collective-permute-done((f32[1]{0:T(128)}, f32[1]{0:T(128)}, u32[]{:S(2)}, u32[]{:S(2)}) %collective-permute-start.50) | collective-permute-done | bytes 36 | tf_op jit(solution)/shard_map/cond/branch_1_fun/ppermute | solution.py:18
  273.5 4.9 fusion.81
  302.3 57.1 %collective-permute-done.38 = bf16[128,1024]{1,0:T(8,128)(2,1)S(1)} collective-permute-done((bf16[128,1024]{1,0:T(8,128)(2,1)S(1)}, bf16[128,1024]{1,0:T(8,128)(2,1)S(1)}, u32[]{:S(2)}, u32[]{:S(2)}) %collective-permute-start.38) | collective-permute-done | bytes 262176 | tf_op jit(solution)/shard_map/cond/branch_1_fun/ppermute | solution.py:18
  360.2 49.8 %collective-permute-done.39 = bf16[256,1024]{1,0:T(8,128)(2,1)S(1)} collective-permute-done((bf16[256,1024]{1,0:T(8,128)(2,1)S(1)}, bf16[256,1024]{1,0:T(8,128)(2,1)S(1)}, u32[]{:S(2)}, u32[]{:S(2)}) %collective-permute-start.39) | collective-permute-done | bytes 524320 | tf_op jit(solution)/shard_map/cond/branch_1_fun/ppermute | solution.py:18
  411.0 32.7 %collective-permute-done.40 = bf16[512,1024]{1,0:T(8,128)(2,1)S(1)} collective-permute-done((bf16[512,1024]{1,0:T(8,128)(2,1)S(1)}, bf16[512,1024]{1,0:T(8,128)(2,1)S(1)}, u32[]{:S(2)}, u32[]{:S(2)}) %collective-permute-start.40) | collective-permute-done | bytes 1048608 | tf_op jit(solution)/shard_map/cond/branch_1_fun/ppermute | solution.py:18
  445.1 60.4 %collective-permute-done.41 = bf16[896,1024]{1,0:T(8,128)(2,1)S(1)} collective-permute-done((bf16[896,1024]{1,0:T(8,128)(2,1)S(1)}, bf16[896,1024]{1,0:T(8,128)(2,1)S(1)}, u32[]{:S(2)}, u32[]{:S(2)}) %collective-permute-start.41) | collective-permute-done | bytes 1835040 | tf_op jit(solution)/shard_map/cond/branch_1_fun/ppermute | solution.py:18
  507.6 9.1 %collective-permute-done.42 = bf16[128,1024]{1,0:T(8,128)(2,1)S(1)} collective-permute-done((bf16[128,1024]{1,0:T(8,128)(2,1)S(1)}, bf16[128,1024]{1,0:T(8,128)(2,1)S(1)}, u32[]{:S(2)}, u32[]{:S(2)}) %collective-permute-start.42) | collective-permute-done | bytes 262176 | tf_op jit(solution)/shard_map/cond/branch_1_fun/ppermute | solution.py:18
  517.5 89.1 %collective-permute-done.43 = bf16[256,1024]{1,0:T(8,128)(2,1)S(1)} collective-permute-done((bf16[256,1024]{1,0:T(8,128)(2,1)S(1)}, bf16[256,1024]{1,0:T(8,128)(2,1)S(1)}, u32[]{:S(2)}, u32[]{:S(2)}) %collective-permute-start.43) | collective-permute-done | bytes 524320 | tf_op jit(solution)/shard_map/cond/branch_1_fun/ppermute | solution.py:18
  607.6 32.7 %collective-permute-done.44 = bf16[512,1024]{1,0:T(8,128)(2,1)S(1)} collective-permute-done((bf16[512,1024]{1,0:T(8,128)(2,1)S(1)}, bf16[512,1024]{1,0:T(8,128)(2,1)S(1)}, u32[]{:S(2)}, u32[]{:S(2)}) %collective-permute-start.44) | collective-permute-done | bytes 1048608 | tf_op jit(solution)/shard_map/cond/branch_1_fun/ppermute | solution.py:18
  643.8 24.6 %collective-permute-done.46 = bf16[128,1024]{1,0:T(8,128)(2,1)S(1)} collective-permute-done((bf16[128,1024]{1,0:T(8,128)(2,1)S(1)}, bf16[128,1024]{1,0:T(8,128)(2,1)S(1)}, u32[]{:S(2)}, u32[]{:S(2)}) %collective-permute-start.46) | collective-permute-done | bytes 262176 | tf_op jit(solution)/shard_map/cond/branch_1_fun/ppermute | solution.py:18
  669.2 49.8 %collective-permute-done.47 = bf16[256,1024]{1,0:T(8,128)(2,1)S(1)} collective-permute-done((bf16[256,1024]{1,0:T(8,128)(2,1)S(1)}, bf16[256,1024]{1,0:T(8,128)(2,1)S(1)}, u32[]{:S(2)}, u32[]{:S(2)}) %collective-permute-start.47) | collective-permute-done | bytes 524320 | tf_op jit(solution)/shard_map/cond/branch_1_fun/ppermute | solution.py:18
  719.9 19.9 %collective-permute-done.48 = bf16[512,1024]{1,0:T(8,128)(2,1)S(1)} collective-permute-done((bf16[512,1024]{1,0:T(8,128)(2,1)S(1)}, bf16[512,1024]{1,0:T(8,128)(2,1)S(1)}, u32[]{:S(2)}, u32[]{:S(2)}) %collective-permute-start.48) | collective-permute-done | bytes 1048608 | tf_op jit(solution)/shard_map/cond/branch_1_fun/ppermute | solution.py:18
  (92 shorter events, 99.6 us)
Async XLA Ops:
  15.2 36.2 %all-gather.9.cloned.1.call-start = ((), (), s32[]{:S(2)}) async-start(), calls=%async_computation.8 | async-start | bytes 2359296 | tf_op jit(solution)/shard_map/cond/branch_1_fun/all_gather | solution.py:48
  16.9 242.9 %all-gather.11.cloned.1.call-start = ((), (), s32[]{:S(2)}) async-start(), calls=%async_computation.9 | async-start | bytes 7077888 | tf_op jit(solution)/shard_map/cond/branch_1_fun/all_gather | solution.py:51
  27.2 21.0 %all-to-all-start.3 = ((bf16[128,8,384]{0,2,1:T(8,128)(2,1)}), bf16[128,8,384]{0,2,1:T(8,128)(2,1)S(1)}, u32[]{:S(2)}, u32[]{:S(2)}) async-start(bf16[128,8,384]{0,2,1:T(8,128)(2,1)} %slice.260), calls=%async_computation.3 | async-start | bytes 1572864 | tf_op jit(solution)/shard_map/cond/branch_1_fun/all_to_all | solution.py:68
  56.5 27.3 %all-to-all-start.4 = ((bf16[128,8,512]{0,2,1:T(8,128)(2,1)}), bf16[128,8,512]{0,2,1:T(8,128)(2,1)S(1)}, u32[]{:S(2)}, u32[]{:S(2)}) async-start(bf16[128,8,512]{0,2,1:T(8,128)(2,1)} %slice.263), calls=%async_computation.4 | async-start | bytes 2097152 | tf_op jit(solution)/shard_map/cond/branch_1_fun/all_to_all | solution.py:68
  90.1 38.2 %all-to-all-start.5 = ((bf16[128,8,896]{0,2,1:T(8,128)(2,1)}), bf16[128,8,896]{0,2,1:T(8,128)(2,1)S(1)}, u32[]{:S(2)}, u32[]{:S(2)}) async-start(bf16[128,8,896]{0,2,1:T(8,128)(2,1)} %slice.264), calls=%async_computation.5 | async-start | bytes 3670016 | tf_op jit(solution)/shard_map/cond/branch_1_fun/all_to_all | solution.py:68
  93.7 26.9 %collective-permute-start.34 = (bf16[128,1024]{1,0:T(8,128)(2,1)S(1)}, bf16[128,1024]{1,0:T(8,128)(2,1)S(1)}, u32[]{:S(2)}, u32[]{:S(2)}) collective-permute-start(bf16[128,1024]{1,0:T(8,128)(2,1)S(1)} %fusion.131), channel_id=1, source_target_pairs={{0,16},{8,24},{16,0},{24,8},{1,17},{9,25},{17,1},{25,9},{2,18},{10... | collective-permute-start | bytes 786440 | tf_op jit(solution)/shard_map/cond/branch_1_fun/ppermute | solution.py:18
  97.0 96.7 %collective-permute-start.35 = (bf16[256,1024]{1,0:T(8,128)(2,1)}, bf16[256,1024]{1,0:T(8,128)(2,1)}, u32[]{:S(2)}, u32[]{:S(2)}) collective-permute-start(bf16[256,1024]{1,0:T(8,128)(2,1)} %fusion.115), channel_id=1, source_target_pairs={{0,16},{8,24},{16,0},{24,8},{1,17},{9,25},{17,1},{25,9},{2,18},{10... | collective-permute-start | bytes 1572872 | tf_op jit(solution)/shard_map/cond/branch_1_fun/ppermute | solution.py:18
  120.7 95.5 %collective-permute-start.36 = (bf16[512,1024]{1,0:T(8,128)(2,1)}, bf16[512,1024]{1,0:T(8,128)(2,1)}, u32[]{:S(2)}, u32[]{:S(2)}) collective-permute-start(bf16[512,1024]{1,0:T(8,128)(2,1)} %fusion.90), channel_id=1, source_target_pairs={{0,16},{8,24},{16,0},{24,8},{1,17},{9,25},{17,1},{25,9},{2,18},{10... | collective-permute-start | bytes 3145736 | tf_op jit(solution)/shard_map/cond/branch_1_fun/ppermute | solution.py:18
  137.2 56.5 %copy-start.8 = (bf16[256,1024]{1,0:T(8,128)(2,1)S(1)}, bf16[256,1024]{1,0:T(8,128)(2,1)}, u32[]{:S(2)}) copy-start(bf16[256,1024]{1,0:T(8,128)(2,1)} %fusion.115) | copy-start | bytes 1572868 | tf_op jit(solution)/shard_map/cond
  137.3 118.9 %collective-permute-start.37 = (bf16[896,1024]{1,0:T(8,128)(2,1)S(1)}, bf16[896,1024]{1,0:T(8,128)(2,1)}, u32[]{:S(2)}, u32[]{:S(2)}) collective-permute-start(bf16[896,1024]{1,0:T(8,128)(2,1)S(1)} %fusion.82), channel_id=1, source_target_pairs={{0,16},{8,24},{16,0},{24,8},{1,17},{9,25},{17,1},{25,9},{2,18},{10... | collective-permute-start | bytes 5505032 | tf_op jit(solution)/shard_map/cond/branch_1_fun/ppermute | solution.py:18
  147.1 69.2 %copy-start.5 = (bf16[512,1024]{1,0:T(8,128)(2,1)S(1)}, bf16[512,1024]{1,0:T(8,128)(2,1)}, u32[]{:S(2)}) copy-start(bf16[512,1024]{1,0:T(8,128)(2,1)} %fusion.90) | copy-start | bytes 3145732 | tf_op jit(solution)/shard_map/cond
  218.8 36.2 %collective-permute-start.50 = (f32[1]{0:T(128)}, f32[1]{0:T(128)}, u32[]{:S(2)}, u32[]{:S(2)}) collective-permute-start(f32[1]{0:T(128)} %get-tuple-element.107), channel_id=1, source_target_pairs={{0,16},{8,24},{16,0},{24,8},{1,17},{9,25},{17,1},{25,9},{2,18},{10... | collective-permute-start | bytes 20 | tf_op jit(solution)/shard_map/cond/branch_1_fun/ppermute | solution.py:18
  265.0 94.4 %collective-permute-start.38 = (bf16[128,1024]{1,0:T(8,128)(2,1)S(1)}, bf16[128,1024]{1,0:T(8,128)(2,1)S(1)}, u32[]{:S(2)}, u32[]{:S(2)}) collective-permute-start(bf16[128,1024]{1,0:T(8,128)(2,1)S(1)} %fusion.132), channel_id=1, source_target_pairs={{0,16},{8,24},{16,0},{24,8},{1,17},{9,25},{17,1},{25,9},{2,18},{10... | collective-permute-start | bytes 786440 | tf_op jit(solution)/shard_map/cond/branch_1_fun/ppermute | solution.py:18
  267.2 142.8 %collective-permute-start.39 = (bf16[256,1024]{1,0:T(8,128)(2,1)S(1)}, bf16[256,1024]{1,0:T(8,128)(2,1)S(1)}, u32[]{:S(2)}, u32[]{:S(2)}) collective-permute-start(bf16[256,1024]{1,0:T(8,128)(2,1)S(1)} %fusion.116), channel_id=1, source_target_pairs={{0,16},{8,24},{16,0},{24,8},{1,17},{9,25},{17,1},{25,9},{2,18},{10... | collective-permute-start | bytes 1572872 | tf_op jit(solution)/shard_map/cond/branch_1_fun/ppermute | solution.py:18
  273.3 170.4 %collective-permute-start.40 = (bf16[512,1024]{1,0:T(8,128)(2,1)S(1)}, bf16[512,1024]{1,0:T(8,128)(2,1)S(1)}, u32[]{:S(2)}, u32[]{:S(2)}) collective-permute-start(bf16[512,1024]{1,0:T(8,128)(2,1)S(1)} %fusion.89), channel_id=1, source_target_pairs={{0,16},{8,24},{16,0},{24,8},{1,17},{9,25},{17,1},{25,9},{2,18},{10... | collective-permute-start | bytes 3145736 | tf_op jit(solution)/shard_map/cond/branch_1_fun/ppermute | solution.py:18
  278.4 227.1 %collective-permute-start.41 = (bf16[896,1024]{1,0:T(8,128)(2,1)S(1)}, bf16[896,1024]{1,0:T(8,128)(2,1)S(1)}, u32[]{:S(2)}, u32[]{:S(2)}) collective-permute-start(bf16[896,1024]{1,0:T(8,128)(2,1)S(1)} %fusion.81), channel_id=1, source_target_pairs={{0,16},{8,24},{16,0},{24,8},{1,17},{9,25},{17,1},{25,9},{2,18},{10... | collective-permute-start | bytes 5505032 | tf_op jit(solution)/shard_map/cond/branch_1_fun/ppermute | solution.py:18
  282.6 234.1 %collective-permute-start.42 = (bf16[128,1024]{1,0:T(8,128)(2,1)S(1)}, bf16[128,1024]{1,0:T(8,128)(2,1)S(1)}, u32[]{:S(2)}, u32[]{:S(2)}) collective-permute-start(bf16[128,1024]{1,0:T(8,128)(2,1)S(1)} %fusion.133), channel_id=1, source_target_pairs={{0,16},{8,24},{16,0},{24,8},{1,17},{9,25},{17,1},{25,9},{2,18},{10... | collective-permute-start | bytes 786440 | tf_op jit(solution)/shard_map/cond/branch_1_fun/ppermute | solution.py:18
  359.4 282.3 %collective-permute-start.45 = (bf16[896,1024]{1,0:T(8,128)(2,1)S(1)}, bf16[896,1024]{1,0:T(8,128)(2,1)S(1)}, u32[]{:S(2)}, u32[]{:S(2)}) collective-permute-start(bf16[896,1024]{1,0:T(8,128)(2,1)S(1)} %fusion.80), channel_id=1, source_target_pairs={{0,16},{8,24},{16,0},{24,8},{1,17},{9,25},{17,1},{25,9},{2,18},{10... | collective-permute-start | bytes 5505032 | tf_op jit(solution)/shard_map/cond/branch_1_fun/ppermute | solution.py:18
  410.0 196.6 %collective-permute-start.43 = (bf16[256,1024]{1,0:T(8,128)(2,1)S(1)}, bf16[256,1024]{1,0:T(8,128)(2,1)S(1)}, u32[]{:S(2)}, u32[]{:S(2)}) collective-permute-start(bf16[256,1024]{1,0:T(8,128)(2,1)S(1)} %fusion.117), channel_id=1, source_target_pairs={{0,16},{8,24},{16,0},{24,8},{1,17},{9,25},{17,1},{25,9},{2,18},{10... | collective-permute-start | bytes 1572872 | tf_op jit(solution)/shard_map/cond/branch_1_fun/ppermute | solution.py:18
  443.7 196.6 %collective-permute-start.44 = (bf16[512,1024]{1,0:T(8,128)(2,1)S(1)}, bf16[512,1024]{1,0:T(8,128)(2,1)S(1)}, u32[]{:S(2)}, u32[]{:S(2)}) collective-permute-start(bf16[512,1024]{1,0:T(8,128)(2,1)S(1)} %fusion.88), channel_id=1, source_target_pairs={{0,16},{8,24},{16,0},{24,8},{1,17},{9,25},{17,1},{25,9},{2,18},{10... | collective-permute-start | bytes 3145736 | tf_op jit(solution)/shard_map/cond/branch_1_fun/ppermute | solution.py:18
  505.5 162.9 %collective-permute-start.46 = (bf16[128,1024]{1,0:T(8,128)(2,1)S(1)}, bf16[128,1024]{1,0:T(8,128)(2,1)S(1)}, u32[]{:S(2)}, u32[]{:S(2)}) collective-permute-start(bf16[128,1024]{1,0:T(8,128)(2,1)S(1)} %fusion.134), channel_id=1, source_target_pairs={{0,16},{8,24},{16,0},{24,8},{1,17},{9,25},{17,1},{25,9},{2,18},{10... | collective-permute-start | bytes 786440 | tf_op jit(solution)/shard_map/cond/branch_1_fun/ppermute | solution.py:18
  516.7 224.6 %collective-permute-start.49 = (bf16[896,1024]{1,0:T(8,128)(2,1)S(1)}, bf16[896,1024]{1,0:T(8,128)(2,1)S(1)}, u32[]{:S(2)}, u32[]{:S(2)}) collective-permute-start(bf16[896,1024]{1,0:T(8,128)(2,1)S(1)} %fusion.79), channel_id=1, source_target_pairs={{0,16},{8,24},{16,0},{24,8},{1,17},{9,25},{17,1},{25,9},{2,18},{10... | collective-permute-start | bytes 5505032 | tf_op jit(solution)/shard_map/cond/branch_1_fun/ppermute | solution.py:18
  606.6 112.4 %collective-permute-start.47 = (bf16[256,1024]{1,0:T(8,128)(2,1)S(1)}, bf16[256,1024]{1,0:T(8,128)(2,1)S(1)}, u32[]{:S(2)}, u32[]{:S(2)}) collective-permute-start(bf16[256,1024]{1,0:T(8,128)(2,1)S(1)} %fusion.118), channel_id=1, source_target_pairs={{0,16},{8,24},{16,0},{24,8},{1,17},{9,25},{17,1},{25,9},{2,18},{10... | collective-permute-start | bytes 1572872 | tf_op jit(solution)/shard_map/cond/branch_1_fun/ppermute | solution.py:18
  640.3 99.6 %collective-permute-start.48 = (bf16[512,1024]{1,0:T(8,128)(2,1)S(1)}, bf16[512,1024]{1,0:T(8,128)(2,1)S(1)}, u32[]{:S(2)}, u32[]{:S(2)}) collective-permute-start(bf16[512,1024]{1,0:T(8,128)(2,1)S(1)} %fusion.87), channel_id=1, source_target_pairs={{0,16},{8,24},{16,0},{24,8},{1,17},{9,25},{17,1},{25,9},{2,18},{10... | collective-permute-start | bytes 3145736 | tf_op jit(solution)/shard_map/cond/branch_1_fun/ppermute | solution.py:18
  (9 other events, 61.3 us)
Sparse Core Ops, SparseCore 0:
  17.9 33.3 all-gather.8
  53.2 71.0 all-gather.10

commit v8 on v2

--- a/solution.py
+++ b/solution.py
@@ -57,7 +57,11 @@
     last = None
     for b in range(n_cols):
         span = slice(b * col_size, (b + 1) * col_size)
-        for a, (start, size) in enumerate(zip(starts, sizes)):
+        order = list(range(len(sizes)))
+        if b == n_cols - 1 and b > 0:
+            order.reverse()
+        for a in order:
+            start, size = starts[a], sizes[a]
             if columns[a] is None:
                 members = [0, 1][:len(sizes)] if a == 0 else [a]
                 width_a = sum(sizes[m] for m in members)

time: 742 us -> 720 us (0.970)
  starting transfers between devices: 64.5 us -> 30.8 us
  other arithmetic: 18.7 us -> 29.3 us
  waiting for transfers between devices: 527 us -> 536 us
    ppermute x34 -> x17, starting transfers between devices: 52 us -> 18.3 us  [shifted(): return lax.ppermute(value, axis, pairs)]
    dynamic_update_slice x15, other arithmetic: 18.5 us -> 29.2 us  [pipeline(): lax.dynamic_update_slice(mixed, total.astype(jnp.bfloat16), (start, b * c...]
    ppermute x34 -> x17, waiting for transfers between devices: 494 us -> 498 us  [shifted(): return lax.ppermute(value, axis, pairs)]
  transfers between devices with their start and end apart: 41 -> 24, of which waited for: 13 -> 12; matrix products, arithmetic and copies ran while one was open for 14% -> 16% of each run, Pallas kernels for 0% -> 0%
where the time goes in v8:
time: 720 us; the launch traced here: 712 us
  waiting for transfers between devices  536 us (74%)
  matrix products  60.1 us (8%)
  starting transfers between devices  30.8 us (4%)
  other arithmetic  29.3 us (4%)
  local copies, waits for them, and re-layouts  28.7 us (4%)
  between operations  17.7 us (2%)
  loops' own time  9.5 us (1%)
    ppermute x17, waiting for transfers between devices, shifted(): return lax.ppermute(value, axis, pairs)  498 us
    dot_general x16, matrix products, pipeline(): lax.dot_general(cols, cot, rows_by_tokens, preferred_element_type=jnp.flo...  60.1 us
    dynamic_update_slice x15, other arithmetic, pipeline(): lax.dynamic_update_slice(mixed, total.astype(jnp.bfloat16), (start, b * c...  29.2 us
    all_gather x4, waiting for transfers between devices, pipeline(): lax.all_gather(cotangent[:, b * col_size:(b + 1) * col_size], 'node', axi...  22.6 us
    ppermute x17, starting transfers between devices, shifted(): return lax.ppermute(value, axis, pairs)  18.3 us
  transfers between devices with their start and end apart: 24, of which 12 were waited for; matrix products, arithmetic and copies ran while one was open for 16% of the time, Pallas kernels for 0%

profile of v8, /device:TPU:0, one launch (start us, length us, event | category | flops | bytes accessed | tf_op | source)
XLA Modules:
  0.0 712.2 jit_solution(10549584293138926459)
XLA Ops:
  11.0 693.3 %conditional.1 = (bf16[1,1792,4096]{2,1,0:T(8,128)(2,1)}, f32[1]{0:T(128)}) conditional(s32[]{:T(128)} %clamp.3, (bf16[1,1792,4096]{2,1,0:T(8,128)(2,1)}, f32[]{:T(128)}, bf16[1,1792,4096]{2,1,0:T(8,128)(2,1)}, bf16[1,128,14336]{2,1,0:T(8,128)(2,1)}, bf16[128,4096]{1,0:T(8,128)(2,1)}, /*index=5*/pred[]{:T(512)}, f32[1]{0:T(128)}) %tuple.89, ...), branch_computations={%region_0.1_spmd, %region_1.2_spmd} | conditional | flops 15157166080 | bytes 445924416 | solution.py:115
  21.8 6.1 copy.20
  29.9 5.2 all-to-all-start.3
  37.4 13.3 %all-to-all-done.3 = bf16[128,8,384]{0,2,1:T(8,128)(2,1)S(1)} async-done(((bf16[128,8,384]{0,2,1:T(8,128)(2,1)}), bf16[128,8,384]{0,2,1:T(8,128)(2,1)S(1)}, u32[]{:S(2)}, u32[]{:S(2)}) %all-to-all-start.3) | async-done | bytes 786464 | tf_op jit(solution)/shard_map/cond/branch_1_fun/all_to_all | solution.py:71
  59.2 3.6 all-to-all-start.4
  70.0 19.7 %all-gather.19.cloned.1.call-done = bf16[1024,1024]{1,0:T(8,128)(2,1)} async-done(((bf16[128,1024]{1,0:T(8,128)(2,1)}), bf16[1024,1024]{1,0:T(8,128)(2,1)}) %all-gather.19.cloned.1.call-update) | async-done | bytes 2097168 | tf_op jit(solution)/shard_map/cond/branch_1_fun/all_gather | solution.py:49
  99.4 4.0 fusion.90
  104.1 3.6 all-to-all-start.5
  107.7 7.3 %pad_bitcast_fusion.1 = bf16[1,1792,4096]{2,1,0:T(8,128)(2,1)} fusion(bf16[128,1024]{1,0:T(8,128)(2,1)S(1)} %multiply_convert_fusion.15), kind=kLoop, calls=%fused_computation.120 | loop fusion | bytes 14942208 | tf_op jit(solution)/shard_map/cond/branch_1_fun/broadcast_in_dim | solution.py:100
  115.1 18.3 %collective-permute-done.35 = bf16[256,1024]{1,0:T(8,128)(2,1)} collective-permute-done((bf16[256,1024]{1,0:T(8,128)(2,1)}, bf16[256,1024]{1,0:T(8,128)(2,1)}, u32[]{:S(2)}, u32[]{:S(2)}) %collective-permute-start.35) | collective-permute-done | bytes 524320 | tf_op jit(solution)/shard_map/cond/branch_1_fun/ppermute | solution.py:18
  135.6 5.0 fusion.89
  140.5 43.4 %collective-permute-done.36 = bf16[512,1024]{1,0:T(8,128)(2,1)} collective-permute-done((bf16[512,1024]{1,0:T(8,128)(2,1)S(1)}, bf16[512,1024]{1,0:T(8,128)(2,1)}, u32[]{:S(2)}, u32[]{:S(2)}) %collective-permute-start.36) | collective-permute-done | bytes 1048608 | tf_op jit(solution)/shard_map/cond/branch_1_fun/ppermute | solution.py:18
  189.3 7.3 %fusion.82 = bf16[896,1024]{1,0:T(8,128)(2,1)} fusion(bf16[896,1024]{0,1:T(8,128)(2,1)} %bitcast.483, bf16[1024,1024]{1,0:T(8,128)(2,1)} %all-gather.17.cloned.1.call-done, bf16[1,1792,4096]{2,1,0:T(8,128)(2,1)} %get-tuple-element.70, f32[]{:T(128)} %get-tuple-element.69, bf16[1,1792,4096]{2,1,0:T(8,128)(2,1)} %get-tuple-element.68), kind=kOutput, calls=%fused_computation.128 | convolution fusion | flops 1886388224 | bytes 9437188 | tf_op jit(solution)/shard_map/cond/branch_1_fun/dot_general | solution.py:82
  196.6 6.1 fusion.81
  214.0 6.0 fusion.80
  220.0 5.7 fusion.79
  232.7 130.4 %collective-permute-done.50 = f32[1]{0:T(128)} collective-permute-done((f32[1]{0:T(128)}, f32[1]{0:T(128)}, u32[]{:S(2)}, u32[]{:S(2)}) %collective-permute-start.50) | collective-permute-done | bytes 36 | tf_op jit(solution)/shard_map/cond/branch_1_fun/ppermute | solution.py:18
  367.5 4.1 fusion.96
  373.5 61.6 %collective-permute-done.39 = bf16[256,1024]{1,0:T(8,128)(2,1)S(1)} collective-permute-done((bf16[256,1024]{1,0:T(8,128)(2,1)S(1)}, bf16[256,1024]{1,0:T(8,128)(2,1)S(1)}, u32[]{:S(2)}, u32[]{:S(2)}) %collective-permute-start.39) | collective-permute-done | bytes 524320 | tf_op jit(solution)/shard_map/cond/branch_1_fun/ppermute | solution.py:18
  441.9 4.1 fusion.98
  446.0 67.7 %collective-permute-done.42 = bf16[128,1024]{1,0:T(8,128)(2,1)S(1)} collective-permute-done((bf16[128,1024]{1,0:T(8,128)(2,1)S(1)}, bf16[128,1024]{1,0:T(8,128)(2,1)S(1)}, u32[]{:S(2)}, u32[]{:S(2)}) %collective-permute-start.42) | collective-permute-done | bytes 262176 | tf_op jit(solution)/shard_map/cond/branch_1_fun/ppermute | solution.py:18
  514.5 134.0 %collective-permute-done.43 = bf16[256,1024]{1,0:T(8,128)(2,1)S(1)} collective-permute-done((bf16[256,1024]{1,0:T(8,128)(2,1)S(1)}, bf16[256,1024]{1,0:T(8,128)(2,1)S(1)}, u32[]{:S(2)}, u32[]{:S(2)}) %collective-permute-start.43) | collective-permute-done | bytes 524320 | tf_op jit(solution)/shard_map/cond/branch_1_fun/ppermute | solution.py:18
  658.1 29.8 %collective-permute-done.47 = bf16[512,1024]{1,0:T(8,128)(2,1)S(1)} collective-permute-done((bf16[512,1024]{1,0:T(8,128)(2,1)S(1)}, bf16[512,1024]{1,0:T(8,128)(2,1)S(1)}, u32[]{:S(2)}, u32[]{:S(2)}) %collective-permute-start.47) | collective-permute-done | bytes 1048608 | tf_op jit(solution)/shard_map/cond/branch_1_fun/ppermute | solution.py:18
  689.3 9.9 %collective-permute-done.48 = bf16[256,1024]{1,0:T(8,128)(2,1)S(1)} collective-permute-done((bf16[256,1024]{1,0:T(8,128)(2,1)S(1)}, bf16[256,1024]{1,0:T(8,128)(2,1)S(1)}, u32[]{:S(2)}, u32[]{:S(2)}) %collective-permute-start.48) | collective-permute-done | bytes 524320 | tf_op jit(solution)/shard_map/cond/branch_1_fun/ppermute | solution.py:18
  (101 shorter events, 89.0 us)
Async XLA Ops:
  18.1 36.0 %all-gather.17.cloned.1.call-start = ((), (), s32[]{:S(2)}) async-start(), calls=%async_computation.10 | async-start | bytes 2359296 | tf_op jit(solution)/shard_map/cond/branch_1_fun/all_gather | solution.py:49
  20.3 69.3 %all-gather.19.cloned.1.call-start = ((), (), s32[]{:S(2)}) async-start(), calls=%async_computation.11 | async-start | bytes 2359296 | tf_op jit(solution)/shard_map/cond/branch_1_fun/all_gather | solution.py:49
  21.1 184.6 %all-gather.21.cloned.1.call-start = ((), (), s32[]{:S(2)}) async-start(), calls=%async_computation.12 | async-start | bytes 2359296 | tf_op jit(solution)/shard_map/cond/branch_1_fun/all_gather | solution.py:49
  29.9 20.8 %all-to-all-start.3 = ((bf16[128,8,384]{0,2,1:T(8,128)(2,1)}), bf16[128,8,384]{0,2,1:T(8,128)(2,1)S(1)}, u32[]{:S(2)}, u32[]{:S(2)}) async-start(bf16[128,8,384]{0,2,1:T(8,128)(2,1)} %slice.251), calls=%async_computation.3 | async-start | bytes 1572864 | tf_op jit(solution)/shard_map/cond/branch_1_fun/all_to_all | solution.py:71
  59.2 38.9 %all-to-all-start.4 = ((bf16[128,8,512]{0,2,1:T(8,128)(2,1)}), bf16[128,8,512]{0,2,1:T(8,128)(2,1)S(1)}, u32[]{:S(2)}, u32[]{:S(2)}) async-start(bf16[128,8,512]{0,2,1:T(8,128)(2,1)} %slice.254), calls=%async_computation.4 | async-start | bytes 2097152 | tf_op jit(solution)/shard_map/cond/branch_1_fun/all_to_all | solution.py:71
  62.8 157.2 %all-gather.23.cloned.1.call-start = ((), (), s32[]{:S(2)}) async-start(), calls=%async_computation.13 | async-start | bytes 2359296 | tf_op jit(solution)/shard_map/cond/branch_1_fun/all_gather | solution.py:49
  67.0 31.0 %collective-permute-start.34 = (bf16[128,1024]{1,0:T(8,128)(2,1)S(1)}, bf16[128,1024]{1,0:T(8,128)(2,1)S(1)}, u32[]{:S(2)}, u32[]{:S(2)}) collective-permute-start(bf16[128,1024]{1,0:T(8,128)(2,1)S(1)} %fusion.131), channel_id=1, source_target_pairs={{0,16},{8,24},{16,0},{24,8},{1,17},{9,25},{17,1},{25,9},{2,18},{10... | collective-permute-start | bytes 786440 | tf_op jit(solution)/shard_map/cond/branch_1_fun/ppermute | solution.py:18
  69.6 63.8 %collective-permute-start.35 = (bf16[256,1024]{1,0:T(8,128)(2,1)}, bf16[256,1024]{1,0:T(8,128)(2,1)}, u32[]{:S(2)}, u32[]{:S(2)}) collective-permute-start(bf16[256,1024]{1,0:T(8,128)(2,1)} %fusion.115), channel_id=1, source_target_pairs={{0,16},{8,24},{16,0},{24,8},{1,17},{9,25},{17,1},{25,9},{2,18},{10... | collective-permute-start | bytes 1572872 | tf_op jit(solution)/shard_map/cond/branch_1_fun/ppermute | solution.py:18
  92.7 278.8 %collective-permute-start.38 = (bf16[128,1024]{1,0:T(8,128)(2,1)}, bf16[128,1024]{1,0:T(8,128)(2,1)}, u32[]{:S(2)}, u32[]{:S(2)}) collective-permute-start(bf16[128,1024]{1,0:T(8,128)(2,1)} %fusion.132), channel_id=1, source_target_pairs={{0,16},{8,24},{16,0},{24,8},{1,17},{9,25},{17,1},{25,9},{2,18},{10... | collective-permute-start | bytes 786440 | tf_op jit(solution)/shard_map/cond/branch_1_fun/ppermute | solution.py:18
  103.4 80.5 %collective-permute-start.36 = (bf16[512,1024]{1,0:T(8,128)(2,1)S(1)}, bf16[512,1024]{1,0:T(8,128)(2,1)}, u32[]{:S(2)}, u32[]{:S(2)}) collective-permute-start(bf16[512,1024]{1,0:T(8,128)(2,1)S(1)} %fusion.90), channel_id=1, source_target_pairs={{0,16},{8,24},{16,0},{24,8},{1,17},{9,25},{17,1},{25,9},{2,18},{10... | collective-permute-start | bytes 3145736 | tf_op jit(solution)/shard_map/cond/branch_1_fun/ppermute | solution.py:18
  104.1 82.4 %all-to-all-start.5 = ((bf16[128,8,896]{0,2,1:T(8,128)(2,1)}), bf16[128,8,896]{0,2,1:T(8,128)(2,1)S(1)}, u32[]{:S(2)}, u32[]{:S(2)}) async-start(bf16[128,8,896]{0,2,1:T(8,128)(2,1)} %slice.255), calls=%async_computation.5 | async-start | bytes 3670016 | tf_op jit(solution)/shard_map/cond/branch_1_fun/all_to_all | solution.py:71
  140.5 295.6 %collective-permute-start.40 = (bf16[512,1024]{1,0:T(8,128)(2,1)}, bf16[512,1024]{1,0:T(8,128)(2,1)}, u32[]{:S(2)}, u32[]{:S(2)}) collective-permute-start(bf16[512,1024]{1,0:T(8,128)(2,1)} %fusion.89), channel_id=1, source_target_pairs={{0,16},{8,24},{16,0},{24,8},{1,17},{9,25},{17,1},{25,9},{2,18},{10... | collective-permute-start | bytes 3145736 | tf_op jit(solution)/shard_map/cond/branch_1_fun/ppermute | solution.py:18
  196.6 167.8 %collective-permute-start.37 = (bf16[896,1024]{1,0:T(8,128)(2,1)}, bf16[896,1024]{1,0:T(8,128)(2,1)}, u32[]{:S(2)}, u32[]{:S(2)}) collective-permute-start(bf16[896,1024]{1,0:T(8,128)(2,1)} %fusion.82), channel_id=1, source_target_pairs={{0,16},{8,24},{16,0},{24,8},{1,17},{9,25},{17,1},{25,9},{2,18},{10... | collective-permute-start | bytes 5505032 | tf_op jit(solution)/shard_map/cond/branch_1_fun/ppermute | solution.py:18
  202.7 239.2 %collective-permute-start.41 = (bf16[896,1024]{1,0:T(8,128)(2,1)}, bf16[896,1024]{1,0:T(8,128)(2,1)}, u32[]{:S(2)}, u32[]{:S(2)}) collective-permute-start(bf16[896,1024]{1,0:T(8,128)(2,1)} %fusion.81), channel_id=1, source_target_pairs={{0,16},{8,24},{16,0},{24,8},{1,17},{9,25},{17,1},{25,9},{2,18},{10... | collective-permute-start | bytes 5505032 | tf_op jit(solution)/shard_map/cond/branch_1_fun/ppermute | solution.py:18
  230.9 132.2 %collective-permute-start.50 = (f32[1]{0:T(128)}, f32[1]{0:T(128)}, u32[]{:S(2)}, u32[]{:S(2)}) collective-permute-start(f32[1]{0:T(128)} %get-tuple-element.107), channel_id=1, source_target_pairs={{0,16},{8,24},{16,0},{24,8},{1,17},{9,25},{17,1},{25,9},{2,18},{10... | collective-permute-start | bytes 20 | tf_op jit(solution)/shard_map/cond/branch_1_fun/ppermute | solution.py:18
  363.2 71.9 %collective-permute-start.39 = (bf16[256,1024]{1,0:T(8,128)(2,1)S(1)}, bf16[256,1024]{1,0:T(8,128)(2,1)S(1)}, u32[]{:S(2)}, u32[]{:S(2)}) collective-permute-start(bf16[256,1024]{1,0:T(8,128)(2,1)S(1)} %copy-done.22), channel_id=1, source_target_pairs={{0,16},{8,24},{16,0},{24,8},{1,17},{9,25},{17,1},{25,9},{2,18},{10... | collective-permute-start | bytes 1572872 | tf_op jit(solution)/shard_map/cond/branch_1_fun/ppermute | solution.py:18
  364.5 149.3 %collective-permute-start.42 = (bf16[128,1024]{1,0:T(8,128)(2,1)S(1)}, bf16[128,1024]{1,0:T(8,128)(2,1)S(1)}, u32[]{:S(2)}, u32[]{:S(2)}) collective-permute-start(bf16[128,1024]{1,0:T(8,128)(2,1)S(1)} %fusion.133), channel_id=1, source_target_pairs={{0,16},{8,24},{16,0},{24,8},{1,17},{9,25},{17,1},{25,9},{2,18},{10... | collective-permute-start | bytes 786440 | tf_op jit(solution)/shard_map/cond/branch_1_fun/ppermute | solution.py:18
  371.6 282.3 %collective-permute-start.45 = (bf16[896,1024]{1,0:T(8,128)(2,1)S(1)}, bf16[896,1024]{1,0:T(8,128)(2,1)S(1)}, u32[]{:S(2)}, u32[]{:S(2)}) collective-permute-start(bf16[896,1024]{1,0:T(8,128)(2,1)S(1)} %copy-done.15), channel_id=1, source_target_pairs={{0,16},{8,24},{16,0},{24,8},{1,17},{9,25},{17,1},{25,9},{2,18},{10... | collective-permute-start | bytes 5505032 | tf_op jit(solution)/shard_map/cond/branch_1_fun/ppermute | solution.py:18
  435.1 214.5 %collective-permute-start.44 = (bf16[512,1024]{1,0:T(8,128)(2,1)S(1)}, bf16[512,1024]{1,0:T(8,128)(2,1)S(1)}, u32[]{:S(2)}, u32[]{:S(2)}) collective-permute-start(bf16[512,1024]{1,0:T(8,128)(2,1)S(1)} %fusion.88), channel_id=1, source_target_pairs={{0,16},{8,24},{16,0},{24,8},{1,17},{9,25},{17,1},{25,9},{2,18},{10... | collective-permute-start | bytes 3145736 | tf_op jit(solution)/shard_map/cond/branch_1_fun/ppermute | solution.py:18
  436.1 219.9 %collective-permute-start.46 = (bf16[896,1024]{1,0:T(8,128)(2,1)S(1)}, bf16[896,1024]{1,0:T(8,128)(2,1)S(1)}, u32[]{:S(2)}, u32[]{:S(2)}) collective-permute-start(bf16[896,1024]{1,0:T(8,128)(2,1)S(1)} %fusion.79), channel_id=1, source_target_pairs={{0,16},{8,24},{16,0},{24,8},{1,17},{9,25},{17,1},{25,9},{2,18},{10... | collective-permute-start | bytes 5505032 | tf_op jit(solution)/shard_map/cond/branch_1_fun/ppermute | solution.py:18
  441.9 206.6 %collective-permute-start.43 = (bf16[256,1024]{1,0:T(8,128)(2,1)S(1)}, bf16[256,1024]{1,0:T(8,128)(2,1)S(1)}, u32[]{:S(2)}, u32[]{:S(2)}) collective-permute-start(bf16[256,1024]{1,0:T(8,128)(2,1)S(1)} %copy-done.23), channel_id=1, source_target_pairs={{0,16},{8,24},{16,0},{24,8},{1,17},{9,25},{17,1},{25,9},{2,18},{10... | collective-permute-start | bytes 1572872 | tf_op jit(solution)/shard_map/cond/branch_1_fun/ppermute | solution.py:18
  513.7 174.1 %collective-permute-start.47 = (bf16[512,1024]{1,0:T(8,128)(2,1)S(1)}, bf16[512,1024]{1,0:T(8,128)(2,1)S(1)}, u32[]{:S(2)}, u32[]{:S(2)}) collective-permute-start(bf16[512,1024]{1,0:T(8,128)(2,1)S(1)} %fusion.87), channel_id=1, source_target_pairs={{0,16},{8,24},{16,0},{24,8},{1,17},{9,25},{17,1},{25,9},{2,18},{10... | collective-permute-start | bytes 3145736 | tf_op jit(solution)/shard_map/cond/branch_1_fun/ppermute | solution.py:18
  648.6 50.6 %collective-permute-start.48 = (bf16[256,1024]{1,0:T(8,128)(2,1)S(1)}, bf16[256,1024]{1,0:T(8,128)(2,1)S(1)}, u32[]{:S(2)}, u32[]{:S(2)}) collective-permute-start(bf16[256,1024]{1,0:T(8,128)(2,1)S(1)} %fusion.118), channel_id=1, source_target_pairs={{0,16},{8,24},{16,0},{24,8},{1,17},{9,25},{17,1},{25,9},{2,18},{10... | collective-permute-start | bytes 1572872 | tf_op jit(solution)/shard_map/cond/branch_1_fun/ppermute | solution.py:18
  649.6 53.7 %collective-permute-start.49 = (bf16[128,1024]{1,0:T(8,128)(2,1)S(1)}, bf16[128,1024]{1,0:T(8,128)(2,1)S(1)}, u32[]{:S(2)}, u32[]{:S(2)}) collective-permute-start(bf16[128,1024]{1,0:T(8,128)(2,1)S(1)} %fusion.134), channel_id=1, source_target_pairs={{0,16},{8,24},{16,0},{24,8},{1,17},{9,25},{17,1},{25,9},{2,18},{10... | collective-permute-start | bytes 786440 | tf_op jit(solution)/shard_map/cond/branch_1_fun/ppermute | solution.py:18
  (14 other events, 299.5 us)
Sparse Core Ops, SparseCore 0:
  20.8 33.1 all-gather.16
  55.9 33.7 all-gather.18
  91.6 38.3 all-gather.20
  131.7 31.4 all-gather.22
